TPU v7x, 128 devices: a whole 4x4x4 slice. The times are simulated.
128 devices in a mesh: dp: 2 (over core), cent: 64 (over z, y, x).
Axes of the slice: x: 4, y: 4, z: 4, core: 2. Of those that a mesh axis runs over, the one named last changes fastest.
Arguments:
- points: bfloat16 [16384, 768], P(('dp', 'cent')), may hold values from -16 to 16
- centroids: float32 [32768, 768], P(('dp', 'cent')), may hold values from -1.5 to 1.5
Outputs:
- new_centroids: float32 [32768, 768], P(('dp', 'cent'))
- log_total: float32 [16384], P(('dp', 'cent'))
All inputs are finite; a program needn't handle non-finite values.
Results may differ from a plain program's by a relative error of at most 0.0088.
Values may be sent and summed in bfloat16 or wider, within the bound.
No kernel may reach another device: no remote copies, remote signals or barrier semaphores. Data moves between devices by JAX's collectives and lax.ppermute only.
A program may use at most 128 MiB of HBM per device.

v0:
```python
import math

import jax
import jax.numpy as jnp
from jax import lax
from jax.sharding import PartitionSpec as P

BLOCKS = 2


def score_block(members, cent_block, score_scale):
    sq_norm = jnp.sum(jnp.square(cent_block.astype(jnp.float32)), axis=1)
    products = lax.dot_general(
        members, cent_block, (((1,), (1,)), ((), ())), preferred_element_type=jnp.float32
    )
    return (2.0 * products - sq_norm[None, :]) * score_scale


def fold_stats(running, scores):
    old_max, old_sum = running
    new_max = jnp.maximum(old_max, jnp.max(scores, axis=1))
    new_sum = old_sum * jnp.exp(old_max - new_max) + jnp.sum(
        jnp.exp(scores - new_max[:, None]), axis=1
    )
    return (new_max, new_sum)


def on_device(points, centroids):
    feature_width = centroids.shape[1]
    own_rows = centroids.shape[0]
    dp_count = lax.axis_size("dp")
    score_scale = 7.0 / math.sqrt(feature_width)
    copies = centroids.astype(jnp.bfloat16)
    members = lax.all_gather(points, "cent", axis=0, tiled=True)
    member_rows = members.shape[0]
    start = (jnp.full((member_rows,), -1e30, jnp.float32), jnp.zeros((member_rows,), jnp.float32))
    part_rows = own_rows // BLOCKS
    gathered = lax.all_gather(copies, "dp", axis=0, tiled=True)
    running = start
    block_span = gathered.shape[0] // BLOCKS
    for index_j in range(BLOCKS):
        running = fold_stats(
            running,
            score_block(
                members, gathered[index_j * block_span : (index_j + 1) * block_span], score_scale
            ),
        )
    local_max, local_sum = running
    global_max = lax.pmax(local_max.astype(jnp.bfloat16), "cent").astype(local_max.dtype)
    global_sum = lax.psum(local_sum * jnp.exp(local_max - global_max), "cent")
    log_total = global_max + jnp.log(global_sum)
    arranged = gathered.reshape(dp_count, BLOCKS, part_rows, feature_width)
    sum_parts = []
    count_parts = []
    for index_j in range(BLOCKS):
        cent_block = arranged[:, index_j].reshape(dp_count * part_rows, feature_width)
        scores = score_block(members, cent_block, score_scale)
        weights = jnp.exp(scores - log_total[:, None]).astype(jnp.bfloat16)
        partial_sums = lax.dot_general(
            weights, members, (((0,), (0,)), ((), ())), preferred_element_type=jnp.float32
        )
        counts = jnp.sum(weights, axis=0, dtype=jnp.float32)
        owned_sums, owned_counts = (
            lax.psum_scatter(partial_sums, "dp", scatter_dimension=0, tiled=True),
            lax.psum_scatter(counts, "dp", scatter_dimension=0, tiled=True),
        )
        sum_parts.append(owned_sums)
        count_parts.append(owned_counts)
    own_sums = jnp.concatenate(sum_parts, axis=0)
    own_counts = jnp.concatenate(count_parts, axis=0)
    new_centroids = (own_sums + centroids) / (own_counts[:, None] + 1.0)
    own_points = points.shape[0]
    own_total = lax.dynamic_slice_in_dim(log_total, lax.axis_index("cent") * own_points, own_points)
    return (new_centroids, own_total)


def solution(mesh):
    placed = (P(("dp", "cent"), None), P(("dp", "cent"), None))
    return jax.shard_map(
        on_device,
        mesh=mesh,
        in_specs=placed,
        out_specs=(P(("dp", "cent"), None), P(("dp", "cent"))),
        check_vma=False,
    )
```

profile of v0, /device:TPU:1, one launch (start us, length us, event | category | flops | bytes accessed | tf_op | source)
XLA Modules:
  0.0 861.3 jit_solution(398983884775000078)
XLA Ops:
  7.2 0.0 all-gather.2.cloned.1.call-start
  7.2 0.7 all-gather.2.cloned.1.call-update
  7.9 0.0 reduce-scatter.5.cloned.1.call-start
  7.9 1.2 convert_element_type.35
  9.1 3.4 all_gather.7
  12.5 0.2 multiply_reduce_fusion.2
  12.7 0.2 multiply_reduce_fusion.3
  13.0 0.1 fusion.22
  13.0 91.7 %all-gather.2.cloned.1.call-done = bf16[8192,768]{1,0:T(8,128)(2,1)} async-done(((bf16[128,768]{1,0:T(8,128)(2,1)}), bf16[8192,768]{1,0:T(8,128)(2,1)}) %all-gather.2.cloned.1.call-update) | async-done | bytes 12582928 | tf_op jit(solution)/shard_map/all_gather | solution.py:34
  104.7 0.0 copy-start
  104.7 11.4 %fusion.23 = (f32[8192]{0:T(1024)S(1)}, f32[8192,256]{1,0:T(8,128)}) fusion(f32[256]{0:T(256)S(1)} %get-tuple-element.5, bf16[8192,768]{1,0:T(8,128)(2,1)} %all-gather.2.cloned.1.call-done, bf16[512,768]{1,0:T(8,128)(2,1)S(1)} %all_gather.7), kind=kOutput, calls=%fused_computation.39 | convolution fusion | flops 3229605888 | bytes 21398528 | tf_op jit(solution)/shard_map/dot_general | solution.py:13
  116.1 0.0 copy-done
  116.1 5.7 fusion.24
  121.9 291.5 %pmax.7 = bf16[8192]{0:T(1024)(128)(2,1)S(1)} all-reduce(bf16[8192]{0:T(1024)(128)(2,1)S(1)} %get-tuple-element.8), channel_id=1, replica_groups=mesh['dp'=2,'cent'=64] {'cent'}, use_global_device_ids=true, to_apply=%region_5.0 | all-reduce | flops 8192 | bytes 32768 | tf_op jit(solution)/shard_map/pmax | solution.py:49
  413.4 8.3 exponential_reduce_fusion
  421.7 286.7 %psum.7 = f32[8192]{0:T(1024)S(1)} all-reduce(f32[8192]{0:T(1024)S(1)} %fusion.18), channel_id=1, replica_groups=mesh['dp'=2,'cent'=64] {'cent'}, use_global_device_ids=true, to_apply=%region_8.0 | all-reduce | flops 8192 | bytes 65536 | tf_op jit(solution)/shard_map/psum | solution.py:50
  708.4 6.8 convert_reduce_fusion
  715.3 7.4 fusion.26
  722.6 0.0 reduce-scatter.5.cloned.1.call-update
  722.7 0.2 reduce-scatter.3.cloned.1.call-start
  722.9 6.8 convert_reduce_fusion.1
  729.7 0.0 copy-start.2
  729.7 0.0 copy-start.1
  729.7 7.5 fusion.25
  737.2 0.0 reduce-scatter.3.cloned.1.call-update
  737.3 0.0 copy-done.2
  737.3 0.6 dynamic-slice
  738.5 113.3 %all-reduce.2 = (f32[256]{0:T(256)S(1)}, f32[256]{0:T(256)S(1)}) all-reduce(f32[256]{0:T(256)S(1)} %get-tuple-element.17, f32[256]{0:T(256)S(1)} %get-tuple-element.19), channel_id=5, replica_groups=mesh['dp'=2,'cent'=64] {'dp'}, use_global_device_ids=true, to_apply=%region_15.0.clone | all-reduce | flops 512 | bytes 4096
  851.9 0.1 dynamic-slice.3
  851.9 0.1 dynamic-slice.1
  852.0 0.6 dynamic_slice.3
  852.6 0.0 reduce-scatter.5.cloned.1.call-done
  852.6 0.0 reduce-scatter.3.cloned.1.call-done
  852.6 0.0 copy-done.1
  852.7 2.1 fusion.14
  (4 shorter events, 0.1 us)
Async XLA Ops:
  7.2 97.6 %all-gather.2.cloned.1.call-start = ((), (), s32[]{:S(2)}) async-start(), calls=%async_computation.2 | async-start | bytes 12779520 | tf_op jit(solution)/shard_map/all_gather | solution.py:34
  7.9 844.7 %reduce-scatter.5.cloned.1.call-start = ((), (), s32[]{:S(2)}) async-start(), calls=%async_computation.4 | async-start | bytes 1179648 | tf_op jit(solution)/shard_map/reduce_scatter | solution.py:64
  104.7 11.4 %copy-start = (bf16[8192,768]{1,0:T(8,128)(2,1)S(1)}, bf16[8192,768]{1,0:T(8,128)(2,1)}, u32[]{:S(2)}) copy-start(bf16[8192,768]{1,0:T(8,128)(2,1)} %all-gather.2.cloned.1.call-done) | copy-start | bytes 37748740
  722.7 130.0 %reduce-scatter.3.cloned.1.call-start = ((), (), s32[]{:S(2)}) async-start(), calls=%async_computation.3 | async-start | bytes 1179648 | tf_op jit(solution)/shard_map/reduce_scatter | solution.py:64
  729.7 7.5 copy-start.2
  729.7 122.9 %copy-start.1 = (f32[256,768]{1,0:T(8,128)S(1)}, f32[256,768]{1,0:T(8,128)}, u32[]{:S(2)}) copy-start(f32[256,768]{1,0:T(8,128)} %param.3) | copy-start | bytes 2359300
Sparse Core Ops, SparseCore 0:
  10.7 93.9 all-gather.1
  722.8 114.9 reduce-scatter.4
  840.1 12.4 reduce-scatter.2
where the time goes:
time: 862 us; the launch traced here: 861 us
  blocking collectives  695 us (81%)
  waiting for transfers between devices  92.4 us (11%)
  matrix products  45.7 us (5%)
  between operations  14.5 us (2%)
  other arithmetic  12.1 us (1%)
    pmax x1, blocking collectives, on_device(): lax.pmax(local_max.astype(jnp.bfloat16), 'cent').astype(local_max.dtype)  292 us
    psum x1, blocking collectives, on_device(): global_sum = lax.psum(local_sum * jnp.exp(local_max - global_max), 'cent')  287 us
    unnamed x1, blocking collectives  113 us
    all_gather x1, waiting for transfers between devices, on_device(): members = lax.all_gather(points, 'cent', axis=0, tiled=True)  91.7 us
    dot_general x4, matrix products, score_block(): lax.dot_general(members, cent_block, (((1,), (1,)), ((), ())), preferred_...  30.8 us
  transfers between devices with their start and end apart: 3, of which 1 were waited for; matrix products, arithmetic and copies ran while one was open for 2% of the time, Pallas kernels for 0%

commit v1 on v0

--- a/solution.py
+++ b/solution.py
@@ -25,6 +25,21 @@
     return (new_max, new_sum)
 
 
+def group_log_total(local_max, local_sum, own_points):
+    cent_count = lax.axis_size("cent")
+    packed = jnp.stack(
+        [local_max.reshape(cent_count, own_points), local_sum.reshape(cent_count, own_points)], axis=1
+    )
+    parts = lax.all_to_all(packed, "cent", 0, 0, tiled=True)
+    part_max, part_sum = parts[:, 0], parts[:, 1]
+    top = jnp.max(part_max, axis=0)
+    total = jnp.sum(part_sum * jnp.exp(part_max - top[None, :]), axis=0)
+    own_total = top + jnp.log(total)
+    spread = jnp.broadcast_to(own_total[None], (cent_count, own_points))
+    log_total = lax.all_to_all(spread, "cent", 0, 0, tiled=True).reshape(cent_count * own_points)
+    return own_total, log_total
+
+
 def on_device(points, centroids):
     feature_width = centroids.shape[1]
     own_rows = centroids.shape[0]
@@ -46,9 +61,7 @@
             ),
         )
     local_max, local_sum = running
-    global_max = lax.pmax(local_max.astype(jnp.bfloat16), "cent").astype(local_max.dtype)
-    global_sum = lax.psum(local_sum * jnp.exp(local_max - global_max), "cent")
-    log_total = global_max + jnp.log(global_sum)
+    own_total, log_total = group_log_total(local_max, local_sum, points.shape[0])
     arranged = gathered.reshape(dp_count, BLOCKS, part_rows, feature_width)
     sum_parts = []
     count_parts = []
@@ -69,8 +82,6 @@
     own_sums = jnp.concatenate(sum_parts, axis=0)
     own_counts = jnp.concatenate(count_parts, axis=0)
     new_centroids = (own_sums + centroids) / (own_counts[:, None] + 1.0)
-    own_points = points.shape[0]
-    own_total = lax.dynamic_slice_in_dim(log_total, lax.axis_index("cent") * own_points, own_points)
     return (new_centroids, own_total)
 
 

time: 862 us -> 206 us (0.24)
  blocking collectives: 695 us -> 8.74 us
  waiting for transfers between devices: 92.4 us -> 113 us
  starting transfers between devices: 0.3 us -> 13.6 us
    pmax x1 -> x0, blocking collectives: 292 us -> none  [on_device(): lax.pmax(local_max.astype(jnp.bfloat16), 'cent').astype(local_max.dtype)]
    psum x1 -> x0, blocking collectives: 287 us -> none  [on_device(): global_sum = lax.psum(local_sum * jnp.exp(local_max - global_max), 'cent')]
    unnamed x1, blocking collectives: 113 us -> 5.36 us
    all_to_all x0 -> x2, waiting for transfers between devices: none -> 16.5 us  [the longest x1 8.38 us: group_log_total(): parts = lax.all_to_all(packed, 'cent', 0, 0, tiled=True)]
    all_to_all x0 -> x2, starting transfers between devices: none -> 13.3 us  [the longest x1 8.32 us: group_log_total(): parts = lax.all_to_all(packed, 'cent', 0, 0, tiled=True)]
  transfers between devices with their start and end apart: 3 -> 5, of which waited for: 1 -> 4; matrix products, arithmetic and copies ran while one was open for 2% -> 8% of each run, Pallas kernels for 0% -> 0%
where the time goes in v1:
time: 206 us; the launch traced here: 205 us
  waiting for transfers between devices  113 us (55%)
  matrix products  42.3 us (21%)
  between operations  14.5 us (7%)
  starting transfers between devices  13.6 us (7%)
  other arithmetic  11.5 us (6%)
  blocking collectives  8.74 us (4%)
    all_gather x1, waiting for transfers between devices, on_device(): members = lax.all_gather(points, 'cent', axis=0, tiled=True)  92 us
    dot_general x4, matrix products, score_block(): lax.dot_general(members, cent_block, (((1,), (1,)), ((), ())), preferred_...  27.3 us
    dot_general x2, matrix products, on_device(): lax.dot_general(weights, members, (((0,), (0,)), ((), ())), preferred_ele...  15 us
    all_to_all x1, waiting for transfers between devices, group_log_total(): parts = lax.all_to_all(packed, 'cent', 0, 0, tiled=True)  8.38 us
    all_to_all x1, starting transfers between devices, group_log_total(): parts = lax.all_to_all(packed, 'cent', 0, 0, tiled=True)  8.32 us
    all_to_all x1, waiting for transfers between devices, group_log_total(): lax.all_to_all(spread, 'cent', 0, 0, tiled=True)  8.07 us
    reduce_sum x1, other arithmetic, fold_stats(): jnp.sum(jnp.exp(scores - new_max[:, None]), axis=1)  6.84 us
    unnamed x1, blocking collectives  5.36 us
  transfers between devices with their start and end apart: 5, of which 4 were waited for; matrix products, arithmetic and copies ran while one was open for 8% of the time, Pallas kernels for 0%

profile of v1, /device:TPU:1, one launch (start us, length us, event | category | flops | bytes accessed | tf_op | source)
XLA Modules:
  0.0 205.3 jit_solution(9722181552665388045)
XLA Ops:
  7.2 0.0 all-gather.2.cloned.1.call-start
  7.2 0.7 all-gather.2.cloned.1.call-update
  7.9 1.2 convert_element_type.29
  9.1 3.4 %all_gather.7 = bf16[512,768]{1,0:T(8,128)(2,1)S(1)} all-gather(bf16[256,768]{1,0:T(8,128)(2,1)S(1)} %convert_element_type.29), channel_id=1, replica_groups=mesh['dp'=2,'cent'=64] {'dp'}, dimensions={0}, use_global_device_ids=true | all-gather | bytes 1179648 | tf_op jit(solution)/shard_map/all_gather | solution.py:53
  12.5 0.2 multiply_reduce_fusion.2
  12.7 92.0 %all-gather.2.cloned.1.call-done = bf16[8192,768]{1,0:T(8,128)(2,1)} async-done(((bf16[128,768]{1,0:T(8,128)(2,1)}), bf16[8192,768]{1,0:T(8,128)(2,1)}) %all-gather.2.cloned.1.call-update) | async-done | bytes 12582928 | tf_op jit(solution)/shard_map/all_gather | solution.py:49
  104.7 0.0 copy-start
  104.7 8.0 %fusion.21 = (f32[8192]{0:T(1024)S(1)}, f32[8192,256]{1,0:T(8,128)S(1)}) fusion(f32[256]{0:T(256)S(1)} %get-tuple-element.5, bf16[8192,768]{1,0:T(8,128)(2,1)} %all-gather.2.cloned.1.call-done, bf16[512,768]{1,0:T(8,128)(2,1)S(1)} %all_gather.7), kind=kOutput, calls=%fused_computation.40 | convolution fusion | flops 3229605888 | bytes 21398528 | tf_op jit(solution)/shard_map/dot_general | solution.py:13
  112.7 0.2 copy-done
  112.9 5.7 %fusion.20 = (f32[8192]{0:T(1024)S(1)}, f32[8192,256]{1,0:T(8,128)}) fusion(f32[256]{0:T(256)S(1)} %get-tuple-element.4, bf16[8192,768]{1,0:T(8,128)(2,1)S(1)} %copy-done, bf16[512,768]{1,0:T(8,128)(2,1)S(1)} %all_gather.7), kind=kOutput, calls=%fused_computation.39 | convolution fusion | flops 3229605888 | bytes 21398528 | tf_op jit(solution)/shard_map/dot_general | solution.py:13
  118.6 6.8 %exponential_reduce_fusion = (f32[8192]{0:T(1024)S(1)}, f32[8192]{0:T(1024)S(1)}) fusion(f32[8192,256]{1,0:T(8,128)S(1)} %get-tuple-element.19, f32[8192]{0:T(1024)S(1)} %get-tuple-element.15, f32[8192,256]{1,0:T(8,128)} %get-tuple-element.17, f32[8192]{0:T(1024)S(1)} %get-tuple-element.14), kind=kLoop, calls=%fused_computation.20 | loop fusion | flops 8372224 | bytes 16908288 | tf_op jit(solution)/shard_map/reduce_sum | solution.py:22
  125.4 0.1 multiply_add_fusion
  125.6 0.7 pad_maximum_fusion
  126.2 8.3 %all-to-all-start = ((f32[64,2,128]{2,1,0:T(2,128)}), f32[64,2,128]{2,1,0:T(2,128)S(1)}, u32[]{:S(2)}, u32[]{:S(2)}) async-start(f32[64,2,128]{2,1,0:T(2,128)} %pad_maximum_fusion), calls=%async_computation | async-start | bytes 131072 | tf_op jit(solution)/shard_map/all_to_all | solution.py:33
  134.6 0.1 fusion.18
  134.6 8.4 %all-to-all-done = f32[64,2,128]{2,1,0:T(2,128)S(1)} async-done(((f32[64,2,128]{2,1,0:T(2,128)}), f32[64,2,128]{2,1,0:T(2,128)S(1)}, u32[]{:S(2)}, u32[]{:S(2)}) %all-to-all-start) | async-done | bytes 65568 | tf_op jit(solution)/shard_map/all_to_all | solution.py:33
  143.0 0.1 fusion.19
  143.1 0.0 copy-start.2
  143.2 0.6 broadcast_in_dim.11
  143.8 5.0 %all-to-all-start.1 = ((f32[64,1,128]{2,1,0:T(1,128)}), f32[64,1,128]{2,1,0:T(1,128)S(1)}, u32[]{:S(2)}, u32[]{:S(2)}) async-start(f32[64,1,128]{2,1,0:T(1,128)} %broadcast_in_dim.11), calls=%async_computation.1 | async-start | bytes 65536 | tf_op jit(solution)/shard_map/all_to_all | solution.py:39
  148.8 0.0 reduce-scatter.3.cloned.1.call-start
  148.8 0.2 multiply_reduce_fusion.3
  149.0 8.1 %all-to-all-done.1 = f32[64,1,128]{2,1,0:T(1,128)S(1)} async-done(((f32[64,1,128]{2,1,0:T(1,128)}), f32[64,1,128]{2,1,0:T(1,128)S(1)}, u32[]{:S(2)}, u32[]{:S(2)}) %all-to-all-start.1) | async-done | bytes 32800 | tf_op jit(solution)/shard_map/all_to_all | solution.py:39
  157.1 6.8 %convert_reduce_fusion.1 = (f32[256]{0:T(256)S(1)}, bf16[8192,256]{1,0:T(8,128)(2,1)S(1)}) fusion(f32[8192]{0:T(1024)S(1)} %bitcast.36, f32[256]{0:T(256)S(1)} %bitcast.39, bf16[8192,768]{1,0:T(8,128)(2,1)} %all-gather.2.cloned.1.call-done, bf16[256,768]{1,0:T(8,128)(2,1)S(1)} %bitcast.28), kind=kOutput, calls=%fused_computation.19 | convolution fusion | flops 3235905280 | bytes 17205248 | tf_op jit(solution)/shard_map/dot_general | solution.py:13
  164.0 0.0 copy-done.2
  164.0 7.4 %fusion.22 = f32[256,768]{1,0:T(8,128)} fusion(bf16[8192,256]{1,0:T(8,128)(2,1)S(1)} %get-tuple-element.23, bf16[8192,768]{1,0:T(8,128)(2,1)} %all-gather.2.cloned.1.call-done), kind=kOutput, calls=%fused_computation.41 | convolution fusion | flops 3221225472 | bytes 17563648 | tf_op jit(solution)/shard_map/dot_general | solution.py:72
  171.4 0.0 reduce-scatter.3.cloned.1.call-update
  171.4 0.2 reduce-scatter.5.cloned.1.call-start
  171.6 6.8 %convert_reduce_fusion = (f32[256]{0:T(256)S(1)}, bf16[8192,256]{1,0:T(8,128)(2,1)S(1)}) fusion(f32[8192]{0:T(1024)S(1)} %bitcast.37, f32[256]{0:T(256)S(1)} %bitcast.38, bf16[8192,768]{1,0:T(8,128)(2,1)} %all-gather.2.cloned.1.call-done, bf16[256,768]{1,0:T(8,128)(2,1)S(1)} %bitcast.27), kind=kOutput, calls=%fused_computation.18 | convolution fusion | flops 3235905280 | bytes 17205248 | tf_op jit(solution)/shard_map/dot_general | solution.py:13
  178.5 0.0 copy-start.3
  178.5 0.0 copy-start.1
  178.5 7.6 %fusion.23 = f32[256,768]{1,0:T(8,128)} fusion(bf16[8192,256]{1,0:T(8,128)(2,1)S(1)} %get-tuple-element.21, bf16[8192,768]{1,0:T(8,128)(2,1)} %all-gather.2.cloned.1.call-done), kind=kOutput, calls=%fused_computation.42 | convolution fusion | flops 3221225472 | bytes 17563648 | tf_op jit(solution)/shard_map/dot_general | solution.py:72
  186.1 0.0 reduce-scatter.5.cloned.1.call-update
  186.1 0.0 copy-done.3
  186.2 0.6 dynamic-slice
  187.4 5.4 %all-reduce.2 = (f32[256]{0:T(256)S(1)}, f32[256]{0:T(256)S(1)}) all-reduce(f32[256]{0:T(256)S(1)} %get-tuple-element.20, f32[256]{0:T(256)S(1)} %get-tuple-element.22), channel_id=5, replica_groups=mesh['dp'=2,'cent'=64] {'dp'}, use_global_device_ids=true, to_apply=%region_15.0.clone | all-reduce | flops 512 | bytes 4096
  192.8 0.1 dynamic-slice.1
  192.9 0.1 dynamic-slice.3
  193.0 0.0 reduce-scatter.3.cloned.1.call-done
  193.0 3.7 %reduce-scatter.5.cloned.1.call-done = f32[128,768]{1,0:T(8,128)} async-done(((f32[256,768]{1,0:T(8,128)}), f32[128,768]{1,0:T(8,128)}) %reduce-scatter.5.cloned.1.call-update) | async-done | bytes 393232 | tf_op jit(solution)/shard_map/reduce_scatter | solution.py:77
  196.6 0.0 copy-done.1
  196.6 2.1 %fusion.14 = f32[256,768]{1,0:T(8,128)} fusion(f32[256,768]{1,0:T(8,128)S(1)} %copy-done.1, f32[128,768]{1,0:T(8,128)} %reduce-scatter.5.cloned.1.call-done, f32[128,768]{1,0:T(8,128)} %reduce-scatter.3.cloned.1.call-done, f32[256]{0:T(256)S(1)} %maximum_add_fusion.1), kind=kLoop, calls=%fused_computation.23 | loop fusion | flops 589824 | bytes 2360320 | tf_op jit(solution)/shard_map/div | solution.py:84
  (5 shorter events, 0.1 us)
Async XLA Ops:
  7.2 97.6 %all-gather.2.cloned.1.call-start = ((), (), s32[]{:S(2)}) async-start(), calls=%async_computation.4 | async-start | bytes 12779520 | tf_op jit(solution)/shard_map/all_gather | solution.py:49
  104.7 8.2 %copy-start = (bf16[8192,768]{1,0:T(8,128)(2,1)S(1)}, bf16[8192,768]{1,0:T(8,128)(2,1)}, u32[]{:S(2)}) copy-start(bf16[8192,768]{1,0:T(8,128)(2,1)} %all-gather.2.cloned.1.call-done) | copy-start | bytes 37748740
  126.2 16.8 %all-to-all-start = ((f32[64,2,128]{2,1,0:T(2,128)}), f32[64,2,128]{2,1,0:T(2,128)S(1)}, u32[]{:S(2)}, u32[]{:S(2)}) async-start(f32[64,2,128]{2,1,0:T(2,128)} %pad_maximum_fusion), calls=%async_computation | async-start | bytes 131072 | tf_op jit(solution)/shard_map/all_to_all | solution.py:33
  143.1 20.8 %copy-start.2 = (f32[128]{0:T(128)}, f32[128]{0:T(128)S(1)}, u32[]{:S(2)}) copy-start(f32[128]{0:T(128)S(1)} %log_add_fusion) | copy-start | bytes 1540
  143.8 13.3 %all-to-all-start.1 = ((f32[64,1,128]{2,1,0:T(1,128)}), f32[64,1,128]{2,1,0:T(1,128)S(1)}, u32[]{:S(2)}, u32[]{:S(2)}) async-start(f32[64,1,128]{2,1,0:T(1,128)} %broadcast_in_dim.11), calls=%async_computation.1 | async-start | bytes 65536 | tf_op jit(solution)/shard_map/all_to_all | solution.py:39
  148.8 44.2 %reduce-scatter.3.cloned.1.call-start = ((), (), s32[]{:S(2)}) async-start(), calls=%async_computation.5 | async-start | bytes 1179648 | tf_op jit(solution)/shard_map/reduce_scatter | solution.py:77
  171.4 25.2 %reduce-scatter.5.cloned.1.call-start = ((), (), s32[]{:S(2)}) async-start(), calls=%async_computation.6 | async-start | bytes 1179648 | tf_op jit(solution)/shard_map/reduce_scatter | solution.py:77
  178.5 7.7 %copy-start.3 = (u32[128]{0:T(128)S(1)}, u32[128]{0:T(128)}, u32[]{:S(2)}) copy-start(u32[128]{0:T(128)} %constant.15) | copy-start | bytes 1540
  178.5 18.1 %copy-start.1 = (f32[256,768]{1,0:T(8,128)S(1)}, f32[256,768]{1,0:T(8,128)}, u32[]{:S(2)}) copy-start(f32[256,768]{1,0:T(8,128)} %param.3) | copy-start | bytes 2359300
Sparse Core Ops, SparseCore 0:
  10.7 93.9 all-gather.1
  171.5 9.9 reduce-scatter.2
  186.3 10.3 reduce-scatter.4

commit v2 on v1

v2 whole, which is shorter than its diff:
```python
import math

import jax
import jax.numpy as jnp
from jax import lax
from jax.sharding import PartitionSpec as P

HALVES = 2


def score_block(members, cent_block, score_scale):
    sq_norm = jnp.sum(jnp.square(cent_block.astype(jnp.float32)), axis=1)
    products = lax.dot_general(
        members, cent_block, (((1,), (1,)), ((), ())), preferred_element_type=jnp.float32
    )
    return (2.0 * products - sq_norm[None, :]) * score_scale


def group_log_total(local_max, local_sum, own_points):
    cent_count = lax.axis_size("cent")
    packed = jnp.stack(
        [local_max.reshape(cent_count, own_points), local_sum.reshape(cent_count, own_points)], axis=1
    )
    parts = lax.all_to_all(packed, "cent", 0, 0, tiled=True)
    part_max, part_sum = parts[:, 0], parts[:, 1]
    top = jnp.max(part_max, axis=0)
    total = jnp.sum(part_sum * jnp.exp(part_max - top[None, :]), axis=0)
    own_total = top + jnp.log(total)
    spread = jnp.broadcast_to(own_total[None], (cent_count, own_points))
    log_total = lax.all_to_all(spread, "cent", 0, 0, tiled=True).reshape(cent_count * own_points)
    return own_total, log_total


def on_device(points, centroids):
    feature_width = centroids.shape[1]
    own_points = points.shape[0]
    cent_count = lax.axis_size("cent")
    score_scale = 7.0 / math.sqrt(feature_width)
    copies = centroids.astype(jnp.bfloat16)
    members = lax.all_gather(points, "cent", axis=0, tiled=True)
    gathered = lax.all_gather(copies, "dp", axis=0, tiled=True)
    half_points = own_points // HALVES
    split = members.reshape(cent_count, HALVES, half_points, feature_width)
    own_parts = []
    sums = None
    counts = None
    for index_h in range(HALVES):
        half = split[:, index_h].reshape(cent_count * half_points, feature_width)
        scores = score_block(half, gathered, score_scale)
        local_max = jnp.max(scores, axis=1)
        local_sum = jnp.sum(jnp.exp(scores - local_max[:, None]), axis=1)
        own_total, log_total = group_log_total(local_max, local_sum, half_points)
        own_parts.append(own_total)
        weights = jnp.exp(scores - log_total[:, None]).astype(jnp.bfloat16)
        part_sums = lax.dot_general(
            weights, half, (((0,), (0,)), ((), ())), preferred_element_type=jnp.float32
        )
        part_counts = jnp.sum(weights, axis=0, dtype=jnp.float32)
        sums = part_sums if sums is None else sums + part_sums
        counts = part_counts if counts is None else counts + part_counts
    own_sums = lax.psum_scatter(sums, "dp", scatter_dimension=0, tiled=True)
    own_counts = lax.psum_scatter(counts, "dp", scatter_dimension=0, tiled=True)
    new_centroids = (own_sums + centroids) / (own_counts[:, None] + 1.0)
    return (new_centroids, jnp.concatenate(own_parts))


def solution(mesh):
    placed = (P(("dp", "cent"), None), P(("dp", "cent"), None))
    return jax.shard_map(
        on_device,
        mesh=mesh,
        in_specs=placed,
        out_specs=(P(("dp", "cent"), None), P(("dp", "cent"))),
        check_vma=False,
    )
```

time: 206 us -> 231 us (1.12)
  starting transfers between devices: 13.6 us -> 27.7 us
  other arithmetic: 11.5 us -> 23.6 us
  local copies, waits for them, and re-layouts: 1.77 us -> 13.8 us
  matrix products: 42.3 us -> 31.7 us
  waiting for transfers between devices: 113 us -> 109 us
    dot_general x4 -> x2, matrix products: 27.3 us -> 14.2 us  [score_block(): lax.dot_general(members, cent_block, (((1,), (1,)), ((), ())), preferred_...]
    all_to_all x1 -> x2, starting transfers between devices: 8.32 us -> 18.1 us  [group_log_total(): parts = lax.all_to_all(packed, 'cent', 0, 0, tiled=True)]
    reduce_sum x1 -> x3, other arithmetic: 6.84 us -> 16.2 us  [the longest x2 9.06 us: on_device(): local_sum = jnp.sum(jnp.exp(scores - local_max[:, None]), axis=1)]
    slice x1, local copies, waits for them, and re-layouts: 0.05 us -> 8.65 us  [on_device(): half = split[:, index_h].reshape(cent_count * half_points, feature_width)]
    all_to_all x1 -> x2, starting transfers between devices: 4.97 us -> 9.36 us  [group_log_total(): lax.all_to_all(spread, 'cent', 0, 0, tiled=True)]
    all_to_all x0 -> x4, other arithmetic: none -> 2.89 us  [the longest x2 1.45 us: group_log_total(): lax.all_to_all(spread, 'cent', 0, 0, tiled=True)]
    dot_general x2, matrix products: 15 us -> 17.5 us  [on_device(): lax.dot_general(weights, half, (((0,), (0,)), ((), ())), preferred_elemen...]
    all_to_all x1 -> x2, waiting for transfers between devices: 8.38 us -> 6.95 us  [group_log_total(): parts = lax.all_to_all(packed, 'cent', 0, 0, tiled=True)]
  transfers between devices with their start and end apart: 5 -> 6, of which waited for: 4 -> 4; matrix products, arithmetic and copies ran while one was open for 8% -> 15% of each run, Pallas kernels for 0% -> 0%
where the time goes in v2:
time: 231 us; the launch traced here: 230 us
  waiting for transfers between devices  109 us (47%)
  matrix products  31.7 us (14%)
  starting transfers between devices  27.7 us (12%)
  other arithmetic  23.6 us (10%)
  between operations  14.9 us (6%)
  local copies, waits for them, and re-layouts  13.8 us (6%)
  blocking collectives  10.2 us (4%)
    all_gather x1, waiting for transfers between devices, on_device(): members = lax.all_gather(points, 'cent', axis=0, tiled=True)  92 us
    all_to_all x2, starting transfers between devices, group_log_total(): parts = lax.all_to_all(packed, 'cent', 0, 0, tiled=True)  18.1 us
    dot_general x2, matrix products, on_device(): lax.dot_general(weights, half, (((0,), (0,)), ((), ())), preferred_elemen...  17.5 us
    dot_general x2, matrix products, score_block(): lax.dot_general(members, cent_block, (((1,), (1,)), ((), ())), preferred_...  14.2 us
    all_to_all x2, starting transfers between devices, group_log_total(): lax.all_to_all(spread, 'cent', 0, 0, tiled=True)  9.36 us
    reduce_sum x2, other arithmetic, on_device(): local_sum = jnp.sum(jnp.exp(scores - local_max[:, None]), axis=1)  9.06 us
    slice x1, local copies, waits for them, and re-layouts, on_device(): half = split[:, index_h].reshape(cent_count * half_points, feature_width)  8.65 us
    all_to_all x2, waiting for transfers between devices, group_log_total(): lax.all_to_all(spread, 'cent', 0, 0, tiled=True)  7.39 us
  transfers between devices with their start and end apart: 6, of which 4 were waited for; matrix products, arithmetic and copies ran while one was open for 15% of the time, Pallas kernels for 0%

profile of v2, /device:TPU:1, one launch (start us, length us, event | category | flops | bytes accessed | tf_op | source)
XLA Modules:
  0.0 230.5 jit_solution(3304867153175038017)
XLA Ops:
  7.2 0.7 all-gather.2.cloned.1.call-update
  7.9 1.2 convert_element_type.19
  9.1 3.4 %all_gather.7 = bf16[512,768]{1,0:T(8,128)(2,1)S(1)} all-gather(bf16[256,768]{1,0:T(8,128)(2,1)S(1)} %convert_element_type.19), channel_id=1, replica_groups=mesh['dp'=2,'cent'=64] {'dp'}, dimensions={0}, use_global_device_ids=true | all-gather | bytes 1179648 | tf_op jit(solution)/shard_map/all_gather | solution.py:41
  12.5 0.2 multiply_reduce_fusion
  12.7 92.0 %all-gather.2.cloned.1.call-done = bf16[8192,768]{1,0:T(8,128)(2,1)} async-done(((bf16[128,768]{1,0:T(8,128)(2,1)}), bf16[8192,768]{1,0:T(8,128)(2,1)}) %all-gather.2.cloned.1.call-update) | async-done | bytes 12582928 | tf_op jit(solution)/shard_map/all_gather | solution.py:40
  104.7 8.6 %fusion.1 = (bf16[64,1,64,768]{3,2,1,0:T(8,128)(2,1)}, bf16[64,1,64,768]{3,2,1,0:T(8,128)(2,1)S(1)}) fusion(bf16[64,2,64,768]{3,2,1,0:T(8,128)(2,1)} %bitcast.18), kind=kLoop, calls=%fused_computation.20 | loop fusion | bytes 25165824 | tf_op jit(solution)/shard_map/slice | solution.py:48
  113.4 5.8 %fusion.4 = (f32[4096]{0:T(1024)S(1)}, f32[4096,512]{0,1:T(8,128)}) fusion(f32[512]{0:T(512)S(1)} %multiply_reduce_fusion, bf16[4096,768]{1,0:T(8,128)(2,1)S(1)} %bitcast.21, bf16[512,768]{1,0:T(8,128)(2,1)S(1)} %all_gather.7), kind=kOutput, calls=%fused_computation.23 | convolution fusion | flops 3229609984 | bytes 15484928 | tf_op jit(solution)/shard_map/dot_general | solution.py:13
  119.1 0.1 stack_reshape.12
  119.2 4.5 %exponential_reduce_fusion.1 = f32[4096]{0:T(1024)S(1)} fusion(f32[4096,512]{0,1:T(8,128)} %get-tuple-element.9, f32[4096]{0:T(1024)S(1)} %get-tuple-element.8), kind=kLoop, calls=%fused_computation.6 | loop fusion | flops 4190208 | bytes 8421376 | tf_op jit(solution)/shard_map/reduce_sum | solution.py:51
  123.7 0.1 stack_reshape.13
  123.8 0.1 pad_maximum_fusion
  123.9 0.7 reshape.60
  124.7 8.3 %all-to-all-start = ((f32[64,1,128]{2,1,0:T(1,128)}), f32[64,1,128]{2,1,0:T(1,128)S(1)}, u32[]{:S(2)}, u32[]{:S(2)}) async-start(f32[64,1,128]{2,1,0:T(1,128)} %reshape.60), calls=%async_computation | async-start | bytes 65536 | tf_op jit(solution)/shard_map/all_to_all | solution.py:24
  133.0 8.5 %fusion.5 = (f32[4096]{0:T(1024)S(1)}, f32[4096,512]{0,1:T(8,128)}) fusion(f32[512]{0:T(512)S(1)} %multiply_reduce_fusion, bf16[4096,768]{1,0:T(8,128)(2,1)} %bitcast.19, bf16[512,768]{1,0:T(8,128)(2,1)S(1)} %all_gather.7), kind=kOutput, calls=%fused_computation.24 | convolution fusion | flops 3229609984 | bytes 15484928 | tf_op jit(solution)/shard_map/dot_general | solution.py:13
  141.5 0.1 stack_reshape.14
  141.6 4.5 %exponential_reduce_fusion = f32[4096]{0:T(1024)S(1)} fusion(f32[4096,512]{0,1:T(8,128)} %get-tuple-element.11, f32[4096]{0:T(1024)S(1)} %get-tuple-element.10), kind=kLoop, calls=%fused_computation.3 | loop fusion | flops 4190208 | bytes 8421376 | tf_op jit(solution)/shard_map/reduce_sum | solution.py:51
  146.1 0.1 stack_reshape.15
  146.2 0.1 pad_maximum_fusion.1
  146.3 0.7 reshape.62
  147.0 9.8 %all-to-all-start.2 = ((f32[64,1,128]{2,1,0:T(1,128)}), f32[64,1,128]{2,1,0:T(1,128)S(1)}, u32[]{:S(2)}, u32[]{:S(2)}) async-start(f32[64,1,128]{2,1,0:T(1,128)} %reshape.62), calls=%async_computation.2 | async-start | bytes 65536 | tf_op jit(solution)/shard_map/all_to_all | solution.py:24
  156.8 0.5 broadcast.35
  157.3 0.7 reduce.10
  158.0 0.1 reshape.61
  158.1 0.1 fusion.3
  158.3 7.0 %all-to-all-done.2 = f32[64,1,128]{2,1,0:T(1,128)S(1)} async-done(((f32[64,1,128]{2,1,0:T(1,128)}), f32[64,1,128]{2,1,0:T(1,128)S(1)}, u32[]{:S(2)}, u32[]{:S(2)}) %all-to-all-start.2) | async-done | bytes 32800 | tf_op jit(solution)/shard_map/all_to_all | solution.py:24
  165.2 0.6 broadcast_in_dim.4
  165.8 4.7 %all-to-all-start.1 = ((f32[64,1,64]{2,1,0:T(1,128)}), f32[64,1,64]{2,1,0:T(1,128)S(1)}, u32[]{:S(2)}, u32[]{:S(2)}) async-start(f32[64,1,64]{2,1,0:T(1,128)} %broadcast_in_dim.4), calls=%async_computation.1 | async-start | bytes 65536 | tf_op jit(solution)/shard_map/all_to_all | solution.py:30
  170.5 0.7 reduce.11
  171.3 0.1 reshape.63
  171.4 0.1 fusion.2
  171.5 7.4 %all-to-all-done.1 = f32[64,1,64]{2,1,0:T(1,128)S(1)} async-done(((f32[64,1,64]{2,1,0:T(1,128)}), f32[64,1,64]{2,1,0:T(1,128)S(1)}, u32[]{:S(2)}, u32[]{:S(2)}) %all-to-all-start.1) | async-done | bytes 16416 | tf_op jit(solution)/shard_map/all_to_all | solution.py:30
  178.9 0.6 broadcast_in_dim.5
  179.5 4.7 %all-to-all-start.3 = ((f32[64,1,64]{2,1,0:T(1,128)}), f32[64,1,64]{2,1,0:T(1,128)S(1)}, u32[]{:S(2)}, u32[]{:S(2)}) async-start(f32[64,1,64]{2,1,0:T(1,128)} %broadcast_in_dim.5), calls=%async_computation.3 | async-start | bytes 65536 | tf_op jit(solution)/shard_map/all_to_all | solution.py:30
  184.2 0.2 reduce-scatter.2.cloned.1.call-start
  184.4 0.5 broadcast.33
  185.0 0.7 reduce.8
  185.7 0.1 sub.72
  185.8 7.7 %fusion = f32[512,768]{1,0:T(8,128)S(1)} fusion(bf16[4096,768]{1,0:T(8,128)(2,1)} %bitcast.22, f32[4096,512]{0,1:T(8,128)} %get-tuple-element.9, f32[4096]{0:T(1024)S(1)} %sub.72), kind=kOutput, calls=%fused_computation.10 | convolution fusion | flops 3225419776 | bytes 16269312 | tf_op jit(solution)/shard_map/dot_general | solution.py:55
  193.5 0.7 reduce.9
  194.2 0.1 sub.80
  194.3 9.8 %convolution_add_fusion = f32[512,768]{1,0:T(8,128)} fusion(f32[512,768]{1,0:T(8,128)S(1)} %fusion, bf16[4096,768]{1,0:T(8,128)(2,1)} %bitcast.20, f32[4096,512]{0,1:T(8,128)} %get-tuple-element.11, f32[4096]{0:T(1024)S(1)} %sub.80), kind=kOutput, calls=%fused_computation.9 | convolution fusion | flops 3225812992 | bytes 17842176 | tf_op jit(solution)/shard_map/dot_general | solution.py:55
  204.1 0.6 dynamic-slice
  205.4 0.6 pad_maximum_fusion.2
  205.9 7.1 %convert_reduce_fusion = (f32[512]{0:T(512)S(1)}, f32[512]{0:T(512)S(1)}) fusion(f32[4096,512]{0,1:T(8,128)} %get-tuple-element.11, f32[4096]{0:T(1024)S(1)} %sub.80, f32[4096,512]{0,1:T(8,128)} %get-tuple-element.9, f32[4096]{0:T(1024)S(1)} %sub.72), kind=kLoop, calls=%fused_computation | loop fusion | flops 16776192 | bytes 16814080 | tf_op jit(solution)/shard_map/reduce_sum | solution.py:58
  213.1 6.9 %all-reduce = f32[512]{0:T(512)S(1)} all-reduce(f32[512]{0:T(512)S(1)} %add.38), channel_id=3, replica_groups=mesh['dp'=2,'cent'=64] {'dp'}, use_global_device_ids=true, to_apply=%region_12.0.clone | all-reduce | flops 512 | bytes 4096
  220.0 0.1 dynamic-slice_add_fusion
  220.0 1.4 reduce-scatter.2.cloned.1.call-done
  221.5 2.1 add_divide_fusion
  (17 shorter events, 0.2 us)
Async XLA Ops:
  7.2 97.6 %all-gather.2.cloned.1.call-start = ((), (), s32[]{:S(2)}) async-start(), calls=%async_computation.5 | async-start | bytes 12779520 | tf_op jit(solution)/shard_map/all_gather | solution.py:40
  113.4 5.8 %copy-start = (bf16[64,1,64,768]{3,2,1,0:T(8,128)(2,1)}, bf16[64,1,64,768]{3,2,1,0:T(8,128)(2,1)S(1)}, u32[]{:S(2)}) copy-start(bf16[64,1,64,768]{3,2,1,0:T(8,128)(2,1)S(1)} %get-tuple-element.3) | copy-start | bytes 18874372
  124.7 22.3 %all-to-all-start = ((f32[64,1,128]{2,1,0:T(1,128)}), f32[64,1,128]{2,1,0:T(1,128)S(1)}, u32[]{:S(2)}, u32[]{:S(2)}) async-start(f32[64,1,128]{2,1,0:T(1,128)} %reshape.60), calls=%async_computation | async-start | bytes 65536 | tf_op jit(solution)/shard_map/all_to_all | solution.py:24
  147.0 18.2 %all-to-all-start.2 = ((f32[64,1,128]{2,1,0:T(1,128)}), f32[64,1,128]{2,1,0:T(1,128)S(1)}, u32[]{:S(2)}, u32[]{:S(2)}) async-start(f32[64,1,128]{2,1,0:T(1,128)} %reshape.62), calls=%async_computation.2 | async-start | bytes 65536 | tf_op jit(solution)/shard_map/all_to_all | solution.py:24
  165.8 13.0 %all-to-all-start.1 = ((f32[64,1,64]{2,1,0:T(1,128)}), f32[64,1,64]{2,1,0:T(1,128)S(1)}, u32[]{:S(2)}, u32[]{:S(2)}) async-start(f32[64,1,64]{2,1,0:T(1,128)} %broadcast_in_dim.4), calls=%async_computation.1 | async-start | bytes 65536 | tf_op jit(solution)/shard_map/all_to_all | solution.py:30
  179.5 14.0 %all-to-all-start.3 = ((f32[64,1,64]{2,1,0:T(1,128)}), f32[64,1,64]{2,1,0:T(1,128)S(1)}, u32[]{:S(2)}, u32[]{:S(2)}) async-start(f32[64,1,64]{2,1,0:T(1,128)} %broadcast_in_dim.5), calls=%async_computation.3 | async-start | bytes 65536 | tf_op jit(solution)/shard_map/all_to_all | solution.py:30
  184.2 37.3 %reduce-scatter.2.cloned.1.call-start = ((), (), s32[]{:S(2)}) async-start(), calls=%async_computation.6 | async-start | bytes 2359296 | tf_op jit(solution)/shard_map/reduce_scatter | solution.py:61
  194.3 9.8 %copy-start.2 = (u32[128]{0:T(128)S(1)}, u32[128]{0:T(128)}, u32[]{:S(2)}) copy-start(u32[128]{0:T(128)} %constant.12) | copy-start | bytes 1540
  205.9 15.5 %copy-start.1 = (f32[256,768]{1,0:T(8,128)S(1)}, f32[256,768]{1,0:T(8,128)}, u32[]{:S(2)}) copy-start(f32[256,768]{1,0:T(8,128)} %param.3) | copy-start | bytes 2359300
Sparse Core Ops, SparseCore 0:
  10.7 93.9 all-gather.1
  204.2 17.1 reduce-scatter.1

commit v3 on v2

v3 whole, which is shorter than its diff:
```python
import math

import jax
import jax.numpy as jnp
from jax import lax
from jax.sharding import PartitionSpec as P


def score_block(members, cent_block, score_scale):
    sq_norm = jnp.sum(jnp.square(cent_block.astype(jnp.float32)), axis=1)
    products = lax.dot_general(
        members, cent_block, (((1,), (1,)), ((), ())), preferred_element_type=jnp.float32
    )
    return (2.0 * products - sq_norm[None, :]) * score_scale


def group_log_total(local_max, local_sum, own_points):
    cent_count = lax.axis_size("cent")
    packed = jnp.stack(
        [local_max.reshape(cent_count, own_points), local_sum.reshape(cent_count, own_points)], axis=1
    )
    parts = lax.all_to_all(packed, "cent", 0, 0, tiled=True)
    part_max, part_sum = parts[:, 0], parts[:, 1]
    top = jnp.max(part_max, axis=0)
    total = jnp.sum(part_sum * jnp.exp(part_max - top[None, :]), axis=0)
    own_total = top + jnp.log(total)
    spread = jnp.broadcast_to(own_total[None], (cent_count, own_points))
    log_total = lax.all_to_all(spread, "cent", 0, 0, tiled=True).reshape(cent_count * own_points)
    return own_total, log_total


def block_sums(scores, log_total, members):
    weights = jnp.exp(scores - log_total[:, None]).astype(jnp.bfloat16)
    sums = lax.dot_general(
        weights, members, (((0,), (0,)), ((), ())), preferred_element_type=jnp.float32
    )
    counts = jnp.sum(weights, axis=0, dtype=jnp.float32)
    return sums, counts


def on_device(points, centroids):
    feature_width = centroids.shape[1]
    score_scale = 7.0 / math.sqrt(feature_width)
    swap = [(0, 1), (1, 0)]
    copies = centroids.astype(jnp.bfloat16)
    members = lax.all_gather(points, "cent", axis=0, tiled=True)
    other_copies = lax.ppermute(copies, "dp", swap)
    other_scores = score_block(members, other_copies, score_scale)
    own_scores = score_block(members, copies, score_scale)
    local_max = jnp.maximum(jnp.max(other_scores, axis=1), jnp.max(own_scores, axis=1))
    local_sum = jnp.sum(jnp.exp(other_scores - local_max[:, None]), axis=1) + jnp.sum(
        jnp.exp(own_scores - local_max[:, None]), axis=1
    )
    own_total, log_total = group_log_total(local_max, local_sum, points.shape[0])
    other_sums, other_counts = block_sums(other_scores, log_total, members)
    sent_sums = lax.ppermute(other_sums, "dp", swap)
    sent_counts = lax.ppermute(other_counts, "dp", swap)
    own_sums, own_counts = block_sums(own_scores, log_total, members)
    sums = own_sums + sent_sums
    counts = own_counts + sent_counts
    new_centroids = (sums + centroids) / (counts[:, None] + 1.0)
    return (new_centroids, own_total)


def solution(mesh):
    placed = (P(("dp", "cent"), None), P(("dp", "cent"), None))
    return jax.shard_map(
        on_device,
        mesh=mesh,
        in_specs=placed,
        out_specs=(P(("dp", "cent"), None), P(("dp", "cent"))),
        check_vma=False,
    )
```

time: 231 us -> 189 us (0.82)
  starting transfers between devices: 27.7 us -> 6.92 us
  blocking collectives: 10.2 us -> 29.9 us
  other arithmetic: 23.6 us -> 6.36 us
  waiting for transfers between devices: 109 us -> 95.4 us
  local copies, waits for them, and re-layouts: 13.8 us -> 0.92 us
  matrix products: 31.7 us -> 35.1 us
    all_to_all x0 -> x2, blocking collectives: none -> 29.9 us  [the longest x1 16.7 us: group_log_total(): parts = lax.all_to_all(packed, 'cent', 0, 0, tiled=True)]
    all_to_all x4 -> x0, starting transfers between devices: 27.5 us -> none  [the longest x2 18.1 us: group_log_total(): parts = lax.all_to_all(packed, 'cent', 0, 0, tiled=True)]
    all_to_all x4 -> x0, waiting for transfers between devices: 14.3 us -> none  [the longest x2 7.39 us: group_log_total(): lax.all_to_all(spread, 'cent', 0, 0, tiled=True)]
    reduce_sum x3 -> x2, other arithmetic: 16.2 us -> 4.78 us  [the longest x1 2.41 us: on_device(): jnp.sum(jnp.exp(own_scores - local_max[:, None]), axis=1)]
    slice x1 -> x0, local copies, waits for them, and re-layouts: 8.65 us -> none  [on_device(): half = split[:, index_h].reshape(cent_count * half_points, feature_width)]
    ppermute x0 -> x3, starting transfers between devices: none -> 6.89 us  [the longest x1 3.48 us: on_device(): sent_sums = lax.ppermute(other_sums, 'dp', swap)]
    unnamed x1 -> x0, blocking collectives: 6.87 us -> none
    all_gather x1 -> x0, blocking collectives: 3.38 us -> none  [on_device(): gathered = lax.all_gather(copies, 'dp', axis=0, tiled=True)]
  transfers between devices with their start and end apart: 6 -> 4, of which waited for: 4 -> 3; matrix products, arithmetic and copies ran while one was open for 15% -> 2% of each run, Pallas kernels for 0% -> 0%
where the time goes in v3:
time: 189 us
  waiting for transfers between devices  95.4 us (50%)
  matrix products  35.1 us (19%)
  blocking collectives  29.9 us (16%)
  between operations  14.1 us (7%)
  starting transfers between devices  6.92 us (4%)
  other arithmetic  6.36 us (3%)
    all_gather x1, waiting for transfers between devices, on_device(): members = lax.all_gather(points, 'cent', axis=0, tiled=True)  92.6 us
    dot_general x2, matrix products, block_sums(): lax.dot_general(weights, members, (((0,), (0,)), ((), ())), preferred_ele...  18.9 us
    all_to_all x1, blocking collectives, group_log_total(): parts = lax.all_to_all(packed, 'cent', 0, 0, tiled=True)  16.7 us
    dot_general x2, matrix products, score_block(): lax.dot_general(members, cent_block, (((1,), (1,)), ((), ())), preferred_...  16.2 us
    all_to_all x1, blocking collectives, group_log_total(): lax.all_to_all(spread, 'cent', 0, 0, tiled=True)  13.2 us
  transfers between devices with their start and end apart: 4, of which 3 were waited for; matrix products, arithmetic and copies ran while one was open for 2% of the time, Pallas kernels for 0%

profile of v3, /device:TPU:1, one launch (start us, length us, event | category | flops | bytes accessed | tf_op | source)
XLA Modules:
  0.0 188.7 jit_solution(8039333075859577558)
XLA Ops:
  7.2 0.0 all-gather.2.cloned.1.call-start
  7.2 0.7 all-gather.2.cloned.1.call-update
  7.9 1.3 multiply_reduce_fusion.1
  9.2 1.5 collective-permute-start
  10.6 1.3 collective-permute-done
  12.0 0.2 multiply_reduce_fusion
  12.1 92.6 %all-gather.2.cloned.1.call-done = bf16[8192,768]{1,0:T(8,128)(2,1)} async-done(((bf16[128,768]{1,0:T(8,128)(2,1)}), bf16[8192,768]{1,0:T(8,128)(2,1)}) %all-gather.2.cloned.1.call-update) | async-done | bytes 12582928 | tf_op jit(solution)/shard_map/all_gather | solution.py:46
  104.7 6.6 %fusion.8 = (f32[8192]{0:T(1024)S(1)}, f32[8192,256]{0,1:T(8,128)S(1)}) fusion(f32[256]{0:T(256)S(1)} %multiply_reduce_fusion, bf16[8192,768]{1,0:T(8,128)(2,1)} %all-gather.2.cloned.1.call-done, bf16[256,768]{1,0:T(8,128)(2,1)S(1)} %collective-permute-done), kind=kOutput, calls=%fused_computation.23 | convolution fusion | flops 3229605888 | bytes 21398528 | tf_op jit(solution)/shard_map/dot_general | solution.py:11
  111.3 0.0 copy-start.2
  111.3 9.6 %fusion.9 = (f32[8192]{0:T(1024)S(1)}, f32[8192,256]{0,1:T(8,128)S(1)}) fusion(f32[256]{0:T(256)S(1)} %get-tuple-element.6, bf16[8192,768]{1,0:T(8,128)(2,1)} %all-gather.2.cloned.1.call-done, bf16[256,768]{1,0:T(8,128)(2,1)S(1)} %get-tuple-element.7), kind=kOutput, calls=%fused_computation.24 | convolution fusion | flops 3229605888 | bytes 21398528 | tf_op jit(solution)/shard_map/dot_general | solution.py:11
  120.9 0.0 copy-start
  120.9 0.0 copy-done.2
  120.9 2.4 %exponential_reduce_fusion = (f32[8192]{0:T(1024)S(1)}, f32[8192]{0:T(1024)S(1)}) fusion(f32[8192,256]{0,1:T(8,128)S(1)} %get-tuple-element.13, f32[8192]{0:T(1024)S(1)} %max.17, f32[8192,256]{0,1:T(8,128)S(1)} %get-tuple-element.11), kind=kLoop, calls=%fused_computation.10 | loop fusion | flops 8372224 | bytes 16875520 | tf_op jit(solution)/shard_map/reduce_sum | solution.py:51
  123.4 0.8 copy-done
  124.2 0.1 pad_maximum_fusion
  124.3 16.7 %all_to_all.11 = f32[64,2,128]{2,1,0:T(2,128)S(1)} all-to-all(f32[64,2,128]{2,1,0:T(2,128)S(1)} %pad_maximum_fusion), channel_id=1, replica_groups=mesh['dp'=2,'cent'=64] {'cent'}, dimensions={0} | all-to-all | bytes 131072 | tf_op jit(solution)/shard_map/all_to_all | solution.py:22
  140.9 0.1 fusion.7
  141.1 0.0 copy-start.5
  141.1 13.2 %all_to_all.12 = f32[64,1,128]{2,1,0:T(1,128)S(1)} all-to-all(f32[64,1,128]{2,1,0:T(1,128)S(1)} %broadcast_in_dim.2), channel_id=1, replica_groups=mesh['dp'=2,'cent'=64] {'cent'}, dimensions={0} | all-to-all | bytes 65536 | tf_op jit(solution)/shard_map/all_to_all | solution.py:28
  154.3 0.0 copy-start.1
  154.3 0.0 copy-start.3
  154.3 10.0 %fusion.6 = f32[256,768]{1,0:T(8,128)S(1)} fusion(bf16[8192,768]{1,0:T(8,128)(2,1)} %all-gather.2.cloned.1.call-done, f32[8192,256]{0,1:T(8,128)} %copy-done.2, f32[8192]{0:T(1024)S(1)} %bitcast.16), kind=kOutput, calls=%fused_computation.15 | convolution fusion | flops 3225419776 | bytes 21790720 | tf_op jit(solution)/shard_map/dot_general | solution.py:34
  164.3 0.0 copy-done.5
  164.3 0.0 copy-start.4
  164.3 3.5 %collective-permute-start.1 = (f32[256,768]{1,0:T(8,128)S(1)}, f32[256,768]{1,0:T(8,128)S(1)}, u32[]{:S(2)}, u32[]{:S(2)}) collective-permute-start(f32[256,768]{1,0:T(8,128)S(1)} %fusion.6), channel_id=1, source_target_pairs={{0,64},{64,0},{1,65},{65,1},{2,66},{66,2},{3,67},{67,3},{4,68},{68... | collective-permute-start | bytes 2359304 | tf_op jit(solution)/shard_map/ppermute | solution.py:56
  167.8 0.0 copy-done.1
  167.8 0.0 copy-done.3
  167.8 2.4 %convert_reduce_fusion = (f32[256]{0:T(256)S(1)}, f32[256]{0:T(256)S(1)}) fusion(f32[8192,256]{0,1:T(8,128)S(1)} %copy-done.3, f32[8192]{0:T(1024)S(1)} %bitcast.17, f32[8192,256]{0,1:T(8,128)S(1)} %copy-done.1), kind=kLoop, calls=%fused_computation.6 | loop fusion | flops 16776704 | bytes 16812032 | tf_op jit(solution)/shard_map/reduce_sum | solution.py:37
  170.2 1.9 %collective-permute-start.2 = (f32[256]{0:T(256)S(1)}, f32[256]{0:T(256)S(1)}, u32[]{:S(2)}, u32[]{:S(2)}) collective-permute-start(f32[256]{0:T(256)S(1)} %get-tuple-element.2), channel_id=1, source_target_pairs={{0,64},{64,0},{1,65},{65,1},{2,66},{66,2},{3,67},{67,3},{4,68},{68... | collective-permute-start | bytes 3080 | tf_op jit(solution)/shard_map/ppermute | solution.py:57
  172.1 0.8 collective-permute-done.2
  173.0 0.0 collective-permute-done.1
  173.0 0.0 copy-done.4
  173.0 8.9 %fusion.5 = f32[256,768]{1,0:T(8,128)} fusion(f32[256,768]{1,0:T(8,128)S(1)} %copy-done.4, f32[256,768]{1,0:T(8,128)S(1)} %collective-permute-done.1, bf16[8192,768]{1,0:T(8,128)(2,1)} %all-gather.2.cloned.1.call-done, f32[8192,256]{0,1:T(8,128)S(1)} %copy-done.1, f32[8192]{0:T(1024)S(1)} %bitcast.18, f32[256]{0:T(256)S(1)} %add_add_fusion), kind=kOutput, calls=%fused_computation.14 | convolution fusion | flops 3226009600 | bytes 23364608 | tf_op jit(solution)/shard_map/dot_general | solution.py:34
  (7 shorter events, 0.1 us)
Async XLA Ops:
  7.2 97.6 %all-gather.2.cloned.1.call-start = ((), (), s32[]{:S(2)}) async-start(), calls=%async_computation.2 | async-start | bytes 12779520 | tf_op jit(solution)/shard_map/all_gather | solution.py:46
  9.2 2.8 %collective-permute-start = (bf16[256,768]{1,0:T(8,128)(2,1)S(1)}, bf16[256,768]{1,0:T(8,128)(2,1)S(1)}, u32[]{:S(2)}, u32[]{:S(2)}) collective-permute-start(bf16[256,768]{1,0:T(8,128)(2,1)S(1)} %get-tuple-element.7), channel_id=1, source_target_pairs={{0,64},{64,0},{1,65},{65,1},{2,66},{66,2},{3,67},{67,3},{4,68},{68... | collective-permute-start | bytes 1179656 | tf_op jit(solution)/shard_map/ppermute | solution.py:47
  111.3 9.6 %copy-start.2 = (f32[8192,256]{0,1:T(8,128)}, f32[8192,256]{0,1:T(8,128)S(1)}, u32[]{:S(2)}) copy-start(f32[8192,256]{0,1:T(8,128)S(1)} %get-tuple-element.11) | copy-start | bytes 25165828
  120.9 3.3 %copy-start = (f32[8192,256]{0,1:T(8,128)}, f32[8192,256]{0,1:T(8,128)S(1)}, u32[]{:S(2)}) copy-start(f32[8192,256]{0,1:T(8,128)S(1)} %get-tuple-element.13) | copy-start | bytes 25165828
  141.1 23.2 %copy-start.5 = (f32[128]{0:T(128)}, f32[128]{0:T(128)S(1)}, u32[]{:S(2)}) copy-start(f32[128]{0:T(128)S(1)} %log_add_fusion) | copy-start | bytes 1540
  154.3 13.5 %copy-start.1 = (f32[8192,256]{0,1:T(8,128)S(1)}, f32[8192,256]{0,1:T(8,128)}, u32[]{:S(2)}) copy-start(f32[8192,256]{0,1:T(8,128)} %copy-done) | copy-start | bytes 25165828
  154.3 13.5 %copy-start.3 = (f32[8192,256]{0,1:T(8,128)S(1)}, f32[8192,256]{0,1:T(8,128)}, u32[]{:S(2)}) copy-start(f32[8192,256]{0,1:T(8,128)} %copy-done.2) | copy-start | bytes 25165828
  164.3 8.6 %copy-start.4 = (f32[256,768]{1,0:T(8,128)S(1)}, f32[256,768]{1,0:T(8,128)}, u32[]{:S(2)}) copy-start(f32[256,768]{1,0:T(8,128)} %param.3) | copy-start | bytes 2359300
  164.3 8.6 %collective-permute-start.1 = (f32[256,768]{1,0:T(8,128)S(1)}, f32[256,768]{1,0:T(8,128)S(1)}, u32[]{:S(2)}, u32[]{:S(2)}) collective-permute-start(f32[256,768]{1,0:T(8,128)S(1)} %fusion.6), channel_id=1, source_target_pairs={{0,64},{64,0},{1,65},{65,1},{2,66},{66,2},{3,67},{67,3},{4,68},{68... | collective-permute-start | bytes 2359304 | tf_op jit(solution)/shard_map/ppermute | solution.py:56
  170.2 2.8 %collective-permute-start.2 = (f32[256]{0:T(256)S(1)}, f32[256]{0:T(256)S(1)}, u32[]{:S(2)}, u32[]{:S(2)}) collective-permute-start(f32[256]{0:T(256)S(1)} %get-tuple-element.2), channel_id=1, source_target_pairs={{0,64},{64,0},{1,65},{65,1},{2,66},{66,2},{3,67},{67,3},{4,68},{68... | collective-permute-start | bytes 3080 | tf_op jit(solution)/shard_map/ppermute | solution.py:57
Sparse Core Ops, SparseCore 0:
  10.7 93.9 all-gather.1

commit v4 on v2

v4 whole, which is shorter than its diff:
```python
import math

import jax
import jax.numpy as jnp
from jax import lax
from jax.sharding import PartitionSpec as P

HALVES = 2


def score_block(members, cent_block, score_scale):
    sq_norm = jnp.sum(jnp.square(cent_block.astype(jnp.float32)), axis=1)
    products = lax.dot_general(
        members, cent_block, (((1,), (1,)), ((), ())), preferred_element_type=jnp.float32
    )
    return (2.0 * products - sq_norm[None, :]) * score_scale


def merge_stats(first, second):
    top = jnp.maximum(first[0], second[0])
    total = first[1] * jnp.exp(first[0] - top) + second[1] * jnp.exp(second[0] - top)
    return jnp.stack([top, total])


def group_log_total(local_max, local_sum):
    cent_count = lax.axis_size("cent")
    stats = jnp.stack([local_max, local_sum])
    bit = 1
    while bit < cent_count:
        partner = lax.ppermute(stats, "cent", [(i, i ^ bit) for i in range(cent_count)])
        stats = merge_stats(stats, partner)
        bit *= 2
    return stats[0] + jnp.log(stats[1])


def on_device(points, centroids):
    feature_width = centroids.shape[1]
    own_points = points.shape[0]
    score_scale = 7.0 / math.sqrt(feature_width)
    swap = [(0, 1), (1, 0)]
    copies = centroids.astype(jnp.bfloat16)
    members = lax.all_gather(points, "cent", axis=0, tiled=True)
    other_copies = lax.ppermute(copies, "dp", swap)
    both = jnp.concatenate([other_copies, copies], axis=0)
    own_rows = copies.shape[0]
    span = members.shape[0] // HALVES
    halves = [members[index_h * span : (index_h + 1) * span] for index_h in range(HALVES)]
    scores = [score_block(half, both, score_scale) for half in halves]
    totals = []
    for part in scores:
        local_max = jnp.max(part, axis=1)
        local_sum = jnp.sum(jnp.exp(part - local_max[:, None]), axis=1)
        totals.append(group_log_total(local_max, local_sum))
    sums = None
    counts = None
    for part, total, half in zip(scores, totals, halves):
        weights = jnp.exp(part - total[:, None]).astype(jnp.bfloat16)
        part_sums = lax.dot_general(
            weights, half, (((0,), (0,)), ((), ())), preferred_element_type=jnp.float32
        )
        part_counts = jnp.sum(weights, axis=0, dtype=jnp.float32)
        sums = part_sums if sums is None else sums + part_sums
        counts = part_counts if counts is None else counts + part_counts
    sent_sums = lax.ppermute(sums[:own_rows], "dp", swap)
    sent_counts = lax.ppermute(counts[:own_rows], "dp", swap)
    own_sums = sums[own_rows:] + sent_sums
    own_counts = counts[own_rows:] + sent_counts
    new_centroids = (own_sums + centroids) / (own_counts[:, None] + 1.0)
    log_total = jnp.concatenate(totals)
    own_total = lax.dynamic_slice_in_dim(log_total, lax.axis_index("cent") * own_points, own_points)
    return (new_centroids, own_total)


def solution(mesh):
    placed = (P(("dp", "cent"), None), P(("dp", "cent"), None))
    return jax.shard_map(
        on_device,
        mesh=mesh,
        in_specs=placed,
        out_specs=(P(("dp", "cent"), None), P(("dp", "cent"))),
        check_vma=False,
    )
```

time: 231 us -> 174 us (0.75)
  other arithmetic: 23.6 us -> 9.11 us
  local copies, waits for them, and re-layouts: 13.8 us -> 0.12 us
  blocking collectives: 10.2 us -> 0 us
  waiting for transfers between devices: 109 us -> 100 us
  matrix products: 31.7 us -> 23.8 us
    all_to_all x4 -> x0, starting transfers between devices: 27.5 us -> none  [the longest x2 18.1 us: group_log_total(): parts = lax.all_to_all(packed, 'cent', 0, 0, tiled=True)]
    ppermute x0 -> x15, starting transfers between devices: none -> 26.5 us  [the longest x12 18.1 us: group_log_total(): lax.ppermute(stats, 'cent', [(i, i ^ bit) for i in range(cent_count)])]
    all_to_all x4 -> x0, waiting for transfers between devices: 14.3 us -> none  [the longest x2 7.39 us: group_log_total(): lax.all_to_all(spread, 'cent', 0, 0, tiled=True)]
    slice x3 -> x4, local copies, waits for them, and re-layouts: 8.75 us -> 0.11 us  [the longest x2 0.05 us: merge_stats(): top = jnp.maximum(first[0], second[0])]
    ppermute x0 -> x15, waiting for transfers between devices: none -> 7.04 us  [the longest x12 5.14 us: group_log_total(): lax.ppermute(stats, 'cent', [(i, i ^ bit) for i in range(cent_count)])]
    unnamed x1 -> x0, blocking collectives: 6.87 us -> none
    reduce_sum x4 -> x2, other arithmetic: 9.14 us -> 2.51 us  [on_device(): local_sum = jnp.sum(jnp.exp(part - local_max[:, None]), axis=1)]
    dot_general x2, matrix products: 17.5 us -> 12.5 us  [on_device(): lax.dot_general(weights, half, (((0,), (0,)), ((), ())), preferred_elemen...]
  transfers between devices with their start and end apart: 6 -> 16, of which waited for: 4 -> 8; matrix products, arithmetic and copies ran while one was open for 15% -> 7% of each run, Pallas kernels for 0% -> 0%
where the time goes in v4:
time: 174 us
  waiting for transfers between devices  100 us (57%)
  starting transfers between devices  26.6 us (15%)
  matrix products  23.8 us (14%)
  between operations  14.2 us (8%)
  other arithmetic  9.11 us (5%)
    all_gather x1, waiting for transfers between devices, on_device(): members = lax.all_gather(points, 'cent', axis=0, tiled=True)  92.6 us
    ppermute x12, starting transfers between devices, group_log_total(): lax.ppermute(stats, 'cent', [(i, i ^ bit) for i in range(cent_count)])  18.1 us
    dot_general x2, matrix products, on_device(): lax.dot_general(weights, half, (((0,), (0,)), ((), ())), preferred_elemen...  12.5 us
    dot_general x2, matrix products, score_block(): lax.dot_general(members, cent_block, (((1,), (1,)), ((), ())), preferred_...  11.3 us
    ppermute x1, starting transfers between devices, on_device(): sent_sums = lax.ppermute(sums[:own_rows], 'dp', swap)  6.88 us
    ppermute x12, waiting for transfers between devices, group_log_total(): lax.ppermute(stats, 'cent', [(i, i ^ bit) for i in range(cent_count)])  5.14 us
  transfers between devices with their start and end apart: 16, of which 8 were waited for; matrix products, arithmetic and copies ran while one was open for 7% of the time, Pallas kernels for 0%

profile of v4, /device:TPU:1, one launch (start us, length us, event | category | flops | bytes accessed | tf_op | source)
XLA Modules:
  0.0 174.1 jit_solution(2426358436324475737)
XLA Ops:
  7.2 0.7 all-gather.2.cloned.1.call-update
  7.9 1.2 convert_element_type.19
  9.1 1.5 collective-permute-start
  10.5 1.3 collective-permute-done
  11.9 0.2 multiply_reduce_fusion
  12.1 92.6 %all-gather.2.cloned.1.call-done = bf16[8192,768]{1,0:T(8,128)(2,1)} async-done(((bf16[128,768]{1,0:T(8,128)(2,1)}), bf16[8192,768]{1,0:T(8,128)(2,1)}) %all-gather.2.cloned.1.call-update) | async-done | bytes 12582928 | tf_op jit(solution)/shard_map/all_gather | solution.py:42
  104.7 5.6 %fusion.40 = (f32[4096]{0:T(1024)S(1)}, f32[512,4096]{1,0:T(8,128)S(1)}) fusion(f32[512]{0:T(512)S(1)} %multiply_reduce_fusion, bf16[8192,768]{1,0:T(8,128)(2,1)} %all-gather.2.cloned.1.call-done, bf16[256,768]{1,0:T(8,128)(2,1)S(1)} %convert_element_type.19, bf16[256,768]{1,0:T(8,128)(2,1)S(1)} %collective-permute-done), kind=kOutput, calls=%fused_computation.98 | convolution fusion | flops 3231182848 | bytes 15484928 | tf_op jit(solution)/shard_map/dot_general | solution.py:13
  110.3 1.3 exponential_reduce_fusion
  111.6 1.3 collective-permute-start.7
  112.9 5.6 %fusion.41 = (f32[4096]{0:T(1024)S(1)}, f32[512,4096]{1,0:T(8,128)S(1)}) fusion(f32[512]{0:T(512)S(1)} %multiply_reduce_fusion, bf16[8192,768]{1,0:T(8,128)(2,1)} %all-gather.2.cloned.1.call-done, bf16[256,768]{1,0:T(8,128)(2,1)S(1)} %convert_element_type.19, bf16[256,768]{1,0:T(8,128)(2,1)S(1)} %collective-permute-done), kind=kOutput, calls=%fused_computation.99 | convolution fusion | flops 3231182848 | bytes 15484928 | tf_op jit(solution)/shard_map/dot_general | solution.py:13
  118.6 1.3 exponential_reduce_fusion.1
  119.9 0.4 collective-permute-start.1
  120.2 0.1 multiply_add_fusion.4
  120.3 2.8 %collective-permute-start.8 = (f32[2,4096]{1,0:T(2,128)S(1)}, f32[2,4096]{1,0:T(2,128)S(1)}, u32[]{:S(2)}, u32[]{:S(2)}) collective-permute-start(f32[2,4096]{1,0:T(2,128)S(1)} %pad_maximum_fusion.10), channel_id=1, source_target_pairs={{0,2},{1,3},{2,0},{3,1},{4,6},{5,7},{6,4},{7,5},{8,10},{9,11},{10,... | collective-permute-start | bytes 98312 | tf_op jit(solution)/shard_map/ppermute | solution.py:30
  123.1 0.1 multiply_add_fusion.9
  123.2 2.1 %collective-permute-start.2 = (f32[2,4096]{1,0:T(2,128)S(1)}, f32[2,4096]{1,0:T(2,128)S(1)}, u32[]{:S(2)}, u32[]{:S(2)}) collective-permute-start(f32[2,4096]{1,0:T(2,128)S(1)} %pad_maximum_fusion.4), channel_id=1, source_target_pairs={{0,2},{1,3},{2,0},{3,1},{4,6},{5,7},{6,4},{7,5},{8,10},{9,11},{10,... | collective-permute-start | bytes 98312 | tf_op jit(solution)/shard_map/ppermute | solution.py:30
  125.3 0.1 multiply_add_fusion.3
  125.4 1.3 collective-permute-start.9
  126.7 0.9 collective-permute-done.2
  127.6 0.1 multiply_add_fusion.8
  127.7 1.3 collective-permute-start.3
  129.0 0.1 multiply_add_fusion.2
  129.1 2.5 %collective-permute-start.10 = (f32[2,4096]{1,0:T(2,128)S(1)}, f32[2,4096]{1,0:T(2,128)S(1)}, u32[]{:S(2)}, u32[]{:S(2)}) collective-permute-start(f32[2,4096]{1,0:T(2,128)S(1)} %pad_maximum_fusion.12), channel_id=1, source_target_pairs={{0,8},{1,9},{2,10},{3,11},{4,12},{5,13},{6,14},{7,15},{8,0},{9,1},... | collective-permute-start | bytes 98312 | tf_op jit(solution)/shard_map/ppermute | solution.py:30
  131.6 0.1 multiply_add_fusion.7
  131.7 1.7 collective-permute-start.4
  133.5 0.2 collective-permute-done.10
  133.6 0.1 multiply_add_fusion.1
  133.7 0.4 collective-permute-start.11
  134.2 2.1 %collective-permute-done.4 = f32[2,4096]{1,0:T(2,128)S(1)} collective-permute-done((f32[2,4096]{1,0:T(2,128)S(1)}, f32[2,4096]{1,0:T(2,128)S(1)}, u32[]{:S(2)}, u32[]{:S(2)}) %collective-permute-start.4) | collective-permute-done | bytes 32800 | tf_op jit(solution)/shard_map/ppermute | solution.py:30
  136.3 0.1 multiply_add_fusion.6
  136.4 0.4 collective-permute-start.5
  136.9 0.1 slice_maximum_fusion
  137.0 2.3 %collective-permute-start.12 = (f32[2,4096]{1,0:T(2,128)S(1)}, f32[2,4096]{1,0:T(2,128)S(1)}, u32[]{:S(2)}, u32[]{:S(2)}) collective-permute-start(f32[2,4096]{1,0:T(2,128)S(1)} %pad_maximum_fusion.14), channel_id=1, source_target_pairs={{0,32},{1,33},{2,34},{3,35},{4,36},{5,37},{6,38},{7,39},{8,40},{9,... | collective-permute-start | bytes 98312 | tf_op jit(solution)/shard_map/ppermute | solution.py:30
  139.3 0.3 collective-permute-done.5
  139.6 0.1 slice_maximum_fusion.5
  139.7 1.6 collective-permute-start.6
  141.4 0.1 log_add_fusion
  141.4 1.2 convert_reduce_fusion
  142.6 1.6 collective-permute-done.6
  144.2 0.1 log_add_fusion.1
  144.3 6.3 %fusion = f32[512,768]{1,0:T(8,128)S(1)} fusion(bf16[8192,768]{1,0:T(8,128)(2,1)} %all-gather.2.cloned.1.call-done, f32[512,4096]{1,0:T(8,128)S(1)} %get-tuple-element.47, f32[4096]{0:T(1024)S(1)} %log_add_fusion), kind=kOutput, calls=%fused_computation.8 | convolution fusion | flops 3225419776 | bytes 16269312 | tf_op jit(solution)/shard_map/dot_general | solution.py:58
  150.6 6.2 %fusion.6 = f32[512,768]{1,0:T(8,128)S(1)} fusion(f32[512,768]{1,0:T(8,128)S(1)} %fusion, bf16[8192,768]{1,0:T(8,128)(2,1)} %all-gather.2.cloned.1.call-done, f32[512,4096]{1,0:T(8,128)S(1)} %get-tuple-element.49, f32[4096]{0:T(1024)S(1)} %log_add_fusion.1), kind=kOutput, calls=%fused_computation.15 | convolution fusion | flops 3225812992 | bytes 17842176 | tf_op jit(solution)/shard_map/dot_general | solution.py:58
  156.9 6.9 %collective-permute-start.13 = (f32[256,768]{1,0:T(8,128)S(1)}, f32[256,768]{1,0:T(8,128)S(1)}, u32[]{:S(2)}, u32[]{:S(2)}) collective-permute-start(f32[256,768]{1,0:T(8,128)S(1)} %slice.159), channel_id=1, source_target_pairs={{0,64},{64,0},{1,65},{65,1},{2,66},{66,2},{3,67},{67,3},{4,68},{68... | collective-permute-start | bytes 2359304 | tf_op jit(solution)/shard_map/ppermute | solution.py:64
  163.8 1.2 convert_reduce_fusion.1
  165.0 0.1 collective-permute-start.14
  165.1 0.6 fusion.35
  165.7 0.6 collective-permute-done.14
  166.2 1.0 fusion.10
  (29 shorter events, 0.7 us)
Async XLA Ops:
  7.2 97.5 %all-gather.2.cloned.1.call-start = ((), (), s32[]{:S(2)}) async-start(), calls=%async_computation | async-start | bytes 12779520 | tf_op jit(solution)/shard_map/all_gather | solution.py:42
  9.1 2.8 %collective-permute-start = (bf16[256,768]{1,0:T(8,128)(2,1)S(1)}, bf16[256,768]{1,0:T(8,128)(2,1)S(1)}, u32[]{:S(2)}, u32[]{:S(2)}) collective-permute-start(bf16[256,768]{1,0:T(8,128)(2,1)S(1)} %convert_element_type.19), channel_id=1, source_target_pairs={{0,64},{64,0},{1,65},{65,1},{2,66},{66,2},{3,67},{67,3},{4,68},{68... | collective-permute-start | bytes 1179656 | tf_op jit(solution)/shard_map/ppermute | solution.py:43
  111.6 8.6 %collective-permute-start.7 = (f32[2,4096]{1,0:T(2,128)S(1)}, f32[2,4096]{1,0:T(2,128)S(1)}, u32[]{:S(2)}, u32[]{:S(2)}) collective-permute-start(f32[2,4096]{1,0:T(2,128)S(1)} %pad_maximum_fusion.9), channel_id=1, source_target_pairs={{0,1},{1,0},{2,3},{3,2},{4,5},{5,4},{6,7},{7,6},{8,9},{9,8},{10,11... | collective-permute-start | bytes 98312 | tf_op jit(solution)/shard_map/ppermute | solution.py:30
  119.9 3.3 %collective-permute-start.1 = (f32[2,4096]{1,0:T(2,128)S(1)}, f32[2,4096]{1,0:T(2,128)S(1)}, u32[]{:S(2)}, u32[]{:S(2)}) collective-permute-start(f32[2,4096]{1,0:T(2,128)S(1)} %pad_maximum_fusion.3), channel_id=1, source_target_pairs={{0,1},{1,0},{2,3},{3,2},{4,5},{5,4},{6,7},{7,6},{8,9},{9,8},{10,11... | collective-permute-start | bytes 98312 | tf_op jit(solution)/shard_map/ppermute | solution.py:30
  120.3 5.0 %collective-permute-start.8 = (f32[2,4096]{1,0:T(2,128)S(1)}, f32[2,4096]{1,0:T(2,128)S(1)}, u32[]{:S(2)}, u32[]{:S(2)}) collective-permute-start(f32[2,4096]{1,0:T(2,128)S(1)} %pad_maximum_fusion.10), channel_id=1, source_target_pairs={{0,2},{1,3},{2,0},{3,1},{4,6},{5,7},{6,4},{7,5},{8,10},{9,11},{10,... | collective-permute-start | bytes 98312 | tf_op jit(solution)/shard_map/ppermute | solution.py:30
  123.2 4.3 %collective-permute-start.2 = (f32[2,4096]{1,0:T(2,128)S(1)}, f32[2,4096]{1,0:T(2,128)S(1)}, u32[]{:S(2)}, u32[]{:S(2)}) collective-permute-start(f32[2,4096]{1,0:T(2,128)S(1)} %pad_maximum_fusion.4), channel_id=1, source_target_pairs={{0,2},{1,3},{2,0},{3,1},{4,6},{5,7},{6,4},{7,5},{8,10},{9,11},{10,... | collective-permute-start | bytes 98312 | tf_op jit(solution)/shard_map/ppermute | solution.py:30
  125.4 3.6 %collective-permute-start.9 = (f32[2,4096]{1,0:T(2,128)S(1)}, f32[2,4096]{1,0:T(2,128)S(1)}, u32[]{:S(2)}, u32[]{:S(2)}) collective-permute-start(f32[2,4096]{1,0:T(2,128)S(1)} %pad_maximum_fusion.11), channel_id=1, source_target_pairs={{0,4},{1,5},{2,6},{3,7},{4,0},{5,1},{6,2},{7,3},{8,12},{9,13},{10,... | collective-permute-start | bytes 98312 | tf_op jit(solution)/shard_map/ppermute | solution.py:30
  127.7 3.9 %collective-permute-start.3 = (f32[2,4096]{1,0:T(2,128)S(1)}, f32[2,4096]{1,0:T(2,128)S(1)}, u32[]{:S(2)}, u32[]{:S(2)}) collective-permute-start(f32[2,4096]{1,0:T(2,128)S(1)} %pad_maximum_fusion.5), channel_id=1, source_target_pairs={{0,4},{1,5},{2,6},{3,7},{4,0},{5,1},{6,2},{7,3},{8,12},{9,13},{10,... | collective-permute-start | bytes 98312 | tf_op jit(solution)/shard_map/ppermute | solution.py:30
  129.1 4.6 %collective-permute-start.10 = (f32[2,4096]{1,0:T(2,128)S(1)}, f32[2,4096]{1,0:T(2,128)S(1)}, u32[]{:S(2)}, u32[]{:S(2)}) collective-permute-start(f32[2,4096]{1,0:T(2,128)S(1)} %pad_maximum_fusion.12), channel_id=1, source_target_pairs={{0,8},{1,9},{2,10},{3,11},{4,12},{5,13},{6,14},{7,15},{8,0},{9,1},... | collective-permute-start | bytes 98312 | tf_op jit(solution)/shard_map/ppermute | solution.py:30
  131.7 4.6 %collective-permute-start.4 = (f32[2,4096]{1,0:T(2,128)S(1)}, f32[2,4096]{1,0:T(2,128)S(1)}, u32[]{:S(2)}, u32[]{:S(2)}) collective-permute-start(f32[2,4096]{1,0:T(2,128)S(1)} %pad_maximum_fusion.6), channel_id=1, source_target_pairs={{0,8},{1,9},{2,10},{3,11},{4,12},{5,13},{6,14},{7,15},{8,0},{9,1},... | collective-permute-start | bytes 98312 | tf_op jit(solution)/shard_map/ppermute | solution.py:30
  133.7 3.1 %collective-permute-start.11 = (f32[2,4096]{1,0:T(2,128)S(1)}, f32[2,4096]{1,0:T(2,128)S(1)}, u32[]{:S(2)}, u32[]{:S(2)}) collective-permute-start(f32[2,4096]{1,0:T(2,128)S(1)} %pad_maximum_fusion.13), channel_id=1, source_target_pairs={{0,16},{1,17},{2,18},{3,19},{4,20},{5,21},{6,22},{7,23},{8,24},{9,... | collective-permute-start | bytes 98312 | tf_op jit(solution)/shard_map/ppermute | solution.py:30
  136.4 3.1 %collective-permute-start.5 = (f32[2,4096]{1,0:T(2,128)S(1)}, f32[2,4096]{1,0:T(2,128)S(1)}, u32[]{:S(2)}, u32[]{:S(2)}) collective-permute-start(f32[2,4096]{1,0:T(2,128)S(1)} %pad_maximum_fusion.7), channel_id=1, source_target_pairs={{0,16},{1,17},{2,18},{3,19},{4,20},{5,21},{6,22},{7,23},{8,24},{9,... | collective-permute-start | bytes 98312 | tf_op jit(solution)/shard_map/ppermute | solution.py:30
  137.0 4.3 %collective-permute-start.12 = (f32[2,4096]{1,0:T(2,128)S(1)}, f32[2,4096]{1,0:T(2,128)S(1)}, u32[]{:S(2)}, u32[]{:S(2)}) collective-permute-start(f32[2,4096]{1,0:T(2,128)S(1)} %pad_maximum_fusion.14), channel_id=1, source_target_pairs={{0,32},{1,33},{2,34},{3,35},{4,36},{5,37},{6,38},{7,39},{8,40},{9,... | collective-permute-start | bytes 98312 | tf_op jit(solution)/shard_map/ppermute | solution.py:30
  139.7 4.5 %collective-permute-start.6 = (f32[2,4096]{1,0:T(2,128)S(1)}, f32[2,4096]{1,0:T(2,128)S(1)}, u32[]{:S(2)}, u32[]{:S(2)}) collective-permute-start(f32[2,4096]{1,0:T(2,128)S(1)} %pad_maximum_fusion.8), channel_id=1, source_target_pairs={{0,32},{1,33},{2,34},{3,35},{4,36},{5,37},{6,38},{7,39},{8,40},{9,... | collective-permute-start | bytes 98312 | tf_op jit(solution)/shard_map/ppermute | solution.py:30
  156.8 9.4 %copy-start = (f32[256,768]{1,0:T(8,128)S(1)}, f32[256,768]{1,0:T(8,128)}, u32[]{:S(2)}) copy-start(f32[256,768]{1,0:T(8,128)} %param.3) | copy-start | bytes 2359300
  156.9 9.3 %collective-permute-start.13 = (f32[256,768]{1,0:T(8,128)S(1)}, f32[256,768]{1,0:T(8,128)S(1)}, u32[]{:S(2)}, u32[]{:S(2)}) collective-permute-start(f32[256,768]{1,0:T(8,128)S(1)} %slice.159), channel_id=1, source_target_pairs={{0,64},{64,0},{1,65},{65,1},{2,66},{66,2},{3,67},{67,3},{4,68},{68... | collective-permute-start | bytes 2359304 | tf_op jit(solution)/shard_map/ppermute | solution.py:64
  165.0 1.2 collective-permute-start.14
Sparse Core Ops, SparseCore 0:
  10.7 93.9 all-gather.1

commit v5 on v4

--- a/solution.py
+++ b/solution.py
@@ -46,11 +46,12 @@
     span = members.shape[0] // HALVES
     halves = [members[index_h * span : (index_h + 1) * span] for index_h in range(HALVES)]
     scores = [score_block(half, both, score_scale) for half in halves]
-    totals = []
-    for part in scores:
-        local_max = jnp.max(part, axis=1)
-        local_sum = jnp.sum(jnp.exp(part - local_max[:, None]), axis=1)
-        totals.append(group_log_total(local_max, local_sum))
+    local_max = jnp.concatenate([jnp.max(part, axis=1) for part in scores])
+    local_sum = jnp.concatenate(
+        [jnp.sum(jnp.exp(part - top[:, None]), axis=1) for part, top in zip(scores, jnp.split(local_max, HALVES))]
+    )
+    log_total = group_log_total(local_max, local_sum)
+    totals = jnp.split(log_total, HALVES)
     sums = None
     counts = None
     for part, total, half in zip(scores, totals, halves):
@@ -66,7 +67,6 @@
     own_sums = sums[own_rows:] + sent_sums
     own_counts = counts[own_rows:] + sent_counts
     new_centroids = (own_sums + centroids) / (own_counts[:, None] + 1.0)
-    log_total = jnp.concatenate(totals)
     own_total = lax.dynamic_slice_in_dim(log_total, lax.axis_index("cent") * own_points, own_points)
     return (new_centroids, own_total)
 

time: 174 us -> 177 us (1.017)
  waiting for transfers between devices: 100 us -> 107 us
  starting transfers between devices: 26.6 us -> 21.6 us
    ppermute x12 -> x6, waiting for transfers between devices: 5.14 us -> 11.7 us  [group_log_total(): lax.ppermute(stats, 'cent', [(i, i ^ bit) for i in range(cent_count)])]
    ppermute x12 -> x6, starting transfers between devices: 18.1 us -> 12.2 us  [group_log_total(): lax.ppermute(stats, 'cent', [(i, i ^ bit) for i in range(cent_count)])]
  transfers between devices with their start and end apart: 16 -> 10, of which waited for: 8 -> 9; matrix products, arithmetic and copies ran while one was open for 7% -> 3% of each run, Pallas kernels for 0% -> 0%
where the time goes in v5:
time: 177 us
  waiting for transfers between devices  107 us (60%)
  matrix products  23.8 us (13%)
  starting transfers between devices  21.6 us (12%)
  between operations  14.2 us (8%)
  other arithmetic  9.47 us (5%)
    all_gather x1, waiting for transfers between devices, on_device(): members = lax.all_gather(points, 'cent', axis=0, tiled=True)  92.6 us
    dot_general x2, matrix products, on_device(): lax.dot_general(weights, half, (((0,), (0,)), ((), ())), preferred_elemen...  12.5 us
    ppermute x6, starting transfers between devices, group_log_total(): lax.ppermute(stats, 'cent', [(i, i ^ bit) for i in range(cent_count)])  12.2 us
    ppermute x6, waiting for transfers between devices, group_log_total(): lax.ppermute(stats, 'cent', [(i, i ^ bit) for i in range(cent_count)])  11.7 us
    dot_general x2, matrix products, score_block(): lax.dot_general(members, cent_block, (((1,), (1,)), ((), ())), preferred_...  11.3 us
    ppermute x1, starting transfers between devices, on_device(): sent_sums = lax.ppermute(sums[:own_rows], 'dp', swap)  7.81 us
  transfers between devices with their start and end apart: 10, of which 9 were waited for; matrix products, arithmetic and copies ran while one was open for 3% of the time, Pallas kernels for 0%

profile of v5, /device:TPU:1, one launch (start us, length us, event | category | flops | bytes accessed | tf_op | source)
XLA Modules:
  0.0 176.6 jit_solution(18014311262449881636)
XLA Ops:
  7.2 0.0 all-gather.2.cloned.1.call-start
  7.2 0.7 all-gather.2.cloned.1.call-update
  7.9 1.2 convert_element_type.19
  9.1 1.5 collective-permute-start
  10.5 1.3 collective-permute-done
  11.9 0.2 multiply_reduce_fusion
  12.1 92.6 %all-gather.2.cloned.1.call-done = bf16[8192,768]{1,0:T(8,128)(2,1)} async-done(((bf16[128,768]{1,0:T(8,128)(2,1)}), bf16[8192,768]{1,0:T(8,128)(2,1)}) %all-gather.2.cloned.1.call-update) | async-done | bytes 12582928 | tf_op jit(solution)/shard_map/all_gather | solution.py:42
  104.7 5.6 %fusion.30 = (f32[4096]{0:T(1024)S(1)}, f32[512,4096]{1,0:T(8,128)S(1)}) fusion(f32[512]{0:T(512)S(1)} %multiply_reduce_fusion, bf16[8192,768]{1,0:T(8,128)(2,1)} %all-gather.2.cloned.1.call-done, bf16[256,768]{1,0:T(8,128)(2,1)S(1)} %convert_element_type.19, bf16[256,768]{1,0:T(8,128)(2,1)S(1)} %collective-permute-done), kind=kOutput, calls=%fused_computation.64 | convolution fusion | flops 3231182848 | bytes 15484928 | tf_op jit(solution)/shard_map/dot_general | solution.py:13
  110.3 5.6 %fusion.31 = (f32[4096]{0:T(1024)S(1)}, f32[512,4096]{1,0:T(8,128)S(1)}) fusion(f32[512]{0:T(512)S(1)} %multiply_reduce_fusion, bf16[8192,768]{1,0:T(8,128)(2,1)} %all-gather.2.cloned.1.call-done, bf16[256,768]{1,0:T(8,128)(2,1)S(1)} %convert_element_type.19, bf16[256,768]{1,0:T(8,128)(2,1)S(1)} %collective-permute-done), kind=kOutput, calls=%fused_computation.65 | convolution fusion | flops 3231182848 | bytes 15484928 | tf_op jit(solution)/shard_map/dot_general | solution.py:13
  116.0 2.3 %exponential_reduce_fusion = (f32[4096]{0:T(1024)S(1)}, f32[4096]{0:T(1024)S(1)}) fusion(f32[512,4096]{1,0:T(8,128)S(1)} %get-tuple-element.27, f32[4096]{0:T(1024)S(1)} %get-tuple-element.26, f32[512,4096]{1,0:T(8,128)S(1)} %get-tuple-element.29, f32[4096]{0:T(1024)S(1)} %get-tuple-element.28), kind=kLoop, calls=%fused_computation.4 | loop fusion | flops 8380416 | bytes 16842752 | tf_op jit(solution)/shard_map/reduce_sum | solution.py:51
  118.3 0.1 pad_maximum_fusion.3
  118.4 1.3 collective-permute-start.1
  119.7 1.9 %collective-permute-done.1 = f32[2,8192]{1,0:T(2,128)S(1)} collective-permute-done((f32[2,8192]{1,0:T(2,128)S(1)}, f32[2,8192]{1,0:T(2,128)S(1)}, u32[]{:S(2)}, u32[]{:S(2)}) %collective-permute-start.1) | collective-permute-done | bytes 65568 | tf_op jit(solution)/shard_map/ppermute | solution.py:30
  121.6 0.1 fusion.11
  121.7 0.1 pad_maximum_fusion.4
  121.8 2.8 %collective-permute-start.2 = (f32[2,8192]{1,0:T(2,128)S(1)}, f32[2,8192]{1,0:T(2,128)S(1)}, u32[]{:S(2)}, u32[]{:S(2)}) collective-permute-start(f32[2,8192]{1,0:T(2,128)S(1)} %pad_maximum_fusion.4), channel_id=1, source_target_pairs={{0,2},{1,3},{2,0},{3,1},{4,6},{5,7},{6,4},{7,5},{8,10},{9,11},{10,... | collective-permute-start | bytes 196616 | tf_op jit(solution)/shard_map/ppermute | solution.py:30
  124.6 1.9 %collective-permute-done.2 = f32[2,8192]{1,0:T(2,128)S(1)} collective-permute-done((f32[2,8192]{1,0:T(2,128)S(1)}, f32[2,8192]{1,0:T(2,128)S(1)}, u32[]{:S(2)}, u32[]{:S(2)}) %collective-permute-start.2) | collective-permute-done | bytes 65568 | tf_op jit(solution)/shard_map/ppermute | solution.py:30
  126.5 0.1 multiply_add_fusion.3
  126.6 0.1 pad_maximum_fusion.5
  126.7 1.3 collective-permute-start.3
  128.0 1.9 %collective-permute-done.3 = f32[2,8192]{1,0:T(2,128)S(1)} collective-permute-done((f32[2,8192]{1,0:T(2,128)S(1)}, f32[2,8192]{1,0:T(2,128)S(1)}, u32[]{:S(2)}, u32[]{:S(2)}) %collective-permute-start.3) | collective-permute-done | bytes 65568 | tf_op jit(solution)/shard_map/ppermute | solution.py:30
  129.9 0.1 multiply_add_fusion.2
  130.0 0.1 pad_maximum_fusion.6
  130.1 2.8 %collective-permute-start.4 = (f32[2,8192]{1,0:T(2,128)S(1)}, f32[2,8192]{1,0:T(2,128)S(1)}, u32[]{:S(2)}, u32[]{:S(2)}) collective-permute-start(f32[2,8192]{1,0:T(2,128)S(1)} %pad_maximum_fusion.6), channel_id=1, source_target_pairs={{0,8},{1,9},{2,10},{3,11},{4,12},{5,13},{6,14},{7,15},{8,0},{9,1},... | collective-permute-start | bytes 196616 | tf_op jit(solution)/shard_map/ppermute | solution.py:30
  132.9 1.9 %collective-permute-done.4 = f32[2,8192]{1,0:T(2,128)S(1)} collective-permute-done((f32[2,8192]{1,0:T(2,128)S(1)}, f32[2,8192]{1,0:T(2,128)S(1)}, u32[]{:S(2)}, u32[]{:S(2)}) %collective-permute-start.4) | collective-permute-done | bytes 65568 | tf_op jit(solution)/shard_map/ppermute | solution.py:30
  134.8 0.1 multiply_add_fusion.1
  134.9 0.1 pad_maximum_fusion.7
  135.0 1.1 collective-permute-start.5
  136.1 2.1 %collective-permute-done.5 = f32[2,8192]{1,0:T(2,128)S(1)} collective-permute-done((f32[2,8192]{1,0:T(2,128)S(1)}, f32[2,8192]{1,0:T(2,128)S(1)}, u32[]{:S(2)}, u32[]{:S(2)}) %collective-permute-start.5) | collective-permute-done | bytes 65568 | tf_op jit(solution)/shard_map/ppermute | solution.py:30
  138.2 0.1 slice_maximum_fusion
  138.3 0.1 pad_maximum_fusion.8
  138.4 2.9 %collective-permute-start.6 = (f32[2,8192]{1,0:T(2,128)S(1)}, f32[2,8192]{1,0:T(2,128)S(1)}, u32[]{:S(2)}, u32[]{:S(2)}) collective-permute-start(f32[2,8192]{1,0:T(2,128)S(1)} %pad_maximum_fusion.8), channel_id=1, source_target_pairs={{0,32},{1,33},{2,34},{3,35},{4,36},{5,37},{6,38},{7,39},{8,40},{9,... | collective-permute-start | bytes 196616 | tf_op jit(solution)/shard_map/ppermute | solution.py:30
  141.3 2.0 %collective-permute-done.6 = f32[2,8192]{1,0:T(2,128)S(1)} collective-permute-done((f32[2,8192]{1,0:T(2,128)S(1)}, f32[2,8192]{1,0:T(2,128)S(1)}, u32[]{:S(2)}, u32[]{:S(2)}) %collective-permute-start.6) | collective-permute-done | bytes 65568 | tf_op jit(solution)/shard_map/ppermute | solution.py:30
  143.3 0.1 fusion.28
  143.3 0.1 log_add_fusion
  143.4 6.3 %fusion = f32[512,768]{1,0:T(8,128)S(1)} fusion(bf16[8192,768]{1,0:T(8,128)(2,1)} %all-gather.2.cloned.1.call-done, f32[512,4096]{1,0:T(8,128)S(1)} %get-tuple-element.27, f32[4096]{0:T(1024)S(1)} %get-tuple-element.25), kind=kOutput, calls=%fused_computation.8 | convolution fusion | flops 3225419776 | bytes 16269312 | tf_op jit(solution)/shard_map/dot_general | solution.py:59
  149.7 6.3 %fusion.6 = f32[512,768]{1,0:T(8,128)S(1)} fusion(f32[512,768]{1,0:T(8,128)S(1)} %fusion, bf16[8192,768]{1,0:T(8,128)(2,1)} %all-gather.2.cloned.1.call-done, f32[512,4096]{1,0:T(8,128)S(1)} %get-tuple-element.29, f32[4096]{0:T(1024)S(1)} %get-tuple-element.24), kind=kOutput, calls=%fused_computation.15 | convolution fusion | flops 3225812992 | bytes 17842176 | tf_op jit(solution)/shard_map/dot_general | solution.py:59
  156.0 0.1 slice.93
  156.1 0.0 copy-start
  156.1 7.8 %collective-permute-start.7 = (f32[256,768]{1,0:T(8,128)S(1)}, f32[256,768]{1,0:T(8,128)}, u32[]{:S(2)}, u32[]{:S(2)}) collective-permute-start(f32[256,768]{1,0:T(8,128)S(1)} %slice.93), channel_id=1, source_target_pairs={{0,64},{64,0},{1,65},{65,1},{2,66},{66,2},{3,67},{67,3},{4,68},{68... | collective-permute-start | bytes 2359304 | tf_op jit(solution)/shard_map/ppermute | solution.py:65
  163.9 1.2 convert_reduce_fusion.1
  165.1 1.2 convert_reduce_fusion
  166.4 0.1 collective-permute-start.8
  166.5 0.6 dynamic_slice.3
  167.1 0.6 collective-permute-done.8
  167.6 0.0 collective-permute-done.7
  167.6 0.0 copy-done
  167.6 2.2 %fusion.10 = f32[256,768]{1,0:T(8,128)} fusion(f32[256,768]{1,0:T(8,128)S(1)} %copy-done, f32[256,768]{1,0:T(8,128)} %collective-permute-done.7, f32[512,768]{1,0:T(8,128)S(1)} %fusion.6, f32[256]{0:T(256)S(1)} %add_add_fusion), kind=kLoop, calls=%fused_computation.18 | loop fusion | flops 589824 | bytes 3146752 | tf_op jit(solution)/shard_map/div | solution.py:69
  (6 shorter events, 0.0 us)
Async XLA Ops:
  7.2 97.5 %all-gather.2.cloned.1.call-start = ((), (), s32[]{:S(2)}) async-start(), calls=%async_computation | async-start | bytes 12779520 | tf_op jit(solution)/shard_map/all_gather | solution.py:42
  9.1 2.8 %collective-permute-start = (bf16[256,768]{1,0:T(8,128)(2,1)S(1)}, bf16[256,768]{1,0:T(8,128)(2,1)S(1)}, u32[]{:S(2)}, u32[]{:S(2)}) collective-permute-start(bf16[256,768]{1,0:T(8,128)(2,1)S(1)} %convert_element_type.19), channel_id=1, source_target_pairs={{0,64},{64,0},{1,65},{65,1},{2,66},{66,2},{3,67},{67,3},{4,68},{68... | collective-permute-start | bytes 1179656 | tf_op jit(solution)/shard_map/ppermute | solution.py:43
  118.4 3.2 %collective-permute-start.1 = (f32[2,8192]{1,0:T(2,128)S(1)}, f32[2,8192]{1,0:T(2,128)S(1)}, u32[]{:S(2)}, u32[]{:S(2)}) collective-permute-start(f32[2,8192]{1,0:T(2,128)S(1)} %pad_maximum_fusion.3), channel_id=1, source_target_pairs={{0,1},{1,0},{2,3},{3,2},{4,5},{5,4},{6,7},{7,6},{8,9},{9,8},{10,11... | collective-permute-start | bytes 196616 | tf_op jit(solution)/shard_map/ppermute | solution.py:30
  121.8 4.7 %collective-permute-start.2 = (f32[2,8192]{1,0:T(2,128)S(1)}, f32[2,8192]{1,0:T(2,128)S(1)}, u32[]{:S(2)}, u32[]{:S(2)}) collective-permute-start(f32[2,8192]{1,0:T(2,128)S(1)} %pad_maximum_fusion.4), channel_id=1, source_target_pairs={{0,2},{1,3},{2,0},{3,1},{4,6},{5,7},{6,4},{7,5},{8,10},{9,11},{10,... | collective-permute-start | bytes 196616 | tf_op jit(solution)/shard_map/ppermute | solution.py:30
  126.7 3.2 %collective-permute-start.3 = (f32[2,8192]{1,0:T(2,128)S(1)}, f32[2,8192]{1,0:T(2,128)S(1)}, u32[]{:S(2)}, u32[]{:S(2)}) collective-permute-start(f32[2,8192]{1,0:T(2,128)S(1)} %pad_maximum_fusion.5), channel_id=1, source_target_pairs={{0,4},{1,5},{2,6},{3,7},{4,0},{5,1},{6,2},{7,3},{8,12},{9,13},{10,... | collective-permute-start | bytes 196616 | tf_op jit(solution)/shard_map/ppermute | solution.py:30
  130.1 4.7 %collective-permute-start.4 = (f32[2,8192]{1,0:T(2,128)S(1)}, f32[2,8192]{1,0:T(2,128)S(1)}, u32[]{:S(2)}, u32[]{:S(2)}) collective-permute-start(f32[2,8192]{1,0:T(2,128)S(1)} %pad_maximum_fusion.6), channel_id=1, source_target_pairs={{0,8},{1,9},{2,10},{3,11},{4,12},{5,13},{6,14},{7,15},{8,0},{9,1},... | collective-permute-start | bytes 196616 | tf_op jit(solution)/shard_map/ppermute | solution.py:30
  135.0 3.2 %collective-permute-start.5 = (f32[2,8192]{1,0:T(2,128)S(1)}, f32[2,8192]{1,0:T(2,128)S(1)}, u32[]{:S(2)}, u32[]{:S(2)}) collective-permute-start(f32[2,8192]{1,0:T(2,128)S(1)} %pad_maximum_fusion.7), channel_id=1, source_target_pairs={{0,16},{1,17},{2,18},{3,19},{4,20},{5,21},{6,22},{7,23},{8,24},{9,... | collective-permute-start | bytes 196616 | tf_op jit(solution)/shard_map/ppermute | solution.py:30
  138.4 4.9 %collective-permute-start.6 = (f32[2,8192]{1,0:T(2,128)S(1)}, f32[2,8192]{1,0:T(2,128)S(1)}, u32[]{:S(2)}, u32[]{:S(2)}) collective-permute-start(f32[2,8192]{1,0:T(2,128)S(1)} %pad_maximum_fusion.8), channel_id=1, source_target_pairs={{0,32},{1,33},{2,34},{3,35},{4,36},{5,37},{6,38},{7,39},{8,40},{9,... | collective-permute-start | bytes 196616 | tf_op jit(solution)/shard_map/ppermute | solution.py:30
  156.1 11.6 %copy-start = (f32[256,768]{1,0:T(8,128)S(1)}, f32[256,768]{1,0:T(8,128)}, u32[]{:S(2)}) copy-start(f32[256,768]{1,0:T(8,128)} %param.3) | copy-start | bytes 2359300
  156.1 11.6 %collective-permute-start.7 = (f32[256,768]{1,0:T(8,128)S(1)}, f32[256,768]{1,0:T(8,128)}, u32[]{:S(2)}, u32[]{:S(2)}) collective-permute-start(f32[256,768]{1,0:T(8,128)S(1)} %slice.93), channel_id=1, source_target_pairs={{0,64},{64,0},{1,65},{65,1},{2,66},{66,2},{3,67},{67,3},{4,68},{68... | collective-permute-start | bytes 2359304 | tf_op jit(solution)/shard_map/ppermute | solution.py:65
  166.4 1.2 collective-permute-start.8
Sparse Core Ops, SparseCore 0:
  10.7 93.9 all-gather.1

commit v6 on v4

--- a/solution.py
+++ b/solution.py
@@ -1,19 +1,91 @@
+import functools
 import math
 
 import jax
 import jax.numpy as jnp
 from jax import lax
+from jax.experimental import pallas as pl
+from jax.experimental.pallas import tpu as pltpu
 from jax.sharding import PartitionSpec as P
 
 HALVES = 2
+TILE = 512
 
 
-def score_block(members, cent_block, score_scale):
-    sq_norm = jnp.sum(jnp.square(cent_block.astype(jnp.float32)), axis=1)
-    products = lax.dot_general(
-        members, cent_block, (((1,), (1,)), ((), ())), preferred_element_type=jnp.float32
+def _stats_kernel(x_ref, c_ref, n_ref, m_ref, l_ref, *, scale):
+    s = lax.dot_general(
+        c_ref[...], x_ref[...], (((1,), (1,)), ((), ())), preferred_element_type=jnp.float32
     )
-    return (2.0 * products - sq_norm[None, :]) * score_scale
+    s = (2.0 * s - n_ref[...]) * scale
+    top = jnp.max(s, axis=0, keepdims=True)
+    m_ref[0] = top
+    l_ref[0] = jnp.sum(jnp.exp(s - top), axis=0, keepdims=True)
+
+
+def point_stats(x, c, norm_col, scale):
+    rows, width = x.shape
+    cents = c.shape[0]
+    steps = rows // TILE
+    out = jax.ShapeDtypeStruct((steps, 1, TILE), jnp.float32)
+    m, l = pl.pallas_call(
+        functools.partial(_stats_kernel, scale=scale),
+        grid=(steps,),
+        in_specs=[
+            pl.BlockSpec((TILE, width), lambda i: (i, 0)),
+            pl.BlockSpec((cents, width), lambda i: (0, 0)),
+            pl.BlockSpec((cents, 1), lambda i: (0, 0)),
+        ],
+        out_specs=[
+            pl.BlockSpec((1, 1, TILE), lambda i: (i, 0, 0)),
+            pl.BlockSpec((1, 1, TILE), lambda i: (i, 0, 0)),
+        ],
+        out_shape=[out, out],
+    )(x, c, norm_col)
+    return m.reshape(rows), l.reshape(rows)
+
+
+def _sums_kernel(x_ref, c_ref, n_ref, t_ref, s_ref, k_ref, *, scale):
+    @pl.when(pl.program_id(0) == 0)
+    def _():
+        s_ref[...] = jnp.zeros_like(s_ref)
+        k_ref[...] = jnp.zeros_like(k_ref)
+
+    x = x_ref[...]
+    s = lax.dot_general(
+        c_ref[...], x, (((1,), (1,)), ((), ())), preferred_element_type=jnp.float32
+    )
+    s = (2.0 * s - n_ref[...]) * scale
+    w = jnp.exp(s - t_ref[0]).astype(jnp.bfloat16)
+    s_ref[...] += lax.dot_general(
+        w, x, (((1,), (0,)), ((), ())), preferred_element_type=jnp.float32
+    )
+    k_ref[...] += jnp.sum(w.astype(jnp.float32), axis=1, keepdims=True)
+
+
+def weighted_sums(x, c, norm_col, log_total, scale):
+    rows, width = x.shape
+    cents = c.shape[0]
+    steps = rows // TILE
+    sums, counts = pl.pallas_call(
+        functools.partial(_sums_kernel, scale=scale),
+        grid=(steps,),
+        in_specs=[
+            pl.BlockSpec((TILE, width), lambda i: (i, 0)),
+            pl.BlockSpec((cents, width), lambda i: (0, 0)),
+            pl.BlockSpec((cents, 1), lambda i: (0, 0)),
+            pl.BlockSpec((1, 1, TILE), lambda i: (i, 0, 0)),
+        ],
+        out_specs=[
+            pl.BlockSpec((cents, width), lambda i: (0, 0)),
+            pl.BlockSpec((cents, 1), lambda i: (0, 0)),
+        ],
+        out_shape=[
+            jax.ShapeDtypeStruct((cents, width), jnp.float32),
+            jax.ShapeDtypeStruct((cents, 1), jnp.float32),
+        ],
+        compiler_params=pltpu.CompilerParams(dimension_semantics=("arbitrary",)),
+    )(x, c, norm_col, log_total.reshape(steps, 1, TILE))
+    return sums, counts.reshape(cents)
 
 
 def merge_stats(first, second):
@@ -42,23 +114,18 @@
     members = lax.all_gather(points, "cent", axis=0, tiled=True)
     other_copies = lax.ppermute(copies, "dp", swap)
     both = jnp.concatenate([other_copies, copies], axis=0)
+    norm_col = jnp.sum(jnp.square(both.astype(jnp.float32)), axis=1, keepdims=True)
     own_rows = copies.shape[0]
     span = members.shape[0] // HALVES
     halves = [members[index_h * span : (index_h + 1) * span] for index_h in range(HALVES)]
-    scores = [score_block(half, both, score_scale) for half in halves]
     totals = []
-    for part in scores:
-        local_max = jnp.max(part, axis=1)
-        local_sum = jnp.sum(jnp.exp(part - local_max[:, None]), axis=1)
+    for half in halves:
+        local_max, local_sum = point_stats(half, both, norm_col, score_scale)
         totals.append(group_log_total(local_max, local_sum))
     sums = None
     counts = None
-    for part, total, half in zip(scores, totals, halves):
-        weights = jnp.exp(part - total[:, None]).astype(jnp.bfloat16)
-        part_sums = lax.dot_general(
-            weights, half, (((0,), (0,)), ((), ())), preferred_element_type=jnp.float32
-        )
-        part_counts = jnp.sum(weights, axis=0, dtype=jnp.float32)
+    for total, half in zip(totals, halves):
+        part_sums, part_counts = weighted_sums(half, both, norm_col, total, score_scale)
         sums = part_sums if sums is None else sums + part_sums
         counts = part_counts if counts is None else counts + part_counts
     sent_sums = lax.ppermute(sums[:own_rows], "dp", swap)

time: 174 us -> 205 us (1.18)
  Pallas kernels: 0 us -> 44.3 us
  matrix products: 23.8 us -> 0 us
  local copies, waits for them, and re-layouts: 0.12 us -> 11.5 us
  waiting for transfers between devices: 100 us -> 97.2 us
    pallas_call x0 -> x4, Pallas kernels: none -> 44.3 us  [the longest x2 24.6 us: weighted_sums(): pl.pallas_call(functools.partial(_sums_kernel, scale=scale), grid=(steps,...]
    dot_general x4 -> x0, matrix products: 23.8 us -> none  [the longest x2 12.5 us: on_device(): lax.dot_general(weights, half, (((0,), (0,)), ((), ())), preferred_elemen...]
    slice x0 -> x1, local copies, waits for them, and re-layouts: none -> 10.3 us  [on_device(): members[index_h * span:(index_h + 1) * span]]
    reduce_sum x5 -> x1, other arithmetic: 5.11 us -> 0.23 us  [on_device(): jnp.sum(jnp.square(both.astype(jnp.float32)), axis=1, keepdims=True)]
  transfers between devices with their start and end apart: 16 -> 16, of which waited for: 8 -> 9; matrix products, arithmetic and copies ran while one was open for 7% -> 4% of each run, Pallas kernels for 0% -> 11%
where the time goes in v6:
time: 205 us; the launch traced here: 204 us
  waiting for transfers between devices  97.2 us (47%)
  Pallas kernels  44.3 us (22%)
  starting transfers between devices  26.4 us (13%)
  between operations  14.2 us (7%)
  local copies, waits for them, and re-layouts  11.5 us (6%)
  other arithmetic  10.3 us (5%)
    all_gather x1, waiting for transfers between devices, on_device(): members = lax.all_gather(points, 'cent', axis=0, tiled=True)  90.8 us
    pallas_call x2, Pallas kernels, weighted_sums(): pl.pallas_call(functools.partial(_sums_kernel, scale=scale), grid=(steps,...  24.6 us
    pallas_call x2, Pallas kernels, point_stats(): pl.pallas_call(functools.partial(_stats_kernel, scale=scale), grid=(steps...  19.7 us
    ppermute x12, starting transfers between devices, group_log_total(): lax.ppermute(stats, 'cent', [(i, i ^ bit) for i in range(cent_count)])  17.4 us
    slice x1, local copies, waits for them, and re-layouts, on_device(): members[index_h * span:(index_h + 1) * span]  10.3 us
    ppermute x1, starting transfers between devices, on_device(): sent_sums = lax.ppermute(sums[:own_rows], 'dp', swap)  6.59 us
    ppermute x12, waiting for transfers between devices, group_log_total(): lax.ppermute(stats, 'cent', [(i, i ^ bit) for i in range(cent_count)])  4.25 us
  transfers between devices with their start and end apart: 16, of which 9 were waited for; matrix products, arithmetic and copies ran while one was open for 4% of the time, Pallas kernels for 11%

profile of v6, /device:TPU:1, one launch (start us, length us, event | category | flops | bytes accessed | tf_op | source)
XLA Modules:
  0.0 203.9 jit_solution(6481838127337389734)
XLA Ops:
  7.2 0.7 all-gather.2.cloned.1.call-update
  7.9 1.2 convert_element_type.6
  9.1 1.5 collective-permute-start
  10.5 1.3 collective-permute-done
  11.9 0.2 multiply_reduce_fusion
  12.1 0.9 copy.9.n_ref
  13.0 0.9 pad_maximum_fusion.c_ref
  13.9 90.8 %all-gather.2.cloned.1.call-done = bf16[8192,768]{1,0:T(8,128)(2,1)} async-done(((bf16[128,768]{1,0:T(8,128)(2,1)}), bf16[8192,768]{1,0:T(8,128)(2,1)}) %all-gather.2.cloned.1.call-update) | async-done | bytes 12582928 | tf_op jit(solution)/shard_map/all_gather | solution.py:114
  104.7 10.3 %fusion.51 = (bf16[4096,768]{1,0:T(8,128)(2,1)}, bf16[4096,768]{1,0:T(8,128)(2,1)}) fusion(bf16[8192,768]{1,0:T(8,128)(2,1)} %all-gather.2.cloned.1.call-done), kind=kLoop, calls=%fused_computation.119 | loop fusion | bytes 25165824 | tf_op jit(solution)/shard_map/slice | solution.py:120
  115.0 9.9 %shard_map.41 = (f32[8,1,512]{2,1,0:T(1,128)}, f32[8,1,512]{2,1,0:T(1,128)}) custom-call(bf16[4096,768]{1,0:T(8,128)(2,1)} %get-tuple-element.37.x_ref, bf16[512,768]{1,0:T(8,128)(2,1)} %pad_maximum_fusion.c_ref, f32[512,1]{1,0:T(8,128)} %copy.9.n_ref), custom_call_target="tpu_custom_call" | custom-call | tf_op jit(solution)/shard_map/pallas_call | solution.py:30
  124.9 0.8 pad_maximum_fusion.1
  125.7 1.3 collective-permute-start.1
  127.0 9.9 %shard_map.43 = (f32[8,1,512]{2,1,0:T(1,128)}, f32[8,1,512]{2,1,0:T(1,128)}) custom-call(bf16[4096,768]{1,0:T(8,128)(2,1)} %get-tuple-element.36.x_ref, bf16[512,768]{1,0:T(8,128)(2,1)} %pad_maximum_fusion.c_ref, f32[512,1]{1,0:T(8,128)} %copy.9.n_ref), custom_call_target="tpu_custom_call" | custom-call | tf_op jit(solution)/shard_map/pallas_call | solution.py:30
  136.8 0.8 pad_maximum_fusion.7
  137.6 0.4 collective-permute-start.7
  138.0 0.1 multiply_add_fusion.9
  138.1 2.8 %collective-permute-start.2 = (f32[2,4096]{1,0:T(2,128)S(1)}, f32[2,4096]{1,0:T(2,128)S(1)}, u32[]{:S(2)}, u32[]{:S(2)}) collective-permute-start(f32[2,4096]{1,0:T(2,128)S(1)} %pad_maximum_fusion.2), channel_id=1, source_target_pairs={{0,2},{1,3},{2,0},{3,1},{4,6},{5,7},{6,4},{7,5},{8,10},{9,11},{10,... | collective-permute-start | bytes 98312 | tf_op jit(solution)/shard_map/ppermute | solution.py:102
  140.9 0.8 multiply_add_fusion.4
  141.7 2.1 %collective-permute-start.8 = (f32[2,4096]{1,0:T(2,128)S(1)}, f32[2,4096]{1,0:T(2,128)S(1)}, u32[]{:S(2)}, u32[]{:S(2)}) collective-permute-start(f32[2,4096]{1,0:T(2,128)S(1)} %pad_maximum_fusion.8), channel_id=1, source_target_pairs={{0,2},{1,3},{2,0},{3,1},{4,6},{5,7},{6,4},{7,5},{8,10},{9,11},{10,... | collective-permute-start | bytes 98312 | tf_op jit(solution)/shard_map/ppermute | solution.py:102
  143.8 0.1 multiply_add_fusion.8
  143.9 1.3 collective-permute-start.3
  145.2 0.9 collective-permute-done.8
  146.1 0.1 multiply_add_fusion.3
  146.2 1.3 collective-permute-start.9
  147.5 0.1 multiply_add_fusion.7
  147.6 2.5 %collective-permute-start.4 = (f32[2,4096]{1,0:T(2,128)S(1)}, f32[2,4096]{1,0:T(2,128)S(1)}, u32[]{:S(2)}, u32[]{:S(2)}) collective-permute-start(f32[2,4096]{1,0:T(2,128)S(1)} %pad_maximum_fusion.4), channel_id=1, source_target_pairs={{0,8},{1,9},{2,10},{3,11},{4,12},{5,13},{6,14},{7,15},{8,0},{9,1},... | collective-permute-start | bytes 98312 | tf_op jit(solution)/shard_map/ppermute | solution.py:102
  150.2 1.7 collective-permute-start.10
  151.9 0.2 collective-permute-done.4
  152.1 0.1 multiply_add_fusion.6
  152.2 0.2 collective-permute-start.5
  152.5 2.3 %collective-permute-done.10 = f32[2,4096]{1,0:T(2,128)S(1)} collective-permute-done((f32[2,4096]{1,0:T(2,128)S(1)}, f32[2,4096]{1,0:T(2,128)S(1)}, u32[]{:S(2)}, u32[]{:S(2)}) %collective-permute-start.10) | collective-permute-done | bytes 32800 | tf_op jit(solution)/shard_map/ppermute | solution.py:102
  154.9 0.1 collective-permute-start.11
  155.1 0.3 collective-permute-done.5
  155.5 2.3 %collective-permute-start.6 = (f32[2,4096]{1,0:T(2,128)S(1)}, f32[2,4096]{1,0:T(2,128)S(1)}, u32[]{:S(2)}, u32[]{:S(2)}) collective-permute-start(f32[2,4096]{1,0:T(2,128)S(1)} %pad_maximum_fusion.6), channel_id=1, source_target_pairs={{0,32},{1,33},{2,34},{3,35},{4,36},{5,37},{6,38},{7,39},{8,40},{9,... | collective-permute-start | bytes 98312 | tf_op jit(solution)/shard_map/ppermute | solution.py:102
  157.8 0.3 collective-permute-done.11
  158.2 1.4 collective-permute-start.12
  159.6 0.2 collective-permute-done.6
  159.9 0.7 log_add_fusion.3
  160.5 12.3 %shard_map.42 = (f32[512,768]{1,0:T(8,128)}, f32[512,1]{1,0:T(8,128)}) custom-call(bf16[4096,768]{1,0:T(8,128)(2,1)} %get-tuple-element.37.x_ref, bf16[512,768]{1,0:T(8,128)(2,1)} %pad_maximum_fusion.c_ref, f32[512,1]{1,0:T(8,128)} %copy.9.n_ref, f32[8,1,512]{2,1,0:T(1,128)} %bitcast.152), custom_call_target="tpu_custom_call" | custom-call | tf_op jit(solution)/shard_map/pallas_call | solution.py:69
  172.8 0.7 log_add_fusion.2
  173.5 12.3 %shard_map.44 = (f32[512,768]{1,0:T(8,128)}, f32[512,1]{1,0:T(8,128)}) custom-call(bf16[4096,768]{1,0:T(8,128)(2,1)} %get-tuple-element.36.x_ref, bf16[512,768]{1,0:T(8,128)(2,1)} %pad_maximum_fusion.c_ref, f32[512,1]{1,0:T(8,128)} %copy.9.n_ref, f32[8,1,512]{2,1,0:T(1,128)} %bitcast.151), custom_call_target="tpu_custom_call" | custom-call | tf_op jit(solution)/shard_map/pallas_call | solution.py:69
  185.8 1.6 add.184
  187.5 6.6 %collective-permute-start.13 = (f32[256,768]{1,0:T(8,128)S(1)}, f32[256,768]{1,0:T(8,128)S(1)}, u32[]{:S(2)}, u32[]{:S(2)}) collective-permute-start(f32[256,768]{1,0:T(8,128)S(1)} %slice.167), channel_id=1, source_target_pairs={{0,64},{64,0},{1,65},{65,1},{2,66},{66,2},{3,67},{67,3},{4,68},{68... | collective-permute-start | bytes 2359304 | tf_op jit(solution)/shard_map/ppermute | solution.py:131
  194.2 0.1 slice_reduce_fusion
  194.3 0.9 collective-permute-start.14
  195.3 0.6 fusion.50
  195.9 0.1 collective-permute-done.14
  196.1 1.0 fusion.1
  (45 shorter events, 0.9 us)
Async XLA Ops:
  7.2 97.5 %all-gather.2.cloned.1.call-start = ((), (), s32[]{:S(2)}) async-start(), calls=%async_computation | async-start | bytes 12779520 | tf_op jit(solution)/shard_map/all_gather | solution.py:114
  9.1 2.8 %collective-permute-start = (bf16[256,768]{1,0:T(8,128)(2,1)S(1)}, bf16[256,768]{1,0:T(8,128)(2,1)S(1)}, u32[]{:S(2)}, u32[]{:S(2)}) collective-permute-start(bf16[256,768]{1,0:T(8,128)(2,1)S(1)} %convert_element_type.6), channel_id=1, source_target_pairs={{0,64},{64,0},{1,65},{65,1},{2,66},{66,2},{3,67},{67,3},{4,68},{68... | collective-permute-start | bytes 1179656 | tf_op jit(solution)/shard_map/ppermute | solution.py:115
  125.7 12.3 %collective-permute-start.1 = (f32[2,4096]{1,0:T(2,128)S(1)}, f32[2,4096]{1,0:T(2,128)S(1)}, u32[]{:S(2)}, u32[]{:S(2)}) collective-permute-start(f32[2,4096]{1,0:T(2,128)S(1)} %pad_maximum_fusion.1), channel_id=1, source_target_pairs={{0,1},{1,0},{2,3},{3,2},{4,5},{5,4},{6,7},{7,6},{8,9},{9,8},{10,11... | collective-permute-start | bytes 98312 | tf_op jit(solution)/shard_map/ppermute | solution.py:102
  127.0 11.0 %copy-start.6 = (f32[8,1,512]{2,1,0:T(1,128)S(1)}, f32[8,1,512]{2,1,0:T(1,128)}, u32[]{:S(2)}) copy-start(f32[8,1,512]{2,1,0:T(1,128)} %get-tuple-element.10) | copy-start | bytes 49156
  127.0 11.0 %copy-start.7 = (f32[8,1,512]{2,1,0:T(1,128)S(1)}, f32[8,1,512]{2,1,0:T(1,128)}, u32[]{:S(2)}) copy-start(f32[8,1,512]{2,1,0:T(1,128)} %get-tuple-element.11) | copy-start | bytes 49156
  137.6 3.3 %collective-permute-start.7 = (f32[2,4096]{1,0:T(2,128)S(1)}, f32[2,4096]{1,0:T(2,128)S(1)}, u32[]{:S(2)}, u32[]{:S(2)}) collective-permute-start(f32[2,4096]{1,0:T(2,128)S(1)} %pad_maximum_fusion.7), channel_id=1, source_target_pairs={{0,1},{1,0},{2,3},{3,2},{4,5},{5,4},{6,7},{7,6},{8,9},{9,8},{10,11... | collective-permute-start | bytes 98312 | tf_op jit(solution)/shard_map/ppermute | solution.py:102
  138.1 5.7 %collective-permute-start.2 = (f32[2,4096]{1,0:T(2,128)S(1)}, f32[2,4096]{1,0:T(2,128)S(1)}, u32[]{:S(2)}, u32[]{:S(2)}) collective-permute-start(f32[2,4096]{1,0:T(2,128)S(1)} %pad_maximum_fusion.2), channel_id=1, source_target_pairs={{0,2},{1,3},{2,0},{3,1},{4,6},{5,7},{6,4},{7,5},{8,10},{9,11},{10,... | collective-permute-start | bytes 98312 | tf_op jit(solution)/shard_map/ppermute | solution.py:102
  141.7 4.3 %collective-permute-start.8 = (f32[2,4096]{1,0:T(2,128)S(1)}, f32[2,4096]{1,0:T(2,128)S(1)}, u32[]{:S(2)}, u32[]{:S(2)}) collective-permute-start(f32[2,4096]{1,0:T(2,128)S(1)} %pad_maximum_fusion.8), channel_id=1, source_target_pairs={{0,2},{1,3},{2,0},{3,1},{4,6},{5,7},{6,4},{7,5},{8,10},{9,11},{10,... | collective-permute-start | bytes 98312 | tf_op jit(solution)/shard_map/ppermute | solution.py:102
  143.9 3.6 %collective-permute-start.3 = (f32[2,4096]{1,0:T(2,128)S(1)}, f32[2,4096]{1,0:T(2,128)S(1)}, u32[]{:S(2)}, u32[]{:S(2)}) collective-permute-start(f32[2,4096]{1,0:T(2,128)S(1)} %pad_maximum_fusion.3), channel_id=1, source_target_pairs={{0,4},{1,5},{2,6},{3,7},{4,0},{5,1},{6,2},{7,3},{8,12},{9,13},{10,... | collective-permute-start | bytes 98312 | tf_op jit(solution)/shard_map/ppermute | solution.py:102
  146.2 3.9 %collective-permute-start.9 = (f32[2,4096]{1,0:T(2,128)S(1)}, f32[2,4096]{1,0:T(2,128)S(1)}, u32[]{:S(2)}, u32[]{:S(2)}) collective-permute-start(f32[2,4096]{1,0:T(2,128)S(1)} %pad_maximum_fusion.9), channel_id=1, source_target_pairs={{0,4},{1,5},{2,6},{3,7},{4,0},{5,1},{6,2},{7,3},{8,12},{9,13},{10,... | collective-permute-start | bytes 98312 | tf_op jit(solution)/shard_map/ppermute | solution.py:102
  147.6 4.5 %collective-permute-start.4 = (f32[2,4096]{1,0:T(2,128)S(1)}, f32[2,4096]{1,0:T(2,128)S(1)}, u32[]{:S(2)}, u32[]{:S(2)}) collective-permute-start(f32[2,4096]{1,0:T(2,128)S(1)} %pad_maximum_fusion.4), channel_id=1, source_target_pairs={{0,8},{1,9},{2,10},{3,11},{4,12},{5,13},{6,14},{7,15},{8,0},{9,1},... | collective-permute-start | bytes 98312 | tf_op jit(solution)/shard_map/ppermute | solution.py:102
  150.2 4.6 %collective-permute-start.10 = (f32[2,4096]{1,0:T(2,128)S(1)}, f32[2,4096]{1,0:T(2,128)S(1)}, u32[]{:S(2)}, u32[]{:S(2)}) collective-permute-start(f32[2,4096]{1,0:T(2,128)S(1)} %pad_maximum_fusion.10), channel_id=1, source_target_pairs={{0,8},{1,9},{2,10},{3,11},{4,12},{5,13},{6,14},{7,15},{8,0},{9,1},... | collective-permute-start | bytes 98312 | tf_op jit(solution)/shard_map/ppermute | solution.py:102
  152.2 3.1 %collective-permute-start.5 = (f32[2,4096]{1,0:T(2,128)S(1)}, f32[2,4096]{1,0:T(2,128)S(1)}, u32[]{:S(2)}, u32[]{:S(2)}) collective-permute-start(f32[2,4096]{1,0:T(2,128)S(1)} %pad_maximum_fusion.5), channel_id=1, source_target_pairs={{0,16},{1,17},{2,18},{3,19},{4,20},{5,21},{6,22},{7,23},{8,24},{9,... | collective-permute-start | bytes 98312 | tf_op jit(solution)/shard_map/ppermute | solution.py:102
  154.9 3.1 %collective-permute-start.11 = (f32[2,4096]{1,0:T(2,128)S(1)}, f32[2,4096]{1,0:T(2,128)S(1)}, u32[]{:S(2)}, u32[]{:S(2)}) collective-permute-start(f32[2,4096]{1,0:T(2,128)S(1)} %pad_maximum_fusion.11), channel_id=1, source_target_pairs={{0,16},{1,17},{2,18},{3,19},{4,20},{5,21},{6,22},{7,23},{8,24},{9,... | collective-permute-start | bytes 98312 | tf_op jit(solution)/shard_map/ppermute | solution.py:102
  155.5 4.3 %collective-permute-start.6 = (f32[2,4096]{1,0:T(2,128)S(1)}, f32[2,4096]{1,0:T(2,128)S(1)}, u32[]{:S(2)}, u32[]{:S(2)}) collective-permute-start(f32[2,4096]{1,0:T(2,128)S(1)} %pad_maximum_fusion.6), channel_id=1, source_target_pairs={{0,32},{1,33},{2,34},{3,35},{4,36},{5,37},{6,38},{7,39},{8,40},{9,... | collective-permute-start | bytes 98312 | tf_op jit(solution)/shard_map/ppermute | solution.py:102
  158.2 14.6 %collective-permute-start.12 = (f32[2,4096]{1,0:T(2,128)S(1)}, f32[2,4096]{1,0:T(2,128)S(1)}, u32[]{:S(2)}, u32[]{:S(2)}) collective-permute-start(f32[2,4096]{1,0:T(2,128)S(1)} %pad_maximum_fusion.12), channel_id=1, source_target_pairs={{0,32},{1,33},{2,34},{3,35},{4,36},{5,37},{6,38},{7,39},{8,40},{9,... | collective-permute-start | bytes 98312 | tf_op jit(solution)/shard_map/ppermute | solution.py:102
  160.5 12.3 %copy-start.4 = (f32[8,1,512]{2,1,0:T(1,128)S(1)}, f32[8,1,512]{2,1,0:T(1,128)}, u32[]{:S(2)}) copy-start(f32[8,1,512]{2,1,0:T(1,128)} %get-tuple-element.13) | copy-start | bytes 49156
  160.5 12.3 %copy-start.5 = (f32[8,1,512]{2,1,0:T(1,128)S(1)}, f32[8,1,512]{2,1,0:T(1,128)}, u32[]{:S(2)}) copy-start(f32[8,1,512]{2,1,0:T(1,128)} %get-tuple-element.14) | copy-start | bytes 49156
  173.5 12.3 %copy-start.1 = (f32[512,768]{1,0:T(8,128)S(1)}, f32[512,768]{1,0:T(8,128)}, u32[]{:S(2)}) copy-start(f32[512,768]{1,0:T(8,128)} %get-tuple-element.12) | copy-start | bytes 4718596
  187.4 6.7 %copy-start.2 = (f32[512,1]{1,0:T(8,128)S(1)}, f32[512,1]{1,0:T(8,128)}, u32[]{:S(2)}) copy-start(f32[512,1]{1,0:T(8,128)} %get-tuple-element.16) | copy-start | bytes 6148
  187.4 6.7 %copy-start.3 = (f32[512,1]{1,0:T(8,128)S(1)}, f32[512,1]{1,0:T(8,128)}, u32[]{:S(2)}) copy-start(f32[512,1]{1,0:T(8,128)} %get-tuple-element.17) | copy-start | bytes 6148
  187.5 8.6 %copy-start = (f32[256,768]{1,0:T(8,128)S(1)}, f32[256,768]{1,0:T(8,128)}, u32[]{:S(2)}) copy-start(f32[256,768]{1,0:T(8,128)} %param.3) | copy-start | bytes 2359300
  187.5 8.5 %collective-permute-start.13 = (f32[256,768]{1,0:T(8,128)S(1)}, f32[256,768]{1,0:T(8,128)S(1)}, u32[]{:S(2)}, u32[]{:S(2)}) collective-permute-start(f32[256,768]{1,0:T(8,128)S(1)} %slice.167), channel_id=1, source_target_pairs={{0,64},{64,0},{1,65},{65,1},{2,66},{66,2},{3,67},{67,3},{4,68},{68... | collective-permute-start | bytes 2359304 | tf_op jit(solution)/shard_map/ppermute | solution.py:131
  194.3 1.8 collective-permute-start.14
Sparse Core Ops, SparseCore 0:
  10.7 93.9 all-gather.1

commit v7 on v4

--- a/solution.py
+++ b/solution.py
@@ -5,7 +5,7 @@
 from jax import lax
 from jax.sharding import PartitionSpec as P
 
-HALVES = 2
+LEAD_PARTS = 4
 
 
 def score_block(members, cent_block, score_scale):
@@ -43,8 +43,8 @@
     other_copies = lax.ppermute(copies, "dp", swap)
     both = jnp.concatenate([other_copies, copies], axis=0)
     own_rows = copies.shape[0]
-    span = members.shape[0] // HALVES
-    halves = [members[index_h * span : (index_h + 1) * span] for index_h in range(HALVES)]
+    lead = members.shape[0] // LEAD_PARTS
+    halves = [members[:lead], members[lead:]]
     scores = [score_block(half, both, score_scale) for half in halves]
     totals = []
     for part in scores:

time: 174 us -> 187 us (1.075)
  waiting for transfers between devices: 100 us -> 105 us
  matrix products: 23.8 us -> 27.2 us
  starting transfers between devices: 26.6 us -> 30 us
    ppermute x12, waiting for transfers between devices: 5.14 us -> 9.34 us  [group_log_total(): lax.ppermute(stats, 'cent', [(i, i ^ bit) for i in range(cent_count)])]
    dot_general x2, matrix products: 12.5 us -> 15.7 us  [on_device(): lax.dot_general(weights, half, (((0,), (0,)), ((), ())), preferred_elemen...]
    ppermute x1, starting transfers between devices: 6.88 us -> 9.72 us  [on_device(): sent_sums = lax.ppermute(sums[:own_rows], 'dp', swap)]
  transfers between devices with their start and end apart: 16 -> 16, of which waited for: 8 -> 9; matrix products, arithmetic and copies ran while one was open for 7% -> 11% of each run, Pallas kernels for 0% -> 0%
where the time goes in v7:
time: 187 us
  waiting for transfers between devices  105 us (56%)
  starting transfers between devices  30 us (16%)
  matrix products  27.2 us (15%)
  between operations  14.3 us (8%)
  other arithmetic  9.23 us (5%)
    all_gather x1, waiting for transfers between devices, on_device(): members = lax.all_gather(points, 'cent', axis=0, tiled=True)  92.6 us
    ppermute x12, starting transfers between devices, group_log_total(): lax.ppermute(stats, 'cent', [(i, i ^ bit) for i in range(cent_count)])  18.6 us
    dot_general x2, matrix products, on_device(): lax.dot_general(weights, half, (((0,), (0,)), ((), ())), preferred_elemen...  15.7 us
    dot_general x2, matrix products, score_block(): lax.dot_general(members, cent_block, (((1,), (1,)), ((), ())), preferred_...  11.5 us
    ppermute x1, starting transfers between devices, on_device(): sent_sums = lax.ppermute(sums[:own_rows], 'dp', swap)  9.72 us
    ppermute x12, waiting for transfers between devices, group_log_total(): lax.ppermute(stats, 'cent', [(i, i ^ bit) for i in range(cent_count)])  9.34 us
  transfers between devices with their start and end apart: 16, of which 9 were waited for; matrix products, arithmetic and copies ran while one was open for 11% of the time, Pallas kernels for 0%

profile of v7, /device:TPU:1, one launch (start us, length us, event | category | flops | bytes accessed | tf_op | source)
XLA Modules:
  0.0 186.6 jit_solution(15214502458371588496)
XLA Ops:
  7.2 0.0 all-gather.2.cloned.1.call-start
  7.2 0.7 all-gather.2.cloned.1.call-update
  7.9 1.2 convert_element_type.19
  9.1 1.5 collective-permute-start
  10.5 1.3 collective-permute-done
  11.9 0.2 multiply_reduce_fusion
  12.1 92.6 %all-gather.2.cloned.1.call-done = bf16[8192,768]{1,0:T(8,128)(2,1)} async-done(((bf16[128,768]{1,0:T(8,128)(2,1)}), bf16[8192,768]{1,0:T(8,128)(2,1)}) %all-gather.2.cloned.1.call-update) | async-done | bytes 12582928 | tf_op jit(solution)/shard_map/all_gather | solution.py:42
  104.7 3.7 %fusion.40 = (f32[2048]{0:T(1024)S(1)}, f32[512,2048]{1,0:T(8,128)S(1)}) fusion(f32[512]{0:T(512)S(1)} %multiply_reduce_fusion, bf16[8192,768]{1,0:T(8,128)(2,1)} %all-gather.2.cloned.1.call-done, bf16[256,768]{1,0:T(8,128)(2,1)S(1)} %convert_element_type.19, bf16[256,768]{1,0:T(8,128)(2,1)S(1)} %collective-permute-done), kind=kOutput, calls=%fused_computation.98 | convolution fusion | flops 1616377856 | bytes 8136704 | tf_op jit(solution)/shard_map/dot_general | solution.py:13
  108.5 0.6 exponential_reduce_fusion.1
  109.1 1.3 copy-done
  110.4 1.2 collective-permute-start.1
  111.6 7.7 %fusion.41 = (f32[6144]{0:T(1024)S(1)}, f32[512,6144]{1,0:T(8,128)S(1)}) fusion(f32[512]{0:T(512)S(1)} %multiply_reduce_fusion, bf16[8192,768]{1,0:T(8,128)(2,1)} %all-gather.2.cloned.1.call-done, bf16[256,768]{1,0:T(8,128)(2,1)S(1)} %convert_element_type.19, bf16[256,768]{1,0:T(8,128)(2,1)S(1)} %collective-permute-done), kind=kOutput, calls=%fused_computation.99 | convolution fusion | flops 4845987840 | bytes 22833152 | tf_op jit(solution)/shard_map/dot_general | solution.py:13
  119.3 0.0 collective-permute-done.1
  119.4 2.5 %collective-permute-start.2 = (f32[2,2048]{1,0:T(2,128)S(1)}, f32[2,2048]{1,0:T(2,128)S(1)}, u32[]{:S(2)}, u32[]{:S(2)}) collective-permute-start(f32[2,2048]{1,0:T(2,128)S(1)} %pad_maximum_fusion.10), channel_id=1, source_target_pairs={{0,2},{1,3},{2,0},{3,1},{4,6},{5,7},{6,4},{7,5},{8,10},{9,11},{10,... | collective-permute-start | bytes 49160 | tf_op jit(solution)/shard_map/ppermute | solution.py:30
  121.9 2.0 %exponential_reduce_fusion = f32[6144]{0:T(1024)S(1)} fusion(f32[512,6144]{1,0:T(8,128)S(1)} %get-tuple-element.49, f32[6144]{0:T(1024)S(1)} %get-tuple-element.48), kind=kLoop, calls=%fused_computation.2 | loop fusion | flops 6285312 | bytes 12632064 | tf_op jit(solution)/shard_map/reduce_sum | solution.py:52
  123.9 1.3 collective-permute-start.3
  125.3 0.1 collective-permute-start.7
  125.4 1.2 collective-permute-done.3
  126.7 2.8 %collective-permute-start.4 = (f32[2,2048]{1,0:T(2,128)S(1)}, f32[2,2048]{1,0:T(2,128)S(1)}, u32[]{:S(2)}, u32[]{:S(2)}) collective-permute-start(f32[2,2048]{1,0:T(2,128)S(1)} %pad_maximum_fusion.12), channel_id=1, source_target_pairs={{0,8},{1,9},{2,10},{3,11},{4,12},{5,13},{6,14},{7,15},{8,0},{9,1},... | collective-permute-start | bytes 49160 | tf_op jit(solution)/shard_map/ppermute | solution.py:30
  129.5 0.1 multiply_add_fusion.4
  129.6 1.3 collective-permute-done.4
  130.9 1.1 collective-permute-start.5
  132.1 2.2 %collective-permute-start.8 = (f32[2,6144]{1,0:T(2,128)S(1)}, f32[2,6144]{1,0:T(2,128)S(1)}, u32[]{:S(2)}, u32[]{:S(2)}) collective-permute-start(f32[2,6144]{1,0:T(2,128)S(1)} %pad_maximum_fusion.4), channel_id=1, source_target_pairs={{0,2},{1,3},{2,0},{3,1},{4,6},{5,7},{6,4},{7,5},{8,10},{9,11},{10,... | collective-permute-start | bytes 147464 | tf_op jit(solution)/shard_map/ppermute | solution.py:30
  134.3 2.7 %collective-permute-start.6 = (f32[2,2048]{1,0:T(2,128)S(1)}, f32[2,2048]{1,0:T(2,128)S(1)}, u32[]{:S(2)}, u32[]{:S(2)}) collective-permute-start(f32[2,2048]{1,0:T(2,128)S(1)} %pad_maximum_fusion.14), channel_id=1, source_target_pairs={{0,32},{1,33},{2,34},{3,35},{4,36},{5,37},{6,38},{7,39},{8,40},{9,... | collective-permute-start | bytes 49160 | tf_op jit(solution)/shard_map/ppermute | solution.py:30
  137.0 0.1 multiply_add_fusion.3
  137.2 0.1 collective-permute-start.9
  137.3 1.3 collective-permute-done.6
  138.5 1.6 collective-permute-done.9
  140.2 0.1 multiply_add_fusion.2
  140.3 1.4 collective-permute-start.10
  141.8 3.1 %collective-permute-done.10 = f32[2,6144]{1,0:T(2,128)S(1)} collective-permute-done((f32[2,6144]{1,0:T(2,128)S(1)}, f32[2,6144]{1,0:T(2,128)S(1)}, u32[]{:S(2)}, u32[]{:S(2)}) %collective-permute-start.10) | collective-permute-done | bytes 49184 | tf_op jit(solution)/shard_map/ppermute | solution.py:30
  144.9 0.1 multiply_add_fusion.1
  145.0 0.3 collective-permute-start.11
  145.3 6.3 %fusion.3 = f32[512,768]{1,0:T(8,128)} fusion(bf16[8192,768]{1,0:T(8,128)(2,1)} %all-gather.2.cloned.1.call-done, f32[512,2048]{1,0:T(8,128)} %copy-done, f32[2048]{0:T(1024)S(1)} %log_add_fusion.1), kind=kOutput, calls=%fused_computation.11 | convolution fusion | flops 1612709888 | bytes 8921088 | tf_op jit(solution)/shard_map/dot_general | solution.py:58
  151.7 0.1 slice_maximum_fusion.5
  151.8 3.0 %collective-permute-start.12 = (f32[2,6144]{1,0:T(2,128)S(1)}, f32[2,6144]{1,0:T(2,128)S(1)}, u32[]{:S(2)}, u32[]{:S(2)}) collective-permute-start(f32[2,6144]{1,0:T(2,128)S(1)} %pad_maximum_fusion.8), channel_id=1, source_target_pairs={{0,32},{1,33},{2,34},{3,35},{4,36},{5,37},{6,38},{7,39},{8,40},{9,... | collective-permute-start | bytes 147464 | tf_op jit(solution)/shard_map/ppermute | solution.py:30
  154.9 0.6 convert_reduce_fusion.1
  155.5 0.8 collective-permute-done.12
  156.4 0.1 log_add_fusion
  156.5 9.4 %fusion.6 = f32[512,768]{1,0:T(8,128)S(1)} fusion(f32[512,768]{1,0:T(8,128)} %fusion.3, bf16[8192,768]{1,0:T(8,128)(2,1)} %all-gather.2.cloned.1.call-done, f32[512,6144]{1,0:T(8,128)S(1)} %get-tuple-element.49, f32[6144]{0:T(1024)S(1)} %log_add_fusion), kind=kOutput, calls=%fused_computation.15 | convolution fusion | flops 4838522880 | bytes 25190400 | tf_op jit(solution)/shard_map/dot_general | solution.py:58
  165.9 0.1 slice.159
  165.9 0.0 copy-start.2
  165.9 9.7 %collective-permute-start.13 = (f32[256,768]{1,0:T(8,128)S(1)}, f32[256,768]{1,0:T(8,128)S(1)}, u32[]{:S(2)}, u32[]{:S(2)}) collective-permute-start(f32[256,768]{1,0:T(8,128)S(1)} %slice.159), channel_id=1, source_target_pairs={{0,64},{64,0},{1,65},{65,1},{2,66},{66,2},{3,67},{67,3},{4,68},{68... | collective-permute-start | bytes 2359304 | tf_op jit(solution)/shard_map/ppermute | solution.py:64
  175.7 1.7 convert_reduce_fusion
  177.4 0.1 collective-permute-start.14
  177.5 0.6 fusion.35
  178.1 0.6 collective-permute-done.14
  178.7 1.0 fusion.10
  (33 shorter events, 0.7 us)
Async XLA Ops:
  7.2 97.5 %all-gather.2.cloned.1.call-start = ((), (), s32[]{:S(2)}) async-start(), calls=%async_computation | async-start | bytes 12779520 | tf_op jit(solution)/shard_map/all_gather | solution.py:42
  9.1 2.8 %collective-permute-start = (bf16[256,768]{1,0:T(8,128)(2,1)S(1)}, bf16[256,768]{1,0:T(8,128)(2,1)S(1)}, u32[]{:S(2)}, u32[]{:S(2)}) collective-permute-start(bf16[256,768]{1,0:T(8,128)(2,1)S(1)} %convert_element_type.19), channel_id=1, source_target_pairs={{0,64},{64,0},{1,65},{65,1},{2,66},{66,2},{3,67},{67,3},{4,68},{68... | collective-permute-start | bytes 1179656 | tf_op jit(solution)/shard_map/ppermute | solution.py:43
  108.5 1.9 %copy-start = (f32[512,2048]{1,0:T(8,128)}, f32[512,2048]{1,0:T(8,128)S(1)}, u32[]{:S(2)}) copy-start(f32[512,2048]{1,0:T(8,128)S(1)} %get-tuple-element.47) | copy-start | bytes 12582916
  110.4 8.9 %collective-permute-start.1 = (f32[2,2048]{1,0:T(2,128)S(1)}, f32[2,2048]{1,0:T(2,128)S(1)}, u32[]{:S(2)}, u32[]{:S(2)}) collective-permute-start(f32[2,2048]{1,0:T(2,128)S(1)} %pad_maximum_fusion.9), channel_id=1, source_target_pairs={{0,1},{1,0},{2,3},{3,2},{4,5},{5,4},{6,7},{7,6},{8,9},{9,8},{10,11... | collective-permute-start | bytes 49160 | tf_op jit(solution)/shard_map/ppermute | solution.py:30
  119.4 4.5 %collective-permute-start.2 = (f32[2,2048]{1,0:T(2,128)S(1)}, f32[2,2048]{1,0:T(2,128)S(1)}, u32[]{:S(2)}, u32[]{:S(2)}) collective-permute-start(f32[2,2048]{1,0:T(2,128)S(1)} %pad_maximum_fusion.10), channel_id=1, source_target_pairs={{0,2},{1,3},{2,0},{3,1},{4,6},{5,7},{6,4},{7,5},{8,10},{9,11},{10,... | collective-permute-start | bytes 49160 | tf_op jit(solution)/shard_map/ppermute | solution.py:30
  123.9 2.7 %collective-permute-start.3 = (f32[2,2048]{1,0:T(2,128)S(1)}, f32[2,2048]{1,0:T(2,128)S(1)}, u32[]{:S(2)}, u32[]{:S(2)}) collective-permute-start(f32[2,2048]{1,0:T(2,128)S(1)} %pad_maximum_fusion.11), channel_id=1, source_target_pairs={{0,4},{1,5},{2,6},{3,7},{4,0},{5,1},{6,2},{7,3},{8,12},{9,13},{10,... | collective-permute-start | bytes 49160 | tf_op jit(solution)/shard_map/ppermute | solution.py:30
  125.3 4.2 %collective-permute-start.7 = (f32[2,6144]{1,0:T(2,128)S(1)}, f32[2,6144]{1,0:T(2,128)S(1)}, u32[]{:S(2)}, u32[]{:S(2)}) collective-permute-start(f32[2,6144]{1,0:T(2,128)S(1)} %pad_maximum_fusion.3), channel_id=1, source_target_pairs={{0,1},{1,0},{2,3},{3,2},{4,5},{5,4},{6,7},{7,6},{8,9},{9,8},{10,11... | collective-permute-start | bytes 147464 | tf_op jit(solution)/shard_map/ppermute | solution.py:30
  126.7 4.2 %collective-permute-start.4 = (f32[2,2048]{1,0:T(2,128)S(1)}, f32[2,2048]{1,0:T(2,128)S(1)}, u32[]{:S(2)}, u32[]{:S(2)}) collective-permute-start(f32[2,2048]{1,0:T(2,128)S(1)} %pad_maximum_fusion.12), channel_id=1, source_target_pairs={{0,8},{1,9},{2,10},{3,11},{4,12},{5,13},{6,14},{7,15},{8,0},{9,1},... | collective-permute-start | bytes 49160 | tf_op jit(solution)/shard_map/ppermute | solution.py:30
  130.9 3.4 %collective-permute-start.5 = (f32[2,2048]{1,0:T(2,128)S(1)}, f32[2,2048]{1,0:T(2,128)S(1)}, u32[]{:S(2)}, u32[]{:S(2)}) collective-permute-start(f32[2,2048]{1,0:T(2,128)S(1)} %pad_maximum_fusion.13), channel_id=1, source_target_pairs={{0,16},{1,17},{2,18},{3,19},{4,20},{5,21},{6,22},{7,23},{8,24},{9,... | collective-permute-start | bytes 49160 | tf_op jit(solution)/shard_map/ppermute | solution.py:30
  132.1 4.9 %collective-permute-start.8 = (f32[2,6144]{1,0:T(2,128)S(1)}, f32[2,6144]{1,0:T(2,128)S(1)}, u32[]{:S(2)}, u32[]{:S(2)}) collective-permute-start(f32[2,6144]{1,0:T(2,128)S(1)} %pad_maximum_fusion.4), channel_id=1, source_target_pairs={{0,2},{1,3},{2,0},{3,1},{4,6},{5,7},{6,4},{7,5},{8,10},{9,11},{10,... | collective-permute-start | bytes 147464 | tf_op jit(solution)/shard_map/ppermute | solution.py:30
  134.3 4.2 %collective-permute-start.6 = (f32[2,2048]{1,0:T(2,128)S(1)}, f32[2,2048]{1,0:T(2,128)S(1)}, u32[]{:S(2)}, u32[]{:S(2)}) collective-permute-start(f32[2,2048]{1,0:T(2,128)S(1)} %pad_maximum_fusion.14), channel_id=1, source_target_pairs={{0,32},{1,33},{2,34},{3,35},{4,36},{5,37},{6,38},{7,39},{8,40},{9,... | collective-permute-start | bytes 49160 | tf_op jit(solution)/shard_map/ppermute | solution.py:30
  137.2 3.0 %collective-permute-start.9 = (f32[2,6144]{1,0:T(2,128)S(1)}, f32[2,6144]{1,0:T(2,128)S(1)}, u32[]{:S(2)}, u32[]{:S(2)}) collective-permute-start(f32[2,6144]{1,0:T(2,128)S(1)} %pad_maximum_fusion.5), channel_id=1, source_target_pairs={{0,4},{1,5},{2,6},{3,7},{4,0},{5,1},{6,2},{7,3},{8,12},{9,13},{10,... | collective-permute-start | bytes 147464 | tf_op jit(solution)/shard_map/ppermute | solution.py:30
  140.3 4.5 %collective-permute-start.10 = (f32[2,6144]{1,0:T(2,128)S(1)}, f32[2,6144]{1,0:T(2,128)S(1)}, u32[]{:S(2)}, u32[]{:S(2)}) collective-permute-start(f32[2,6144]{1,0:T(2,128)S(1)} %pad_maximum_fusion.6), channel_id=1, source_target_pairs={{0,8},{1,9},{2,10},{3,11},{4,12},{5,13},{6,14},{7,15},{8,0},{9,1},... | collective-permute-start | bytes 147464 | tf_op jit(solution)/shard_map/ppermute | solution.py:30
  145.0 9.8 %copy-start.1 = (f32[512,2048]{1,0:T(8,128)S(1)}, f32[512,2048]{1,0:T(8,128)}, u32[]{:S(2)}) copy-start(f32[512,2048]{1,0:T(8,128)} %copy-done) | copy-start | bytes 12582916
  145.0 6.6 %collective-permute-start.11 = (f32[2,6144]{1,0:T(2,128)S(1)}, f32[2,6144]{1,0:T(2,128)S(1)}, u32[]{:S(2)}, u32[]{:S(2)}) collective-permute-start(f32[2,6144]{1,0:T(2,128)S(1)} %pad_maximum_fusion.7), channel_id=1, source_target_pairs={{0,16},{1,17},{2,18},{3,19},{4,20},{5,21},{6,22},{7,23},{8,24},{9,... | collective-permute-start | bytes 147464 | tf_op jit(solution)/shard_map/ppermute | solution.py:30
  151.8 4.5 %collective-permute-start.12 = (f32[2,6144]{1,0:T(2,128)S(1)}, f32[2,6144]{1,0:T(2,128)S(1)}, u32[]{:S(2)}, u32[]{:S(2)}) collective-permute-start(f32[2,6144]{1,0:T(2,128)S(1)} %pad_maximum_fusion.8), channel_id=1, source_target_pairs={{0,32},{1,33},{2,34},{3,35},{4,36},{5,37},{6,38},{7,39},{8,40},{9,... | collective-permute-start | bytes 147464 | tf_op jit(solution)/shard_map/ppermute | solution.py:30
  165.9 12.7 %copy-start.2 = (f32[256,768]{1,0:T(8,128)S(1)}, f32[256,768]{1,0:T(8,128)}, u32[]{:S(2)}) copy-start(f32[256,768]{1,0:T(8,128)} %param.3) | copy-start | bytes 2359300
  165.9 12.7 %collective-permute-start.13 = (f32[256,768]{1,0:T(8,128)S(1)}, f32[256,768]{1,0:T(8,128)S(1)}, u32[]{:S(2)}, u32[]{:S(2)}) collective-permute-start(f32[256,768]{1,0:T(8,128)S(1)} %slice.159), channel_id=1, source_target_pairs={{0,64},{64,0},{1,65},{65,1},{2,66},{66,2},{3,67},{67,3},{4,68},{68... | collective-permute-start | bytes 2359304 | tf_op jit(solution)/shard_map/ppermute | solution.py:64
  177.4 1.2 collective-permute-start.14
Sparse Core Ops, SparseCore 0:
  10.7 93.9 all-gather.1

commit v8 on v4

--- a/solution.py
+++ b/solution.py
@@ -4,6 +4,7 @@
 import jax.numpy as jnp
 from jax import lax
 from jax.sharding import PartitionSpec as P
+
 
 HALVES = 2
 
@@ -22,14 +23,15 @@
     return jnp.stack([top, total])
 
 
-def group_log_total(local_max, local_sum):
+def group_log_total(local_max, local_sum, reverse):
     cent_count = lax.axis_size("cent")
     stats = jnp.stack([local_max, local_sum])
-    bit = 1
-    while bit < cent_count:
+    bits = [1 << k for k in range(cent_count.bit_length() - 1)]
+    if reverse:
+        bits = bits[::-1]
+    for bit in bits:
         partner = lax.ppermute(stats, "cent", [(i, i ^ bit) for i in range(cent_count)])
         stats = merge_stats(stats, partner)
-        bit *= 2
     return stats[0] + jnp.log(stats[1])
 
 
@@ -47,10 +49,10 @@
     halves = [members[index_h * span : (index_h + 1) * span] for index_h in range(HALVES)]
     scores = [score_block(half, both, score_scale) for half in halves]
     totals = []
-    for part in scores:
+    for index_h, part in enumerate(scores):
         local_max = jnp.max(part, axis=1)
         local_sum = jnp.sum(jnp.exp(part - local_max[:, None]), axis=1)
-        totals.append(group_log_total(local_max, local_sum))
+        totals.append(group_log_total(local_max, local_sum, index_h % 2 == 1))
     sums = None
     counts = None
     for part, total, half in zip(scores, totals, halves):

time: 174 us -> 175 us (level)
  waiting for transfers between devices: 100 us -> 103 us
  starting transfers between devices: 26.6 us -> 24.5 us
    ppermute x12, waiting for transfers between devices: 5.14 us -> 7.82 us  [group_log_total(): lax.ppermute(stats, 'cent', [(i, i ^ bit) for i in range(cent_count)])]
    ppermute x12, starting transfers between devices: 18.1 us -> 15.8 us  [group_log_total(): lax.ppermute(stats, 'cent', [(i, i ^ bit) for i in range(cent_count)])]
  transfers between devices with their start and end apart: 16 -> 16, of which waited for: 8 -> 11; matrix products, arithmetic and copies ran while one was open for 7% -> 7% of each run, Pallas kernels for 0% -> 0%
where the time goes in v8:
time: 175 us
  waiting for transfers between devices  103 us (59%)
  starting transfers between devices  24.5 us (14%)
  matrix products  23.8 us (14%)
  between operations  14.3 us (8%)
  other arithmetic  9.12 us (5%)
    all_gather x1, waiting for transfers between devices, on_device(): members = lax.all_gather(points, 'cent', axis=0, tiled=True)  92.6 us
    ppermute x12, starting transfers between devices, group_log_total(): lax.ppermute(stats, 'cent', [(i, i ^ bit) for i in range(cent_count)])  15.8 us
    dot_general x2, matrix products, on_device(): lax.dot_general(weights, half, (((0,), (0,)), ((), ())), preferred_elemen...  12.5 us
    dot_general x2, matrix products, score_block(): lax.dot_general(members, cent_block, (((1,), (1,)), ((), ())), preferred_...  11.3 us
    ppermute x12, waiting for transfers between devices, group_log_total(): lax.ppermute(stats, 'cent', [(i, i ^ bit) for i in range(cent_count)])  7.82 us
    ppermute x1, starting transfers between devices, on_device(): sent_sums = lax.ppermute(sums[:own_rows], 'dp', swap)  7.1 us
  transfers between devices with their start and end apart: 16, of which 11 were waited for; matrix products, arithmetic and copies ran while one was open for 7% of the time, Pallas kernels for 0%

profile of v8, /device:TPU:1, one launch (start us, length us, event | category | flops | bytes accessed | tf_op | source)
XLA Modules:
  0.0 174.8 jit_solution(3927220629782615859)
XLA Ops:
  7.2 0.7 all-gather.2.cloned.1.call-update
  7.9 1.2 convert_element_type.19
  9.1 1.5 collective-permute-start
  10.5 1.3 collective-permute-done
  11.9 0.2 multiply_reduce_fusion
  12.1 92.6 %all-gather.2.cloned.1.call-done = bf16[8192,768]{1,0:T(8,128)(2,1)} async-done(((bf16[128,768]{1,0:T(8,128)(2,1)}), bf16[8192,768]{1,0:T(8,128)(2,1)}) %all-gather.2.cloned.1.call-update) | async-done | bytes 12582928 | tf_op jit(solution)/shard_map/all_gather | solution.py:44
  104.7 5.6 %fusion.40 = (f32[4096]{0:T(1024)S(1)}, f32[512,4096]{1,0:T(8,128)S(1)}) fusion(f32[512]{0:T(512)S(1)} %multiply_reduce_fusion, bf16[8192,768]{1,0:T(8,128)(2,1)} %all-gather.2.cloned.1.call-done, bf16[256,768]{1,0:T(8,128)(2,1)S(1)} %convert_element_type.19, bf16[256,768]{1,0:T(8,128)(2,1)S(1)} %collective-permute-done), kind=kOutput, calls=%fused_computation.98 | convolution fusion | flops 3231182848 | bytes 15484928 | tf_op jit(solution)/shard_map/dot_general | solution.py:14
  110.3 1.3 exponential_reduce_fusion
  111.6 2.7 %collective-permute-start.7 = (f32[2,4096]{1,0:T(2,128)S(1)}, f32[2,4096]{1,0:T(2,128)S(1)}, u32[]{:S(2)}, u32[]{:S(2)}) collective-permute-start(f32[2,4096]{1,0:T(2,128)S(1)} %pad_maximum_fusion.9), channel_id=1, source_target_pairs={{0,32},{1,33},{2,34},{3,35},{4,36},{5,37},{6,38},{7,39},{8,40},{9,... | collective-permute-start | bytes 98312 | tf_op jit(solution)/shard_map/ppermute | solution.py:33
  114.4 5.6 %fusion.41 = (f32[4096]{0:T(1024)S(1)}, f32[512,4096]{1,0:T(8,128)S(1)}) fusion(f32[512]{0:T(512)S(1)} %multiply_reduce_fusion, bf16[8192,768]{1,0:T(8,128)(2,1)} %all-gather.2.cloned.1.call-done, bf16[256,768]{1,0:T(8,128)(2,1)S(1)} %convert_element_type.19, bf16[256,768]{1,0:T(8,128)(2,1)S(1)} %collective-permute-done), kind=kOutput, calls=%fused_computation.99 | convolution fusion | flops 3231182848 | bytes 15484928 | tf_op jit(solution)/shard_map/dot_general | solution.py:14
  120.0 1.3 exponential_reduce_fusion.1
  121.3 1.3 collective-permute-start.1
  122.6 0.1 multiply_add_fusion.4
  122.7 0.5 collective-permute-start.8
  123.1 1.0 collective-permute-done.1
  124.2 0.1 multiply_add_fusion.9
  124.3 2.8 %collective-permute-start.2 = (f32[2,4096]{1,0:T(2,128)S(1)}, f32[2,4096]{1,0:T(2,128)S(1)}, u32[]{:S(2)}, u32[]{:S(2)}) collective-permute-start(f32[2,4096]{1,0:T(2,128)S(1)} %pad_maximum_fusion.4), channel_id=1, source_target_pairs={{0,2},{1,3},{2,0},{3,1},{4,6},{5,7},{6,4},{7,5},{8,10},{9,11},{10,... | collective-permute-start | bytes 98312 | tf_op jit(solution)/shard_map/ppermute | solution.py:33
  127.0 0.1 multiply_add_fusion.3
  127.2 1.3 collective-permute-start.9
  128.5 0.1 collective-permute-done.2
  128.6 0.1 multiply_add_fusion.8
  128.7 1.2 collective-permute-start.3
  130.0 1.7 collective-permute-done.9
  131.6 0.1 multiply_add_fusion.2
  131.8 0.1 collective-permute-start.10
  131.9 0.1 multiply_add_fusion.7
  132.0 2.5 %collective-permute-start.4 = (f32[2,4096]{1,0:T(2,128)S(1)}, f32[2,4096]{1,0:T(2,128)S(1)}, u32[]{:S(2)}, u32[]{:S(2)}) collective-permute-start(f32[2,4096]{1,0:T(2,128)S(1)} %pad_maximum_fusion.6), channel_id=1, source_target_pairs={{0,8},{1,9},{2,10},{3,11},{4,12},{5,13},{6,14},{7,15},{8,0},{9,1},... | collective-permute-start | bytes 98312 | tf_op jit(solution)/shard_map/ppermute | solution.py:33
  134.5 0.3 collective-permute-done.10
  134.8 0.1 multiply_add_fusion.1
  134.9 1.1 collective-permute-start.11
  136.0 0.3 collective-permute-done.4
  136.3 0.1 multiply_add_fusion.6
  136.4 0.5 collective-permute-start.5
  136.9 2.4 %collective-permute-done.11 = f32[2,4096]{1,0:T(2,128)S(1)} collective-permute-done((f32[2,4096]{1,0:T(2,128)S(1)}, f32[2,4096]{1,0:T(2,128)S(1)}, u32[]{:S(2)}, u32[]{:S(2)}) %collective-permute-start.11) | collective-permute-done | bytes 32800 | tf_op jit(solution)/shard_map/ppermute | solution.py:33
  139.3 0.1 slice_maximum_fusion
  139.4 0.3 collective-permute-start.12
  139.8 1.6 collective-permute-start.6
  141.4 0.9 collective-permute-done.12
  142.3 1.2 convert_reduce_fusion
  143.5 1.1 collective-permute-done.6
  144.7 6.3 %fusion = f32[512,768]{1,0:T(8,128)S(1)} fusion(bf16[8192,768]{1,0:T(8,128)(2,1)} %all-gather.2.cloned.1.call-done, f32[512,4096]{1,0:T(8,128)S(1)} %get-tuple-element.47, f32[4096]{0:T(1024)S(1)} %log_add_fusion), kind=kOutput, calls=%fused_computation.8 | convolution fusion | flops 3225419776 | bytes 16269312 | tf_op jit(solution)/shard_map/dot_general | solution.py:60
  151.0 6.2 %fusion.6 = f32[512,768]{1,0:T(8,128)S(1)} fusion(f32[512,768]{1,0:T(8,128)S(1)} %fusion, bf16[8192,768]{1,0:T(8,128)(2,1)} %all-gather.2.cloned.1.call-done, f32[512,4096]{1,0:T(8,128)S(1)} %get-tuple-element.49, f32[4096]{0:T(1024)S(1)} %log_add_fusion.1), kind=kOutput, calls=%fused_computation.15 | convolution fusion | flops 3225812992 | bytes 17842176 | tf_op jit(solution)/shard_map/dot_general | solution.py:60
  157.3 7.1 %collective-permute-start.13 = (f32[256,768]{1,0:T(8,128)S(1)}, f32[256,768]{1,0:T(8,128)S(1)}, u32[]{:S(2)}, u32[]{:S(2)}) collective-permute-start(f32[256,768]{1,0:T(8,128)S(1)} %slice.159), channel_id=1, source_target_pairs={{0,64},{64,0},{1,65},{65,1},{2,66},{66,2},{3,67},{67,3},{4,68},{68... | collective-permute-start | bytes 2359304 | tf_op jit(solution)/shard_map/ppermute | solution.py:66
  164.4 1.2 convert_reduce_fusion.1
  165.6 0.1 collective-permute-start.14
  165.7 0.6 fusion.35
  166.3 0.6 collective-permute-done.14
  166.9 1.0 fusion.10
  (29 shorter events, 0.8 us)
Async XLA Ops:
  7.2 97.5 %all-gather.2.cloned.1.call-start = ((), (), s32[]{:S(2)}) async-start(), calls=%async_computation | async-start | bytes 12779520 | tf_op jit(solution)/shard_map/all_gather | solution.py:44
  9.1 2.8 %collective-permute-start = (bf16[256,768]{1,0:T(8,128)(2,1)S(1)}, bf16[256,768]{1,0:T(8,128)(2,1)S(1)}, u32[]{:S(2)}, u32[]{:S(2)}) collective-permute-start(bf16[256,768]{1,0:T(8,128)(2,1)S(1)} %convert_element_type.19), channel_id=1, source_target_pairs={{0,64},{64,0},{1,65},{65,1},{2,66},{66,2},{3,67},{67,3},{4,68},{68... | collective-permute-start | bytes 1179656 | tf_op jit(solution)/shard_map/ppermute | solution.py:45
  111.6 10.9 %collective-permute-start.7 = (f32[2,4096]{1,0:T(2,128)S(1)}, f32[2,4096]{1,0:T(2,128)S(1)}, u32[]{:S(2)}, u32[]{:S(2)}) collective-permute-start(f32[2,4096]{1,0:T(2,128)S(1)} %pad_maximum_fusion.9), channel_id=1, source_target_pairs={{0,32},{1,33},{2,34},{3,35},{4,36},{5,37},{6,38},{7,39},{8,40},{9,... | collective-permute-start | bytes 98312 | tf_op jit(solution)/shard_map/ppermute | solution.py:33
  121.3 2.8 %collective-permute-start.1 = (f32[2,4096]{1,0:T(2,128)S(1)}, f32[2,4096]{1,0:T(2,128)S(1)}, u32[]{:S(2)}, u32[]{:S(2)}) collective-permute-start(f32[2,4096]{1,0:T(2,128)S(1)} %pad_maximum_fusion.3), channel_id=1, source_target_pairs={{0,1},{1,0},{2,3},{3,2},{4,5},{5,4},{6,7},{7,6},{8,9},{9,8},{10,11... | collective-permute-start | bytes 98312 | tf_op jit(solution)/shard_map/ppermute | solution.py:33
  122.7 4.4 %collective-permute-start.8 = (f32[2,4096]{1,0:T(2,128)S(1)}, f32[2,4096]{1,0:T(2,128)S(1)}, u32[]{:S(2)}, u32[]{:S(2)}) collective-permute-start(f32[2,4096]{1,0:T(2,128)S(1)} %pad_maximum_fusion.10), channel_id=1, source_target_pairs={{0,16},{1,17},{2,18},{3,19},{4,20},{5,21},{6,22},{7,23},{8,24},{9,... | collective-permute-start | bytes 98312 | tf_op jit(solution)/shard_map/ppermute | solution.py:33
  124.3 4.3 %collective-permute-start.2 = (f32[2,4096]{1,0:T(2,128)S(1)}, f32[2,4096]{1,0:T(2,128)S(1)}, u32[]{:S(2)}, u32[]{:S(2)}) collective-permute-start(f32[2,4096]{1,0:T(2,128)S(1)} %pad_maximum_fusion.4), channel_id=1, source_target_pairs={{0,2},{1,3},{2,0},{3,1},{4,6},{5,7},{6,4},{7,5},{8,10},{9,11},{10,... | collective-permute-start | bytes 98312 | tf_op jit(solution)/shard_map/ppermute | solution.py:33
  127.2 4.5 %collective-permute-start.9 = (f32[2,4096]{1,0:T(2,128)S(1)}, f32[2,4096]{1,0:T(2,128)S(1)}, u32[]{:S(2)}, u32[]{:S(2)}) collective-permute-start(f32[2,4096]{1,0:T(2,128)S(1)} %pad_maximum_fusion.11), channel_id=1, source_target_pairs={{0,8},{1,9},{2,10},{3,11},{4,12},{5,13},{6,14},{7,15},{8,0},{9,1},... | collective-permute-start | bytes 98312 | tf_op jit(solution)/shard_map/ppermute | solution.py:33
  128.7 3.1 %collective-permute-start.3 = (f32[2,4096]{1,0:T(2,128)S(1)}, f32[2,4096]{1,0:T(2,128)S(1)}, u32[]{:S(2)}, u32[]{:S(2)}) collective-permute-start(f32[2,4096]{1,0:T(2,128)S(1)} %pad_maximum_fusion.5), channel_id=1, source_target_pairs={{0,4},{1,5},{2,6},{3,7},{4,0},{5,1},{6,2},{7,3},{8,12},{9,13},{10,... | collective-permute-start | bytes 98312 | tf_op jit(solution)/shard_map/ppermute | solution.py:33
  131.8 3.1 %collective-permute-start.10 = (f32[2,4096]{1,0:T(2,128)S(1)}, f32[2,4096]{1,0:T(2,128)S(1)}, u32[]{:S(2)}, u32[]{:S(2)}) collective-permute-start(f32[2,4096]{1,0:T(2,128)S(1)} %pad_maximum_fusion.12), channel_id=1, source_target_pairs={{0,4},{1,5},{2,6},{3,7},{4,0},{5,1},{6,2},{7,3},{8,12},{9,13},{10,... | collective-permute-start | bytes 98312 | tf_op jit(solution)/shard_map/ppermute | solution.py:33
  132.0 4.3 %collective-permute-start.4 = (f32[2,4096]{1,0:T(2,128)S(1)}, f32[2,4096]{1,0:T(2,128)S(1)}, u32[]{:S(2)}, u32[]{:S(2)}) collective-permute-start(f32[2,4096]{1,0:T(2,128)S(1)} %pad_maximum_fusion.6), channel_id=1, source_target_pairs={{0,8},{1,9},{2,10},{3,11},{4,12},{5,13},{6,14},{7,15},{8,0},{9,1},... | collective-permute-start | bytes 98312 | tf_op jit(solution)/shard_map/ppermute | solution.py:33
  134.9 4.3 %collective-permute-start.11 = (f32[2,4096]{1,0:T(2,128)S(1)}, f32[2,4096]{1,0:T(2,128)S(1)}, u32[]{:S(2)}, u32[]{:S(2)}) collective-permute-start(f32[2,4096]{1,0:T(2,128)S(1)} %pad_maximum_fusion.13), channel_id=1, source_target_pairs={{0,2},{1,3},{2,0},{3,1},{4,6},{5,7},{6,4},{7,5},{8,10},{9,11},{10,... | collective-permute-start | bytes 98312 | tf_op jit(solution)/shard_map/ppermute | solution.py:33
  136.4 3.3 %collective-permute-start.5 = (f32[2,4096]{1,0:T(2,128)S(1)}, f32[2,4096]{1,0:T(2,128)S(1)}, u32[]{:S(2)}, u32[]{:S(2)}) collective-permute-start(f32[2,4096]{1,0:T(2,128)S(1)} %pad_maximum_fusion.7), channel_id=1, source_target_pairs={{0,16},{1,17},{2,18},{3,19},{4,20},{5,21},{6,22},{7,23},{8,24},{9,... | collective-permute-start | bytes 98312 | tf_op jit(solution)/shard_map/ppermute | solution.py:33
  139.4 2.8 %collective-permute-start.12 = (f32[2,4096]{1,0:T(2,128)S(1)}, f32[2,4096]{1,0:T(2,128)S(1)}, u32[]{:S(2)}, u32[]{:S(2)}) collective-permute-start(f32[2,4096]{1,0:T(2,128)S(1)} %pad_maximum_fusion.14), channel_id=1, source_target_pairs={{0,1},{1,0},{2,3},{3,2},{4,5},{5,4},{6,7},{7,6},{8,9},{9,8},{10,11... | collective-permute-start | bytes 98312 | tf_op jit(solution)/shard_map/ppermute | solution.py:33
  139.8 4.8 %collective-permute-start.6 = (f32[2,4096]{1,0:T(2,128)S(1)}, f32[2,4096]{1,0:T(2,128)S(1)}, u32[]{:S(2)}, u32[]{:S(2)}) collective-permute-start(f32[2,4096]{1,0:T(2,128)S(1)} %pad_maximum_fusion.8), channel_id=1, source_target_pairs={{0,32},{1,33},{2,34},{3,35},{4,36},{5,37},{6,38},{7,39},{8,40},{9,... | collective-permute-start | bytes 98312 | tf_op jit(solution)/shard_map/ppermute | solution.py:33
  157.3 9.6 %copy-start = (f32[256,768]{1,0:T(8,128)S(1)}, f32[256,768]{1,0:T(8,128)}, u32[]{:S(2)}) copy-start(f32[256,768]{1,0:T(8,128)} %param.3) | copy-start | bytes 2359300
  157.3 9.5 %collective-permute-start.13 = (f32[256,768]{1,0:T(8,128)S(1)}, f32[256,768]{1,0:T(8,128)S(1)}, u32[]{:S(2)}, u32[]{:S(2)}) collective-permute-start(f32[256,768]{1,0:T(8,128)S(1)} %slice.159), channel_id=1, source_target_pairs={{0,64},{64,0},{1,65},{65,1},{2,66},{66,2},{3,67},{67,3},{4,68},{68... | collective-permute-start | bytes 2359304 | tf_op jit(solution)/shard_map/ppermute | solution.py:66
  165.6 1.2 collective-permute-start.14
Sparse Core Ops, SparseCore 0:
  10.7 93.9 all-gather.1

commit v9 on v4

--- a/solution.py
+++ b/solution.py
@@ -5,7 +5,9 @@
 from jax import lax
 from jax.sharding import PartitionSpec as P
 
+
 HALVES = 2
+COUNT_LANES = 128
 
 
 def score_block(members, cent_block, score_scale):
@@ -55,10 +57,14 @@
     counts = None
     for part, total, half in zip(scores, totals, halves):
         weights = jnp.exp(part - total[:, None]).astype(jnp.bfloat16)
-        part_sums = lax.dot_general(
-            weights, half, (((0,), (0,)), ((), ())), preferred_element_type=jnp.float32
+        extended = jnp.concatenate(
+            [half, jnp.ones((half.shape[0], COUNT_LANES), half.dtype)], axis=1
         )
-        part_counts = jnp.sum(weights, axis=0, dtype=jnp.float32)
+        both_sums = lax.dot_general(
+            weights, extended, (((0,), (0,)), ((), ())), preferred_element_type=jnp.float32
+        )
+        part_sums = both_sums[:, : half.shape[1]]
+        part_counts = both_sums[:, half.shape[1]]
         sums = part_sums if sums is None else sums + part_sums
         counts = part_counts if counts is None else counts + part_counts
     sent_sums = lax.ppermute(sums[:own_rows], "dp", swap)

time: 174 us -> 179 us (1.029)
  local copies, waits for them, and re-layouts: 0.12 us -> 7.28 us
  starting transfers between devices: 26.6 us -> 24.2 us
    unnamed x2 -> x18, local copies, waits for them, and re-layouts: 0.01 us -> 3.68 us
    slice x0 -> x1, local copies, waits for them, and re-layouts: none -> 3.35 us  [on_device(): members[index_h * span:(index_h + 1) * span]]
    reduce_sum x2 -> x0, other arithmetic: 2.37 us -> none  [on_device(): part_counts = jnp.sum(weights, axis=0, dtype=jnp.float32)]
    dot_general x2, matrix products: 11.3 us -> 9.45 us  [score_block(): lax.dot_general(members, cent_block, (((1,), (1,)), ((), ())), preferred_...]
  transfers between devices with their start and end apart: 16 -> 16, of which waited for: 8 -> 9; matrix products, arithmetic and copies ran while one was open for 7% -> 12% of each run, Pallas kernels for 0% -> 0%
where the time goes in v9:
time: 179 us; the launch traced here: 178 us
  waiting for transfers between devices  99.9 us (56%)
  starting transfers between devices  24.2 us (14%)
  matrix products  22.7 us (13%)
  between operations  14.3 us (8%)
  other arithmetic  9.92 us (6%)
  local copies, waits for them, and re-layouts  7.28 us (4%)
    all_gather x1, waiting for transfers between devices, on_device(): members = lax.all_gather(points, 'cent', axis=0, tiled=True)  91.8 us
    ppermute x12, starting transfers between devices, group_log_total(): lax.ppermute(stats, 'cent', [(i, i ^ bit) for i in range(cent_count)])  16.4 us
    dot_general x2, matrix products, on_device(): lax.dot_general(weights, extended, (((0,), (0,)), ((), ())), preferred_el...  13.3 us
    dot_general x2, matrix products, score_block(): lax.dot_general(members, cent_block, (((1,), (1,)), ((), ())), preferred_...  9.45 us
    ppermute x1, starting transfers between devices, on_device(): sent_sums = lax.ppermute(sums[:own_rows], 'dp', swap)  6.19 us
    ppermute x12, waiting for transfers between devices, group_log_total(): lax.ppermute(stats, 'cent', [(i, i ^ bit) for i in range(cent_count)])  5.5 us
    unnamed x18, local copies, waits for them, and re-layouts  3.68 us
  transfers between devices with their start and end apart: 16, of which 9 were waited for; matrix products, arithmetic and copies ran while one was open for 12% of the time, Pallas kernels for 0%

profile of v9, /device:TPU:1, one launch (start us, length us, event | category | flops | bytes accessed | tf_op | source)
XLA Modules:
  0.0 178.3 jit_solution(16570985452605458364)
XLA Ops:
  7.2 0.7 all-gather.2.cloned.1.call-update
  7.9 1.2 convert_element_type.13
  9.1 1.5 collective-permute-start
  10.6 1.3 collective-permute-done
  11.9 0.8 copy-done.7
  12.7 0.2 multiply_reduce_fusion
  12.9 91.8 %all-gather.2.cloned.1.call-done = bf16[8192,768]{1,0:T(8,128)(2,1)} async-done(((bf16[128,768]{1,0:T(8,128)(2,1)}), bf16[8192,768]{1,0:T(8,128)(2,1)}) %all-gather.2.cloned.1.call-update) | async-done | bytes 12582928 | tf_op jit(solution)/shard_map/all_gather | solution.py:44
  104.7 6.0 %fusion.42 = (f32[4096]{0:T(1024)S(1)}, f32[512,4096]{1,0:T(8,128)S(1)}) fusion(f32[512]{0:T(512)S(1)} %multiply_reduce_fusion, bf16[8192,768]{1,0:T(8,128)(2,1)} %all-gather.2.cloned.1.call-done, bf16[256,768]{1,0:T(8,128)(2,1)} %copy-done.5, bf16[256,768]{1,0:T(8,128)(2,1)} %copy-done.7), kind=kOutput, calls=%fused_computation.104 | convolution fusion | flops 3231182848 | bytes 15484928 | tf_op jit(solution)/shard_map/dot_general | solution.py:15
  110.7 1.3 exponential_reduce_fusion
  112.0 1.9 %copy-done.1 = f32[512,4096]{1,0:T(8,128)} copy-done((f32[512,4096]{1,0:T(8,128)}, f32[512,4096]{1,0:T(8,128)S(1)}, u32[]{:S(2)}) %copy-start.1) | copy-done | bytes 8388632
  113.9 1.2 collective-permute-start.7
  115.1 3.5 %fusion.43 = (f32[4096]{0:T(1024)S(1)}, f32[512,4096]{1,0:T(8,128)S(1)}) fusion(f32[512]{0:T(512)S(1)} %multiply_reduce_fusion, bf16[8192,768]{1,0:T(8,128)(2,1)S(1)} %copy-done, bf16[256,768]{1,0:T(8,128)(2,1)S(1)} %copy-done.6, bf16[256,768]{1,0:T(8,128)(2,1)S(1)} %copy-done.8), kind=kOutput, calls=%fused_computation.105 | convolution fusion | flops 3231182848 | bytes 15484928 | tf_op jit(solution)/shard_map/dot_general | solution.py:15
  118.6 1.3 exponential_reduce_fusion.1
  119.9 0.4 collective-permute-start.1
  120.2 3.3 %fusion.39 = (bf16[4096,768]{1,0:T(8,128)(2,1)S(1)}, bf16[4096,768]{1,0:T(8,128)(2,1)}) fusion(bf16[8192,768]{1,0:T(8,128)(2,1)S(1)} %copy-done), kind=kLoop, calls=%fused_computation.101 | loop fusion | bytes 25165824 | tf_op jit(solution)/shard_map/slice | solution.py:49
  123.6 0.9 multiply_add_fusion.4
  124.5 2.8 %collective-permute-start.8 = (f32[2,4096]{1,0:T(2,128)S(1)}, f32[2,4096]{1,0:T(2,128)S(1)}, u32[]{:S(2)}, u32[]{:S(2)}) collective-permute-start(f32[2,4096]{1,0:T(2,128)S(1)} %pad_maximum_fusion.10), channel_id=1, source_target_pairs={{0,2},{1,3},{2,0},{3,1},{4,6},{5,7},{6,4},{7,5},{8,10},{9,11},{10,... | collective-permute-start | bytes 98312 | tf_op jit(solution)/shard_map/ppermute | solution.py:32
  127.3 0.1 multiply_add_fusion.9
  127.4 0.4 collective-permute-start.2
  127.8 1.1 collective-permute-done.8
  128.9 0.1 multiply_add_fusion.3
  129.0 1.3 collective-permute-start.9
  130.3 1.5 collective-permute-done.2
  131.8 0.1 multiply_add_fusion.8
  131.9 1.3 collective-permute-start.3
  133.2 0.1 multiply_add_fusion.2
  133.3 2.5 %collective-permute-start.10 = (f32[2,4096]{1,0:T(2,128)S(1)}, f32[2,4096]{1,0:T(2,128)S(1)}, u32[]{:S(2)}, u32[]{:S(2)}) collective-permute-start(f32[2,4096]{1,0:T(2,128)S(1)} %pad_maximum_fusion.12), channel_id=1, source_target_pairs={{0,8},{1,9},{2,10},{3,11},{4,12},{5,13},{6,14},{7,15},{8,0},{9,1},... | collective-permute-start | bytes 98312 | tf_op jit(solution)/shard_map/ppermute | solution.py:32
  135.9 2.3 %collective-permute-start.4 = (f32[2,4096]{1,0:T(2,128)S(1)}, f32[2,4096]{1,0:T(2,128)S(1)}, u32[]{:S(2)}, u32[]{:S(2)}) collective-permute-start(f32[2,4096]{1,0:T(2,128)S(1)} %pad_maximum_fusion.6), channel_id=1, source_target_pairs={{0,8},{1,9},{2,10},{3,11},{4,12},{5,13},{6,14},{7,15},{8,0},{9,1},... | collective-permute-start | bytes 98312 | tf_op jit(solution)/shard_map/ppermute | solution.py:32
  138.2 0.1 multiply_add_fusion.1
  138.3 0.1 collective-permute-start.11
  138.4 2.2 %collective-permute-done.4 = f32[2,4096]{1,0:T(2,128)S(1)} collective-permute-done((f32[2,4096]{1,0:T(2,128)S(1)}, f32[2,4096]{1,0:T(2,128)S(1)}, u32[]{:S(2)}, u32[]{:S(2)}) %collective-permute-start.4) | collective-permute-done | bytes 32800 | tf_op jit(solution)/shard_map/ppermute | solution.py:32
  140.7 0.3 collective-permute-start.5
  141.0 0.5 collective-permute-done.11
  141.5 2.2 %collective-permute-start.12 = (f32[2,4096]{1,0:T(2,128)S(1)}, f32[2,4096]{1,0:T(2,128)S(1)}, u32[]{:S(2)}, u32[]{:S(2)}) collective-permute-start(f32[2,4096]{1,0:T(2,128)S(1)} %pad_maximum_fusion.14), channel_id=1, source_target_pairs={{0,32},{1,33},{2,34},{3,35},{4,36},{5,37},{6,38},{7,39},{8,40},{9,... | collective-permute-start | bytes 98312 | tf_op jit(solution)/shard_map/ppermute | solution.py:32
  143.7 0.1 collective-permute-done.5
  143.9 1.8 %collective-permute-start.6 = (f32[2,4096]{1,0:T(2,128)S(1)}, f32[2,4096]{1,0:T(2,128)S(1)}, u32[]{:S(2)}, u32[]{:S(2)}) collective-permute-start(f32[2,4096]{1,0:T(2,128)S(1)} %pad_maximum_fusion.8), channel_id=1, source_target_pairs={{0,32},{1,33},{2,34},{3,35},{4,36},{5,37},{6,38},{7,39},{8,40},{9,... | collective-permute-start | bytes 98312 | tf_op jit(solution)/shard_map/ppermute | solution.py:32
  145.7 0.2 collective-permute-done.12
  146.0 8.8 %fusion = f32[512,896]{1,0:T(8,128)S(1)} fusion(bf16[4096,768]{1,0:T(8,128)(2,1)} %get-tuple-element.21, f32[512,4096]{1,0:T(8,128)} %copy-done.1, f32[4096]{0:T(1024)S(1)} %log_add_fusion), kind=kOutput, calls=%fused_computation.6 | convolution fusion | flops 3762290688 | bytes 16531456 | tf_op jit(solution)/shard_map/dot_general | solution.py:63
  154.9 4.5 %fusion.2 = f32[512,896]{1,0:T(8,128)S(1)} fusion(bf16[4096,768]{1,0:T(8,128)(2,1)S(1)} %get-tuple-element.20, f32[512,4096]{1,0:T(8,128)S(1)} %get-tuple-element.53, f32[4096]{0:T(1024)S(1)} %log_add_fusion.1), kind=kOutput, calls=%fused_computation.8 | convolution fusion | flops 3762290688 | bytes 16531456 | tf_op jit(solution)/shard_map/dot_general | solution.py:63
  159.4 0.2 slice_add_fusion
  159.6 1.0 copy-done.4
  160.7 6.2 %collective-permute-start.13 = (f32[256,768]{1,0:T(8,128)S(1)}, f32[256,768]{1,0:T(8,128)}, u32[]{:S(2)}, u32[]{:S(2)}) collective-permute-start(f32[256,768]{1,0:T(8,128)S(1)} %slice.185), channel_id=1, source_target_pairs={{0,64},{64,0},{1,65},{65,1},{2,66},{66,2},{3,67},{67,3},{4,68},{68... | collective-permute-start | bytes 2359304 | tf_op jit(solution)/shard_map/ppermute | solution.py:70
  166.8 1.1 slice_add_fusion.2
  167.9 0.1 slice_reduce_fusion
  168.1 0.1 collective-permute-start.14
  168.2 0.6 fusion.32
  168.7 0.6 collective-permute-done.14
  169.3 2.2 %fusion.7 = f32[256,768]{1,0:T(8,128)} fusion(f32[256,768]{1,0:T(8,128)S(1)} %copy-done.2, f32[256,768]{1,0:T(8,128)} %collective-permute-done.13, f32[512,768]{1,0:T(8,128)S(1)} %slice_add_fusion, f32[256]{0:T(256)S(1)} %add_add_fusion), kind=kLoop, calls=%fused_computation.16 | loop fusion | flops 589824 | bytes 3146752 | tf_op jit(solution)/shard_map/div | solution.py:74
  (45 shorter events, 1.0 us)
Async XLA Ops:
  7.2 97.5 %all-gather.2.cloned.1.call-start = ((), (), s32[]{:S(2)}) async-start(), calls=%async_computation | async-start | bytes 12779520 | tf_op jit(solution)/shard_map/all_gather | solution.py:44
  9.1 2.8 %copy-start.5 = (bf16[256,768]{1,0:T(8,128)(2,1)}, bf16[256,768]{1,0:T(8,128)(2,1)S(1)}, u32[]{:S(2)}) copy-start(bf16[256,768]{1,0:T(8,128)(2,1)S(1)} %convert_element_type.13) | copy-start | bytes 1179652
  9.1 2.8 %collective-permute-start = (bf16[256,768]{1,0:T(8,128)(2,1)S(1)}, bf16[256,768]{1,0:T(8,128)(2,1)S(1)}, u32[]{:S(2)}, u32[]{:S(2)}) collective-permute-start(bf16[256,768]{1,0:T(8,128)(2,1)S(1)} %convert_element_type.13), channel_id=1, source_target_pairs={{0,64},{64,0},{1,65},{65,1},{2,66},{66,2},{3,67},{67,3},{4,68},{68... | collective-permute-start | bytes 1179656 | tf_op jit(solution)/shard_map/ppermute | solution.py:45
  11.9 0.8 copy-start.7
  104.7 10.4 %copy-start = (bf16[8192,768]{1,0:T(8,128)(2,1)S(1)}, bf16[8192,768]{1,0:T(8,128)(2,1)}, u32[]{:S(2)}) copy-start(bf16[8192,768]{1,0:T(8,128)(2,1)} %all-gather.2.cloned.1.call-done) | copy-start | bytes 37748740
  110.7 3.2 %copy-start.1 = (f32[512,4096]{1,0:T(8,128)}, f32[512,4096]{1,0:T(8,128)S(1)}, u32[]{:S(2)}) copy-start(f32[512,4096]{1,0:T(8,128)S(1)} %get-tuple-element.51) | copy-start | bytes 25165828
  110.7 4.4 %copy-start.6 = (bf16[256,768]{1,0:T(8,128)(2,1)S(1)}, bf16[256,768]{1,0:T(8,128)(2,1)}, u32[]{:S(2)}) copy-start(bf16[256,768]{1,0:T(8,128)(2,1)} %copy-done.5) | copy-start | bytes 1179652
  110.7 4.4 %copy-start.8 = (bf16[256,768]{1,0:T(8,128)(2,1)S(1)}, bf16[256,768]{1,0:T(8,128)(2,1)}, u32[]{:S(2)}) copy-start(bf16[256,768]{1,0:T(8,128)(2,1)} %copy-done.7) | copy-start | bytes 1179652
  113.9 9.7 %collective-permute-start.7 = (f32[2,4096]{1,0:T(2,128)S(1)}, f32[2,4096]{1,0:T(2,128)}, u32[]{:S(2)}, u32[]{:S(2)}) collective-permute-start(f32[2,4096]{1,0:T(2,128)S(1)} %pad_maximum_fusion.9), channel_id=1, source_target_pairs={{0,1},{1,0},{2,3},{3,2},{4,5},{5,4},{6,7},{7,6},{8,9},{9,8},{10,11... | collective-permute-start | bytes 98312 | tf_op jit(solution)/shard_map/ppermute | solution.py:32
  119.9 7.4 %collective-permute-start.1 = (f32[2,4096]{1,0:T(2,128)S(1)}, f32[2,4096]{1,0:T(2,128)S(1)}, u32[]{:S(2)}, u32[]{:S(2)}) collective-permute-start(f32[2,4096]{1,0:T(2,128)S(1)} %pad_maximum_fusion.3), channel_id=1, source_target_pairs={{0,1},{1,0},{2,3},{3,2},{4,5},{5,4},{6,7},{7,6},{8,9},{9,8},{10,11... | collective-permute-start | bytes 98312 | tf_op jit(solution)/shard_map/ppermute | solution.py:32
  124.5 4.3 %collective-permute-start.8 = (f32[2,4096]{1,0:T(2,128)S(1)}, f32[2,4096]{1,0:T(2,128)S(1)}, u32[]{:S(2)}, u32[]{:S(2)}) collective-permute-start(f32[2,4096]{1,0:T(2,128)S(1)} %pad_maximum_fusion.10), channel_id=1, source_target_pairs={{0,2},{1,3},{2,0},{3,1},{4,6},{5,7},{6,4},{7,5},{8,10},{9,11},{10,... | collective-permute-start | bytes 98312 | tf_op jit(solution)/shard_map/ppermute | solution.py:32
  127.4 4.3 %collective-permute-start.2 = (f32[2,4096]{1,0:T(2,128)S(1)}, f32[2,4096]{1,0:T(2,128)S(1)}, u32[]{:S(2)}, u32[]{:S(2)}) collective-permute-start(f32[2,4096]{1,0:T(2,128)S(1)} %pad_maximum_fusion.4), channel_id=1, source_target_pairs={{0,2},{1,3},{2,0},{3,1},{4,6},{5,7},{6,4},{7,5},{8,10},{9,11},{10,... | collective-permute-start | bytes 98312 | tf_op jit(solution)/shard_map/ppermute | solution.py:32
  129.0 4.2 %collective-permute-start.9 = (f32[2,4096]{1,0:T(2,128)S(1)}, f32[2,4096]{1,0:T(2,128)S(1)}, u32[]{:S(2)}, u32[]{:S(2)}) collective-permute-start(f32[2,4096]{1,0:T(2,128)S(1)} %pad_maximum_fusion.11), channel_id=1, source_target_pairs={{0,4},{1,5},{2,6},{3,7},{4,0},{5,1},{6,2},{7,3},{8,12},{9,13},{10,... | collective-permute-start | bytes 98312 | tf_op jit(solution)/shard_map/ppermute | solution.py:32
  131.9 3.9 %collective-permute-start.3 = (f32[2,4096]{1,0:T(2,128)S(1)}, f32[2,4096]{1,0:T(2,128)S(1)}, u32[]{:S(2)}, u32[]{:S(2)}) collective-permute-start(f32[2,4096]{1,0:T(2,128)S(1)} %pad_maximum_fusion.5), channel_id=1, source_target_pairs={{0,4},{1,5},{2,6},{3,7},{4,0},{5,1},{6,2},{7,3},{8,12},{9,13},{10,... | collective-permute-start | bytes 98312 | tf_op jit(solution)/shard_map/ppermute | solution.py:32
  133.3 4.9 %collective-permute-start.10 = (f32[2,4096]{1,0:T(2,128)S(1)}, f32[2,4096]{1,0:T(2,128)S(1)}, u32[]{:S(2)}, u32[]{:S(2)}) collective-permute-start(f32[2,4096]{1,0:T(2,128)S(1)} %pad_maximum_fusion.12), channel_id=1, source_target_pairs={{0,8},{1,9},{2,10},{3,11},{4,12},{5,13},{6,14},{7,15},{8,0},{9,1},... | collective-permute-start | bytes 98312 | tf_op jit(solution)/shard_map/ppermute | solution.py:32
  135.9 4.6 %collective-permute-start.4 = (f32[2,4096]{1,0:T(2,128)S(1)}, f32[2,4096]{1,0:T(2,128)S(1)}, u32[]{:S(2)}, u32[]{:S(2)}) collective-permute-start(f32[2,4096]{1,0:T(2,128)S(1)} %pad_maximum_fusion.6), channel_id=1, source_target_pairs={{0,8},{1,9},{2,10},{3,11},{4,12},{5,13},{6,14},{7,15},{8,0},{9,1},... | collective-permute-start | bytes 98312 | tf_op jit(solution)/shard_map/ppermute | solution.py:32
  138.3 3.1 %collective-permute-start.11 = (f32[2,4096]{1,0:T(2,128)S(1)}, f32[2,4096]{1,0:T(2,128)S(1)}, u32[]{:S(2)}, u32[]{:S(2)}) collective-permute-start(f32[2,4096]{1,0:T(2,128)S(1)} %pad_maximum_fusion.13), channel_id=1, source_target_pairs={{0,16},{1,17},{2,18},{3,19},{4,20},{5,21},{6,22},{7,23},{8,24},{9,... | collective-permute-start | bytes 98312 | tf_op jit(solution)/shard_map/ppermute | solution.py:32
  140.7 3.1 %collective-permute-start.5 = (f32[2,4096]{1,0:T(2,128)S(1)}, f32[2,4096]{1,0:T(2,128)S(1)}, u32[]{:S(2)}, u32[]{:S(2)}) collective-permute-start(f32[2,4096]{1,0:T(2,128)S(1)} %pad_maximum_fusion.7), channel_id=1, source_target_pairs={{0,16},{1,17},{2,18},{3,19},{4,20},{5,21},{6,22},{7,23},{8,24},{9,... | collective-permute-start | bytes 98312 | tf_op jit(solution)/shard_map/ppermute | solution.py:32
  141.5 4.3 %collective-permute-start.12 = (f32[2,4096]{1,0:T(2,128)S(1)}, f32[2,4096]{1,0:T(2,128)S(1)}, u32[]{:S(2)}, u32[]{:S(2)}) collective-permute-start(f32[2,4096]{1,0:T(2,128)S(1)} %pad_maximum_fusion.14), channel_id=1, source_target_pairs={{0,32},{1,33},{2,34},{3,35},{4,36},{5,37},{6,38},{7,39},{8,40},{9,... | collective-permute-start | bytes 98312 | tf_op jit(solution)/shard_map/ppermute | solution.py:32
  143.9 10.9 %collective-permute-start.6 = (f32[2,4096]{1,0:T(2,128)S(1)}, f32[2,4096]{1,0:T(2,128)S(1)}, u32[]{:S(2)}, u32[]{:S(2)}) collective-permute-start(f32[2,4096]{1,0:T(2,128)S(1)} %pad_maximum_fusion.8), channel_id=1, source_target_pairs={{0,32},{1,33},{2,34},{3,35},{4,36},{5,37},{6,38},{7,39},{8,40},{9,... | collective-permute-start | bytes 98312 | tf_op jit(solution)/shard_map/ppermute | solution.py:32
  154.8 4.6 %copy-start.3 = (f32[512,896]{1,0:T(8,128)}, f32[512,896]{1,0:T(8,128)S(1)}, u32[]{:S(2)}) copy-start(f32[512,896]{1,0:T(8,128)S(1)} %fusion) | copy-start | bytes 5505028
  159.4 1.2 copy-start.4
  159.4 9.9 %copy-start.2 = (f32[256,768]{1,0:T(8,128)S(1)}, f32[256,768]{1,0:T(8,128)}, u32[]{:S(2)}) copy-start(f32[256,768]{1,0:T(8,128)} %param.3) | copy-start | bytes 2359300
  160.7 8.6 %collective-permute-start.13 = (f32[256,768]{1,0:T(8,128)S(1)}, f32[256,768]{1,0:T(8,128)}, u32[]{:S(2)}, u32[]{:S(2)}) collective-permute-start(f32[256,768]{1,0:T(8,128)S(1)} %slice.185), channel_id=1, source_target_pairs={{0,64},{64,0},{1,65},{65,1},{2,66},{66,2},{3,67},{67,3},{4,68},{68... | collective-permute-start | bytes 2359304 | tf_op jit(solution)/shard_map/ppermute | solution.py:70
  168.1 1.2 collective-permute-start.14
Sparse Core Ops, SparseCore 0:
  10.7 93.9 all-gather.1

commit v10 on v4

--- a/solution.py
+++ b/solution.py
@@ -4,6 +4,7 @@
 import jax.numpy as jnp
 from jax import lax
 from jax.sharding import PartitionSpec as P
+
 
 HALVES = 2
 
@@ -16,9 +17,11 @@
     return (2.0 * products - sq_norm[None, :]) * score_scale
 
 
-def merge_stats(first, second):
-    top = jnp.maximum(first[0], second[0])
-    total = first[1] * jnp.exp(first[0] - top) + second[1] * jnp.exp(second[0] - top)
+def merge_stats(parts):
+    tops = jnp.stack([part[0] for part in parts])
+    sums = jnp.stack([part[1] for part in parts])
+    top = jnp.max(tops, axis=0)
+    total = jnp.sum(sums * jnp.exp(tops - top[None]), axis=0)
     return jnp.stack([top, total])
 
 
@@ -27,9 +30,13 @@
     stats = jnp.stack([local_max, local_sum])
     bit = 1
     while bit < cent_count:
-        partner = lax.ppermute(stats, "cent", [(i, i ^ bit) for i in range(cent_count)])
-        stats = merge_stats(stats, partner)
-        bit *= 2
+        masks = [bit, 2 * bit, 3 * bit] if 2 * bit < cent_count else [bit]
+        parts = [stats] + [
+            lax.ppermute(stats, "cent", [(i, i ^ mask) for i in range(cent_count)])
+            for mask in masks
+        ]
+        stats = merge_stats(parts)
+        bit *= 4 if len(masks) == 3 else 2
     return stats[0] + jnp.log(stats[1])
 
 

time: 174 us -> 175 us (level)
    ppermute x12 -> x18, starting transfers between devices: 18.1 us -> 20 us  [group_log_total(): lax.ppermute(stats, 'cent', [(i, i ^ mask) for i in range(cent_count)])]
    ppermute x12 -> x18, waiting for transfers between devices: 5.14 us -> 3.18 us  [group_log_total(): lax.ppermute(stats, 'cent', [(i, i ^ mask) for i in range(cent_count)])]
  transfers between devices with their start and end apart: 16 -> 22, of which waited for: 8 -> 5; matrix products, arithmetic and copies ran while one was open for 7% -> 7% of each run, Pallas kernels for 0% -> 0%
where the time goes in v10:
time: 175 us; the launch traced here: 174 us
  waiting for transfers between devices  98.4 us (56%)
  starting transfers between devices  28.2 us (16%)
  matrix products  23.8 us (14%)
  between operations  14.2 us (8%)
  other arithmetic  9.7 us (6%)
    all_gather x1, waiting for transfers between devices, on_device(): members = lax.all_gather(points, 'cent', axis=0, tiled=True)  92.6 us
    ppermute x18, starting transfers between devices, group_log_total(): lax.ppermute(stats, 'cent', [(i, i ^ mask) for i in range(cent_count)])  20 us
    dot_general x2, matrix products, on_device(): lax.dot_general(weights, half, (((0,), (0,)), ((), ())), preferred_elemen...  12.5 us
    dot_general x2, matrix products, score_block(): lax.dot_general(members, cent_block, (((1,), (1,)), ((), ())), preferred_...  11.3 us
    ppermute x1, starting transfers between devices, on_device(): sent_sums = lax.ppermute(sums[:own_rows], 'dp', swap)  6.55 us
  transfers between devices with their start and end apart: 22, of which 5 were waited for; matrix products, arithmetic and copies ran while one was open for 7% of the time, Pallas kernels for 0%

profile of v10, /device:TPU:1, one launch (start us, length us, event | category | flops | bytes accessed | tf_op | source)
XLA Modules:
  0.0 174.3 jit_solution(12229329863950186039)
XLA Ops:
  7.2 0.7 all-gather.2.cloned.1.call-update
  7.9 1.2 convert_element_type.19
  9.1 1.5 collective-permute-start
  10.5 1.3 collective-permute-done
  11.9 0.2 multiply_reduce_fusion
  12.1 92.6 %all-gather.2.cloned.1.call-done = bf16[8192,768]{1,0:T(8,128)(2,1)} async-done(((bf16[128,768]{1,0:T(8,128)(2,1)}), bf16[8192,768]{1,0:T(8,128)(2,1)}) %all-gather.2.cloned.1.call-update) | async-done | bytes 12582928 | tf_op jit(solution)/shard_map/all_gather | solution.py:49
  104.7 5.6 %fusion.26 = (f32[4096]{0:T(1024)S(1)}, f32[512,4096]{1,0:T(8,128)S(1)}) fusion(f32[512]{0:T(512)S(1)} %multiply_reduce_fusion, bf16[8192,768]{1,0:T(8,128)(2,1)} %all-gather.2.cloned.1.call-done, bf16[256,768]{1,0:T(8,128)(2,1)S(1)} %convert_element_type.19, bf16[256,768]{1,0:T(8,128)(2,1)S(1)} %collective-permute-done), kind=kOutput, calls=%fused_computation.64 | convolution fusion | flops 3231182848 | bytes 15484928 | tf_op jit(solution)/shard_map/dot_general | solution.py:14
  110.4 1.3 exponential_reduce_fusion
  111.7 2.5 %collective-permute-start.12 = (f32[2,4096]{1,0:T(2,128)S(1)}, f32[2,4096]{1,0:T(2,128)S(1)}, u32[]{:S(2)}, u32[]{:S(2)}) collective-permute-start(f32[2,4096]{1,0:T(2,128)S(1)} %pad_maximum_fusion.6), channel_id=1, source_target_pairs={{0,3},{1,2},{2,1},{3,0},{4,7},{5,6},{6,5},{7,4},{8,11},{9,10},{10,... | collective-permute-start | bytes 98312 | tf_op jit(solution)/shard_map/ppermute | solution.py:35
  114.1 0.6 collective-permute-start.11
  114.7 0.3 collective-permute-start.10
  115.0 5.6 %fusion.27 = (f32[4096]{0:T(1024)S(1)}, f32[512,4096]{1,0:T(8,128)S(1)}) fusion(f32[512]{0:T(512)S(1)} %multiply_reduce_fusion, bf16[8192,768]{1,0:T(8,128)(2,1)} %all-gather.2.cloned.1.call-done, bf16[256,768]{1,0:T(8,128)(2,1)S(1)} %convert_element_type.19, bf16[256,768]{1,0:T(8,128)(2,1)S(1)} %collective-permute-done), kind=kOutput, calls=%fused_computation.65 | convolution fusion | flops 3231182848 | bytes 15484928 | tf_op jit(solution)/shard_map/dot_general | solution.py:14
  120.6 1.3 exponential_reduce_fusion.1
  121.9 2.5 %collective-permute-start.3 = (f32[2,4096]{1,0:T(2,128)S(1)}, f32[2,4096]{1,0:T(2,128)S(1)}, u32[]{:S(2)}, u32[]{:S(2)}) collective-permute-start(f32[2,4096]{1,0:T(2,128)S(1)} %pad_maximum_fusion.3), channel_id=1, source_target_pairs={{0,3},{1,2},{2,1},{3,0},{4,7},{5,6},{6,5},{7,4},{8,11},{9,10},{10,... | collective-permute-start | bytes 98312 | tf_op jit(solution)/shard_map/ppermute | solution.py:35
  124.4 0.6 collective-permute-start.2
  125.0 0.3 collective-permute-start.1
  125.3 0.1 maximum_maximum_fusion.2
  125.4 0.2 fusion.17
  125.6 2.5 %collective-permute-start.15 = (f32[2,4096]{1,0:T(2,128)S(1)}, f32[2,4096]{1,0:T(2,128)S(1)}, u32[]{:S(2)}, u32[]{:S(2)}) collective-permute-start(f32[2,4096]{1,0:T(2,128)S(1)} %pad_maximum_fusion.7), channel_id=1, source_target_pairs={{0,12},{1,13},{2,14},{3,15},{4,8},{5,9},{6,10},{7,11},{8,4},{9,5},... | collective-permute-start | bytes 98312 | tf_op jit(solution)/shard_map/ppermute | solution.py:35
  128.1 0.5 collective-permute-start.14
  128.7 0.3 collective-permute-start.13
  128.9 0.1 maximum_maximum_fusion.5
  129.0 0.2 fusion.11
  129.2 2.5 %collective-permute-start.6 = (f32[2,4096]{1,0:T(2,128)S(1)}, f32[2,4096]{1,0:T(2,128)S(1)}, u32[]{:S(2)}, u32[]{:S(2)}) collective-permute-start(f32[2,4096]{1,0:T(2,128)S(1)} %pad_maximum_fusion.4), channel_id=1, source_target_pairs={{0,12},{1,13},{2,14},{3,15},{4,8},{5,9},{6,10},{7,11},{8,4},{9,5},... | collective-permute-start | bytes 98312 | tf_op jit(solution)/shard_map/ppermute | solution.py:35
  131.8 0.5 collective-permute-start.5
  132.3 0.3 collective-permute-start.4
  132.7 0.2 fusion.19
  132.9 2.5 %collective-permute-start.18 = (f32[2,4096]{1,0:T(2,128)S(1)}, f32[2,4096]{1,0:T(2,128)S(1)}, u32[]{:S(2)}, u32[]{:S(2)}) collective-permute-start(f32[2,4096]{1,0:T(2,128)S(1)} %pad_maximum_fusion.8), channel_id=1, source_target_pairs={{0,48},{1,49},{2,50},{3,51},{4,52},{5,53},{6,54},{7,55},{8,56},{9,... | collective-permute-start | bytes 98312 | tf_op jit(solution)/shard_map/ppermute | solution.py:35
  135.4 0.4 collective-permute-start.17
  135.8 0.4 collective-permute-start.16
  136.2 0.1 maximum_maximum_fusion.4
  136.3 0.2 fusion.13
  136.5 2.5 %collective-permute-start.9 = (f32[2,4096]{1,0:T(2,128)S(1)}, f32[2,4096]{1,0:T(2,128)S(1)}, u32[]{:S(2)}, u32[]{:S(2)}) collective-permute-start(f32[2,4096]{1,0:T(2,128)S(1)} %pad_maximum_fusion.5), channel_id=1, source_target_pairs={{0,48},{1,49},{2,50},{3,51},{4,52},{5,53},{6,54},{7,55},{8,56},{9,... | collective-permute-start | bytes 98312 | tf_op jit(solution)/shard_map/ppermute | solution.py:35
  139.1 0.5 collective-permute-start.8
  139.5 0.4 collective-permute-start.7
  140.0 0.2 fusion.21
  140.2 0.4 collective-permute-done.9
  140.6 2.7 %collective-permute-done.8 = f32[2,4096]{1,0:T(2,128)S(1)} collective-permute-done((f32[2,4096]{1,0:T(2,128)S(1)}, f32[2,4096]{1,0:T(2,128)S(1)}, u32[]{:S(2)}, u32[]{:S(2)}) %collective-permute-start.8) | collective-permute-done | bytes 32800 | tf_op jit(solution)/shard_map/ppermute | solution.py:35
  143.4 0.2 fusion.15
  143.6 1.2 convert_reduce_fusion.1
  144.8 6.3 %fusion = f32[512,768]{1,0:T(8,128)S(1)} fusion(bf16[8192,768]{1,0:T(8,128)(2,1)} %all-gather.2.cloned.1.call-done, f32[512,4096]{1,0:T(8,128)S(1)} %get-tuple-element.45, f32[4096]{0:T(1024)S(1)} %get-tuple-element.48), kind=kOutput, calls=%fused_computation.8 | convolution fusion | flops 3225419776 | bytes 16269312 | tf_op jit(solution)/shard_map/dot_general | solution.py:65
  151.1 6.2 %fusion.6 = f32[512,768]{1,0:T(8,128)S(1)} fusion(f32[512,768]{1,0:T(8,128)S(1)} %fusion, bf16[8192,768]{1,0:T(8,128)(2,1)} %all-gather.2.cloned.1.call-done, f32[512,4096]{1,0:T(8,128)S(1)} %get-tuple-element.47, f32[4096]{0:T(1024)S(1)} %get-tuple-element.49), kind=kOutput, calls=%fused_computation.15 | convolution fusion | flops 3225812992 | bytes 17842176 | tf_op jit(solution)/shard_map/dot_general | solution.py:65
  157.4 6.5 %collective-permute-start.19 = (f32[256,768]{1,0:T(8,128)S(1)}, f32[256,768]{1,0:T(8,128)S(1)}, u32[]{:S(2)}, u32[]{:S(2)}) collective-permute-start(f32[256,768]{1,0:T(8,128)S(1)} %slice.207), channel_id=1, source_target_pairs={{0,64},{64,0},{1,65},{65,1},{2,66},{66,2},{3,67},{67,3},{4,68},{68... | collective-permute-start | bytes 2359304 | tf_op jit(solution)/shard_map/ppermute | solution.py:71
  163.9 1.2 convert_reduce_fusion
  165.1 0.1 collective-permute-start.20
  165.2 0.6 fusion.23
  165.8 0.6 collective-permute-done.20
  166.4 1.1 fusion.10
  (34 shorter events, 0.6 us)
Async XLA Ops:
  7.2 97.6 %all-gather.2.cloned.1.call-start = ((), (), s32[]{:S(2)}) async-start(), calls=%async_computation | async-start | bytes 12779520 | tf_op jit(solution)/shard_map/all_gather | solution.py:49
  9.1 2.8 %collective-permute-start = (bf16[256,768]{1,0:T(8,128)(2,1)S(1)}, bf16[256,768]{1,0:T(8,128)(2,1)S(1)}, u32[]{:S(2)}, u32[]{:S(2)}) collective-permute-start(bf16[256,768]{1,0:T(8,128)(2,1)S(1)} %convert_element_type.19), channel_id=1, source_target_pairs={{0,64},{64,0},{1,65},{65,1},{2,66},{66,2},{3,67},{67,3},{4,68},{68... | collective-permute-start | bytes 1179656 | tf_op jit(solution)/shard_map/ppermute | solution.py:50
  111.7 13.3 %collective-permute-start.12 = (f32[2,4096]{1,0:T(2,128)S(1)}, f32[2,4096]{1,0:T(2,128)S(1)}, u32[]{:S(2)}, u32[]{:S(2)}) collective-permute-start(f32[2,4096]{1,0:T(2,128)S(1)} %pad_maximum_fusion.6), channel_id=1, source_target_pairs={{0,3},{1,2},{2,1},{3,0},{4,7},{5,6},{6,5},{7,4},{8,11},{9,10},{10,... | collective-permute-start | bytes 98312 | tf_op jit(solution)/shard_map/ppermute | solution.py:35
  114.1 11.1 %collective-permute-start.11 = (f32[2,4096]{1,0:T(2,128)S(1)}, f32[2,4096]{1,0:T(2,128)S(1)}, u32[]{:S(2)}, u32[]{:S(2)}) collective-permute-start(f32[2,4096]{1,0:T(2,128)S(1)} %pad_maximum_fusion.6), channel_id=1, source_target_pairs={{0,2},{1,3},{2,0},{3,1},{4,6},{5,7},{6,4},{7,5},{8,10},{9,11},{10,... | collective-permute-start | bytes 98312 | tf_op jit(solution)/shard_map/ppermute | solution.py:35
  114.7 10.6 %collective-permute-start.10 = (f32[2,4096]{1,0:T(2,128)S(1)}, f32[2,4096]{1,0:T(2,128)S(1)}, u32[]{:S(2)}, u32[]{:S(2)}) collective-permute-start(f32[2,4096]{1,0:T(2,128)S(1)} %pad_maximum_fusion.6), channel_id=1, source_target_pairs={{0,1},{1,0},{2,3},{3,2},{4,5},{5,4},{6,7},{7,6},{8,9},{9,8},{10,11... | collective-permute-start | bytes 98312 | tf_op jit(solution)/shard_map/ppermute | solution.py:35
  121.9 6.7 %collective-permute-start.3 = (f32[2,4096]{1,0:T(2,128)S(1)}, f32[2,4096]{1,0:T(2,128)S(1)}, u32[]{:S(2)}, u32[]{:S(2)}) collective-permute-start(f32[2,4096]{1,0:T(2,128)S(1)} %pad_maximum_fusion.3), channel_id=1, source_target_pairs={{0,3},{1,2},{2,1},{3,0},{4,7},{5,6},{6,5},{7,4},{8,11},{9,10},{10,... | collective-permute-start | bytes 98312 | tf_op jit(solution)/shard_map/ppermute | solution.py:35
  124.4 4.5 %collective-permute-start.2 = (f32[2,4096]{1,0:T(2,128)S(1)}, f32[2,4096]{1,0:T(2,128)S(1)}, u32[]{:S(2)}, u32[]{:S(2)}) collective-permute-start(f32[2,4096]{1,0:T(2,128)S(1)} %pad_maximum_fusion.3), channel_id=1, source_target_pairs={{0,2},{1,3},{2,0},{3,1},{4,6},{5,7},{6,4},{7,5},{8,10},{9,11},{10,... | collective-permute-start | bytes 98312 | tf_op jit(solution)/shard_map/ppermute | solution.py:35
  125.0 3.9 %collective-permute-start.1 = (f32[2,4096]{1,0:T(2,128)S(1)}, f32[2,4096]{1,0:T(2,128)S(1)}, u32[]{:S(2)}, u32[]{:S(2)}) collective-permute-start(f32[2,4096]{1,0:T(2,128)S(1)} %pad_maximum_fusion.3), channel_id=1, source_target_pairs={{0,1},{1,0},{2,3},{3,2},{4,5},{5,4},{6,7},{7,6},{8,9},{9,8},{10,11... | collective-permute-start | bytes 98312 | tf_op jit(solution)/shard_map/ppermute | solution.py:35
  125.6 6.7 %collective-permute-start.15 = (f32[2,4096]{1,0:T(2,128)S(1)}, f32[2,4096]{1,0:T(2,128)S(1)}, u32[]{:S(2)}, u32[]{:S(2)}) collective-permute-start(f32[2,4096]{1,0:T(2,128)S(1)} %pad_maximum_fusion.7), channel_id=1, source_target_pairs={{0,12},{1,13},{2,14},{3,15},{4,8},{5,9},{6,10},{7,11},{8,4},{9,5},... | collective-permute-start | bytes 98312 | tf_op jit(solution)/shard_map/ppermute | solution.py:35
  128.1 4.5 %collective-permute-start.14 = (f32[2,4096]{1,0:T(2,128)S(1)}, f32[2,4096]{1,0:T(2,128)S(1)}, u32[]{:S(2)}, u32[]{:S(2)}) collective-permute-start(f32[2,4096]{1,0:T(2,128)S(1)} %pad_maximum_fusion.7), channel_id=1, source_target_pairs={{0,8},{1,9},{2,10},{3,11},{4,12},{5,13},{6,14},{7,15},{8,0},{9,1},... | collective-permute-start | bytes 98312 | tf_op jit(solution)/shard_map/ppermute | solution.py:35
  128.7 3.9 %collective-permute-start.13 = (f32[2,4096]{1,0:T(2,128)S(1)}, f32[2,4096]{1,0:T(2,128)S(1)}, u32[]{:S(2)}, u32[]{:S(2)}) collective-permute-start(f32[2,4096]{1,0:T(2,128)S(1)} %pad_maximum_fusion.7), channel_id=1, source_target_pairs={{0,4},{1,5},{2,6},{3,7},{4,0},{5,1},{6,2},{7,3},{8,12},{9,13},{10,... | collective-permute-start | bytes 98312 | tf_op jit(solution)/shard_map/ppermute | solution.py:35
  129.2 6.6 %collective-permute-start.6 = (f32[2,4096]{1,0:T(2,128)S(1)}, f32[2,4096]{1,0:T(2,128)S(1)}, u32[]{:S(2)}, u32[]{:S(2)}) collective-permute-start(f32[2,4096]{1,0:T(2,128)S(1)} %pad_maximum_fusion.4), channel_id=1, source_target_pairs={{0,12},{1,13},{2,14},{3,15},{4,8},{5,9},{6,10},{7,11},{8,4},{9,5},... | collective-permute-start | bytes 98312 | tf_op jit(solution)/shard_map/ppermute | solution.py:35
  131.8 4.5 %collective-permute-start.5 = (f32[2,4096]{1,0:T(2,128)S(1)}, f32[2,4096]{1,0:T(2,128)S(1)}, u32[]{:S(2)}, u32[]{:S(2)}) collective-permute-start(f32[2,4096]{1,0:T(2,128)S(1)} %pad_maximum_fusion.4), channel_id=1, source_target_pairs={{0,8},{1,9},{2,10},{3,11},{4,12},{5,13},{6,14},{7,15},{8,0},{9,1},... | collective-permute-start | bytes 98312 | tf_op jit(solution)/shard_map/ppermute | solution.py:35
  132.3 3.9 %collective-permute-start.4 = (f32[2,4096]{1,0:T(2,128)S(1)}, f32[2,4096]{1,0:T(2,128)S(1)}, u32[]{:S(2)}, u32[]{:S(2)}) collective-permute-start(f32[2,4096]{1,0:T(2,128)S(1)} %pad_maximum_fusion.4), channel_id=1, source_target_pairs={{0,4},{1,5},{2,6},{3,7},{4,0},{5,1},{6,2},{7,3},{8,12},{9,13},{10,... | collective-permute-start | bytes 98312 | tf_op jit(solution)/shard_map/ppermute | solution.py:35
  132.9 6.7 %collective-permute-start.18 = (f32[2,4096]{1,0:T(2,128)S(1)}, f32[2,4096]{1,0:T(2,128)S(1)}, u32[]{:S(2)}, u32[]{:S(2)}) collective-permute-start(f32[2,4096]{1,0:T(2,128)S(1)} %pad_maximum_fusion.8), channel_id=1, source_target_pairs={{0,48},{1,49},{2,50},{3,51},{4,52},{5,53},{6,54},{7,55},{8,56},{9,... | collective-permute-start | bytes 98312 | tf_op jit(solution)/shard_map/ppermute | solution.py:35
  135.4 4.5 %collective-permute-start.17 = (f32[2,4096]{1,0:T(2,128)S(1)}, f32[2,4096]{1,0:T(2,128)S(1)}, u32[]{:S(2)}, u32[]{:S(2)}) collective-permute-start(f32[2,4096]{1,0:T(2,128)S(1)} %pad_maximum_fusion.8), channel_id=1, source_target_pairs={{0,32},{1,33},{2,34},{3,35},{4,36},{5,37},{6,38},{7,39},{8,40},{9,... | collective-permute-start | bytes 98312 | tf_op jit(solution)/shard_map/ppermute | solution.py:35
  135.8 4.1 %collective-permute-start.16 = (f32[2,4096]{1,0:T(2,128)S(1)}, f32[2,4096]{1,0:T(2,128)S(1)}, u32[]{:S(2)}, u32[]{:S(2)}) collective-permute-start(f32[2,4096]{1,0:T(2,128)S(1)} %pad_maximum_fusion.8), channel_id=1, source_target_pairs={{0,16},{1,17},{2,18},{3,19},{4,20},{5,21},{6,22},{7,23},{8,24},{9,... | collective-permute-start | bytes 98312 | tf_op jit(solution)/shard_map/ppermute | solution.py:35
  136.5 4.1 %collective-permute-start.9 = (f32[2,4096]{1,0:T(2,128)S(1)}, f32[2,4096]{1,0:T(2,128)S(1)}, u32[]{:S(2)}, u32[]{:S(2)}) collective-permute-start(f32[2,4096]{1,0:T(2,128)S(1)} %pad_maximum_fusion.5), channel_id=1, source_target_pairs={{0,48},{1,49},{2,50},{3,51},{4,52},{5,53},{6,54},{7,55},{8,56},{9,... | collective-permute-start | bytes 98312 | tf_op jit(solution)/shard_map/ppermute | solution.py:35
  139.1 4.3 %collective-permute-start.8 = (f32[2,4096]{1,0:T(2,128)S(1)}, f32[2,4096]{1,0:T(2,128)S(1)}, u32[]{:S(2)}, u32[]{:S(2)}) collective-permute-start(f32[2,4096]{1,0:T(2,128)S(1)} %pad_maximum_fusion.5), channel_id=1, source_target_pairs={{0,32},{1,33},{2,34},{3,35},{4,36},{5,37},{6,38},{7,39},{8,40},{9,... | collective-permute-start | bytes 98312 | tf_op jit(solution)/shard_map/ppermute | solution.py:35
  139.5 3.8 %collective-permute-start.7 = (f32[2,4096]{1,0:T(2,128)S(1)}, f32[2,4096]{1,0:T(2,128)S(1)}, u32[]{:S(2)}, u32[]{:S(2)}) collective-permute-start(f32[2,4096]{1,0:T(2,128)S(1)} %pad_maximum_fusion.5), channel_id=1, source_target_pairs={{0,16},{1,17},{2,18},{3,19},{4,20},{5,21},{6,22},{7,23},{8,24},{9,... | collective-permute-start | bytes 98312 | tf_op jit(solution)/shard_map/ppermute | solution.py:35
  157.3 9.1 %copy-start = (f32[256,768]{1,0:T(8,128)S(1)}, f32[256,768]{1,0:T(8,128)}, u32[]{:S(2)}) copy-start(f32[256,768]{1,0:T(8,128)} %param.3) | copy-start | bytes 2359300
  157.4 9.0 %collective-permute-start.19 = (f32[256,768]{1,0:T(8,128)S(1)}, f32[256,768]{1,0:T(8,128)S(1)}, u32[]{:S(2)}, u32[]{:S(2)}) collective-permute-start(f32[256,768]{1,0:T(8,128)S(1)} %slice.207), channel_id=1, source_target_pairs={{0,64},{64,0},{1,65},{65,1},{2,66},{66,2},{3,67},{67,3},{4,68},{68... | collective-permute-start | bytes 2359304 | tf_op jit(solution)/shard_map/ppermute | solution.py:71
  165.1 1.2 collective-permute-start.20
Sparse Core Ops, SparseCore 0:
  10.7 93.9 all-gather.1

commit v11 on v4

--- a/solution.py
+++ b/solution.py
@@ -4,6 +4,7 @@
 import jax.numpy as jnp
 from jax import lax
 from jax.sharding import PartitionSpec as P
+
 
 HALVES = 2
 
@@ -27,9 +28,11 @@
     stats = jnp.stack([local_max, local_sum])
     bit = 1
     while bit < cent_count:
-        partner = lax.ppermute(stats, "cent", [(i, i ^ bit) for i in range(cent_count)])
-        stats = merge_stats(stats, partner)
-        bit *= 2
+        masks = [bit, 3 * bit] if 2 * bit < cent_count else [bit]
+        for mask in masks:
+            partner = lax.ppermute(stats, "cent", [(i, i ^ mask) for i in range(cent_count)])
+            stats = merge_stats(stats, partner)
+        bit *= 2 * len(masks)
     return stats[0] + jnp.log(stats[1])
 
 

time: 174 us -> 173 us (level)
  no operation moved by 1% of the time
where the time goes in v11:
time: 173 us; the launch traced here: 172 us
  waiting for transfers between devices  98.6 us (57%)
  starting transfers between devices  26.6 us (15%)
  matrix products  23.8 us (14%)
  between operations  14.2 us (8%)
  other arithmetic  9.11 us (5%)
    all_gather x1, waiting for transfers between devices, on_device(): members = lax.all_gather(points, 'cent', axis=0, tiled=True)  92.6 us
    ppermute x12, starting transfers between devices, group_log_total(): lax.ppermute(stats, 'cent', [(i, i ^ mask) for i in range(cent_count)])  17.5 us
    dot_general x2, matrix products, on_device(): lax.dot_general(weights, half, (((0,), (0,)), ((), ())), preferred_elemen...  12.5 us
    dot_general x2, matrix products, score_block(): lax.dot_general(members, cent_block, (((1,), (1,)), ((), ())), preferred_...  11.3 us
    ppermute x1, starting transfers between devices, on_device(): sent_sums = lax.ppermute(sums[:own_rows], 'dp', swap)  7.53 us
  transfers between devices with their start and end apart: 16, of which 8 were waited for; matrix products, arithmetic and copies ran while one was open for 7% of the time, Pallas kernels for 0%

profile of v11, /device:TPU:1, one launch (start us, length us, event | category | flops | bytes accessed | tf_op | source)
XLA Modules:
  0.0 172.4 jit_solution(16331592454744458247)
XLA Ops:
  7.2 0.7 all-gather.2.cloned.1.call-update
  7.9 1.2 convert_element_type.19
  9.1 1.5 collective-permute-start
  10.5 1.3 collective-permute-done
  11.9 0.2 multiply_reduce_fusion
  12.1 92.6 %all-gather.2.cloned.1.call-done = bf16[8192,768]{1,0:T(8,128)(2,1)} async-done(((bf16[128,768]{1,0:T(8,128)(2,1)}), bf16[8192,768]{1,0:T(8,128)(2,1)}) %all-gather.2.cloned.1.call-update) | async-done | bytes 12582928 | tf_op jit(solution)/shard_map/all_gather | solution.py:45
  104.7 5.6 %fusion.40 = (f32[4096]{0:T(1024)S(1)}, f32[512,4096]{1,0:T(8,128)S(1)}) fusion(f32[512]{0:T(512)S(1)} %multiply_reduce_fusion, bf16[8192,768]{1,0:T(8,128)(2,1)} %all-gather.2.cloned.1.call-done, bf16[256,768]{1,0:T(8,128)(2,1)S(1)} %convert_element_type.19, bf16[256,768]{1,0:T(8,128)(2,1)S(1)} %collective-permute-done), kind=kOutput, calls=%fused_computation.98 | convolution fusion | flops 3231182848 | bytes 15484928 | tf_op jit(solution)/shard_map/dot_general | solution.py:14
  110.3 1.3 exponential_reduce_fusion
  111.6 1.3 collective-permute-start.7
  112.9 5.6 %fusion.41 = (f32[4096]{0:T(1024)S(1)}, f32[512,4096]{1,0:T(8,128)S(1)}) fusion(f32[512]{0:T(512)S(1)} %multiply_reduce_fusion, bf16[8192,768]{1,0:T(8,128)(2,1)} %all-gather.2.cloned.1.call-done, bf16[256,768]{1,0:T(8,128)(2,1)S(1)} %convert_element_type.19, bf16[256,768]{1,0:T(8,128)(2,1)S(1)} %collective-permute-done), kind=kOutput, calls=%fused_computation.99 | convolution fusion | flops 3231182848 | bytes 15484928 | tf_op jit(solution)/shard_map/dot_general | solution.py:14
  118.6 1.3 exponential_reduce_fusion.1
  119.9 0.4 collective-permute-start.1
  120.2 0.1 multiply_add_fusion.4
  120.3 2.5 %collective-permute-start.8 = (f32[2,4096]{1,0:T(2,128)S(1)}, f32[2,4096]{1,0:T(2,128)S(1)}, u32[]{:S(2)}, u32[]{:S(2)}) collective-permute-start(f32[2,4096]{1,0:T(2,128)S(1)} %pad_maximum_fusion.10), channel_id=1, source_target_pairs={{0,3},{1,2},{2,1},{3,0},{4,7},{5,6},{6,5},{7,4},{8,11},{9,10},{10,... | collective-permute-start | bytes 98312 | tf_op jit(solution)/shard_map/ppermute | solution.py:33
  122.8 0.1 multiply_add_fusion.9
  122.9 1.7 %collective-permute-start.2 = (f32[2,4096]{1,0:T(2,128)S(1)}, f32[2,4096]{1,0:T(2,128)S(1)}, u32[]{:S(2)}, u32[]{:S(2)}) collective-permute-start(f32[2,4096]{1,0:T(2,128)S(1)} %pad_maximum_fusion.4), channel_id=1, source_target_pairs={{0,3},{1,2},{2,1},{3,0},{4,7},{5,6},{6,5},{7,4},{8,11},{9,10},{10,... | collective-permute-start | bytes 98312 | tf_op jit(solution)/shard_map/ppermute | solution.py:33
  124.7 0.1 multiply_add_fusion.3
  124.8 1.3 collective-permute-start.9
  126.1 0.9 collective-permute-done.2
  127.0 0.1 multiply_add_fusion.8
  127.1 1.3 collective-permute-start.3
  128.4 0.1 multiply_add_fusion.2
  128.5 1.9 %collective-permute-start.10 = (f32[2,4096]{1,0:T(2,128)S(1)}, f32[2,4096]{1,0:T(2,128)S(1)}, u32[]{:S(2)}, u32[]{:S(2)}) collective-permute-start(f32[2,4096]{1,0:T(2,128)S(1)} %pad_maximum_fusion.12), channel_id=1, source_target_pairs={{0,12},{1,13},{2,14},{3,15},{4,8},{5,9},{6,10},{7,11},{8,4},{9,5},... | collective-permute-start | bytes 98312 | tf_op jit(solution)/shard_map/ppermute | solution.py:33
  130.4 0.1 multiply_add_fusion.7
  130.5 2.1 %collective-permute-start.4 = (f32[2,4096]{1,0:T(2,128)S(1)}, f32[2,4096]{1,0:T(2,128)S(1)}, u32[]{:S(2)}, u32[]{:S(2)}) collective-permute-start(f32[2,4096]{1,0:T(2,128)S(1)} %pad_maximum_fusion.6), channel_id=1, source_target_pairs={{0,12},{1,13},{2,14},{3,15},{4,8},{5,9},{6,10},{7,11},{8,4},{9,5},... | collective-permute-start | bytes 98312 | tf_op jit(solution)/shard_map/ppermute | solution.py:33
  132.6 0.1 multiply_add_fusion.1
  132.7 0.3 collective-permute-start.11
  133.1 1.5 collective-permute-done.4
  134.6 0.1 multiply_add_fusion.6
  134.7 0.7 collective-permute-start.5
  135.4 0.2 collective-permute-done.11
  135.6 0.1 slice_maximum_fusion
  135.7 1.8 %collective-permute-start.12 = (f32[2,4096]{1,0:T(2,128)S(1)}, f32[2,4096]{1,0:T(2,128)S(1)}, u32[]{:S(2)}, u32[]{:S(2)}) collective-permute-start(f32[2,4096]{1,0:T(2,128)S(1)} %pad_maximum_fusion.14), channel_id=1, source_target_pairs={{0,48},{1,49},{2,50},{3,51},{4,52},{5,53},{6,54},{7,55},{8,56},{9,... | collective-permute-start | bytes 98312 | tf_op jit(solution)/shard_map/ppermute | solution.py:33
  137.4 0.1 collective-permute-done.5
  137.5 0.1 slice_maximum_fusion.5
  137.6 2.3 %collective-permute-start.6 = (f32[2,4096]{1,0:T(2,128)S(1)}, f32[2,4096]{1,0:T(2,128)S(1)}, u32[]{:S(2)}, u32[]{:S(2)}) collective-permute-start(f32[2,4096]{1,0:T(2,128)S(1)} %pad_maximum_fusion.8), channel_id=1, source_target_pairs={{0,48},{1,49},{2,50},{3,51},{4,52},{5,53},{6,54},{7,55},{8,56},{9,... | collective-permute-start | bytes 98312 | tf_op jit(solution)/shard_map/ppermute | solution.py:33
  139.9 0.1 log_add_fusion
  140.0 1.2 convert_reduce_fusion
  141.2 0.7 collective-permute-done.6
  141.9 0.1 log_add_fusion.1
  142.0 6.3 %fusion = f32[512,768]{1,0:T(8,128)S(1)} fusion(bf16[8192,768]{1,0:T(8,128)(2,1)} %all-gather.2.cloned.1.call-done, f32[512,4096]{1,0:T(8,128)S(1)} %get-tuple-element.47, f32[4096]{0:T(1024)S(1)} %log_add_fusion), kind=kOutput, calls=%fused_computation.8 | convolution fusion | flops 3225419776 | bytes 16269312 | tf_op jit(solution)/shard_map/dot_general | solution.py:61
  148.2 6.2 %fusion.6 = f32[512,768]{1,0:T(8,128)S(1)} fusion(f32[512,768]{1,0:T(8,128)S(1)} %fusion, bf16[8192,768]{1,0:T(8,128)(2,1)} %all-gather.2.cloned.1.call-done, f32[512,4096]{1,0:T(8,128)S(1)} %get-tuple-element.49, f32[4096]{0:T(1024)S(1)} %log_add_fusion.1), kind=kOutput, calls=%fused_computation.15 | convolution fusion | flops 3225812992 | bytes 17842176 | tf_op jit(solution)/shard_map/dot_general | solution.py:61
  154.6 7.5 %collective-permute-start.13 = (f32[256,768]{1,0:T(8,128)S(1)}, f32[256,768]{1,0:T(8,128)S(1)}, u32[]{:S(2)}, u32[]{:S(2)}) collective-permute-start(f32[256,768]{1,0:T(8,128)S(1)} %slice.159), channel_id=1, source_target_pairs={{0,64},{64,0},{1,65},{65,1},{2,66},{66,2},{3,67},{67,3},{4,68},{68... | collective-permute-start | bytes 2359304 | tf_op jit(solution)/shard_map/ppermute | solution.py:67
  162.1 1.2 convert_reduce_fusion.1
  163.3 0.1 collective-permute-start.14
  163.4 0.6 fusion.35
  164.0 0.6 collective-permute-done.14
  164.5 1.0 fusion.10
  (29 shorter events, 0.6 us)
Async XLA Ops:
  7.2 97.5 %all-gather.2.cloned.1.call-start = ((), (), s32[]{:S(2)}) async-start(), calls=%async_computation | async-start | bytes 12779520 | tf_op jit(solution)/shard_map/all_gather | solution.py:45
  9.1 2.8 %collective-permute-start = (bf16[256,768]{1,0:T(8,128)(2,1)S(1)}, bf16[256,768]{1,0:T(8,128)(2,1)S(1)}, u32[]{:S(2)}, u32[]{:S(2)}) collective-permute-start(bf16[256,768]{1,0:T(8,128)(2,1)S(1)} %convert_element_type.19), channel_id=1, source_target_pairs={{0,64},{64,0},{1,65},{65,1},{2,66},{66,2},{3,67},{67,3},{4,68},{68... | collective-permute-start | bytes 1179656 | tf_op jit(solution)/shard_map/ppermute | solution.py:46
  111.6 8.6 %collective-permute-start.7 = (f32[2,4096]{1,0:T(2,128)S(1)}, f32[2,4096]{1,0:T(2,128)S(1)}, u32[]{:S(2)}, u32[]{:S(2)}) collective-permute-start(f32[2,4096]{1,0:T(2,128)S(1)} %pad_maximum_fusion.9), channel_id=1, source_target_pairs={{0,1},{1,0},{2,3},{3,2},{4,5},{5,4},{6,7},{7,6},{8,9},{9,8},{10,11... | collective-permute-start | bytes 98312 | tf_op jit(solution)/shard_map/ppermute | solution.py:33
  119.9 3.0 %collective-permute-start.1 = (f32[2,4096]{1,0:T(2,128)S(1)}, f32[2,4096]{1,0:T(2,128)S(1)}, u32[]{:S(2)}, u32[]{:S(2)}) collective-permute-start(f32[2,4096]{1,0:T(2,128)S(1)} %pad_maximum_fusion.3), channel_id=1, source_target_pairs={{0,1},{1,0},{2,3},{3,2},{4,5},{5,4},{6,7},{7,6},{8,9},{9,8},{10,11... | collective-permute-start | bytes 98312 | tf_op jit(solution)/shard_map/ppermute | solution.py:33
  120.3 4.4 %collective-permute-start.8 = (f32[2,4096]{1,0:T(2,128)S(1)}, f32[2,4096]{1,0:T(2,128)S(1)}, u32[]{:S(2)}, u32[]{:S(2)}) collective-permute-start(f32[2,4096]{1,0:T(2,128)S(1)} %pad_maximum_fusion.10), channel_id=1, source_target_pairs={{0,3},{1,2},{2,1},{3,0},{4,7},{5,6},{6,5},{7,4},{8,11},{9,10},{10,... | collective-permute-start | bytes 98312 | tf_op jit(solution)/shard_map/ppermute | solution.py:33
  122.9 4.1 %collective-permute-start.2 = (f32[2,4096]{1,0:T(2,128)S(1)}, f32[2,4096]{1,0:T(2,128)S(1)}, u32[]{:S(2)}, u32[]{:S(2)}) collective-permute-start(f32[2,4096]{1,0:T(2,128)S(1)} %pad_maximum_fusion.4), channel_id=1, source_target_pairs={{0,3},{1,2},{2,1},{3,0},{4,7},{5,6},{6,5},{7,4},{8,11},{9,10},{10,... | collective-permute-start | bytes 98312 | tf_op jit(solution)/shard_map/ppermute | solution.py:33
  124.8 3.6 %collective-permute-start.9 = (f32[2,4096]{1,0:T(2,128)S(1)}, f32[2,4096]{1,0:T(2,128)S(1)}, u32[]{:S(2)}, u32[]{:S(2)}) collective-permute-start(f32[2,4096]{1,0:T(2,128)S(1)} %pad_maximum_fusion.11), channel_id=1, source_target_pairs={{0,4},{1,5},{2,6},{3,7},{4,0},{5,1},{6,2},{7,3},{8,12},{9,13},{10,... | collective-permute-start | bytes 98312 | tf_op jit(solution)/shard_map/ppermute | solution.py:33
  127.1 3.3 %collective-permute-start.3 = (f32[2,4096]{1,0:T(2,128)S(1)}, f32[2,4096]{1,0:T(2,128)S(1)}, u32[]{:S(2)}, u32[]{:S(2)}) collective-permute-start(f32[2,4096]{1,0:T(2,128)S(1)} %pad_maximum_fusion.5), channel_id=1, source_target_pairs={{0,4},{1,5},{2,6},{3,7},{4,0},{5,1},{6,2},{7,3},{8,12},{9,13},{10,... | collective-permute-start | bytes 98312 | tf_op jit(solution)/shard_map/ppermute | solution.py:33
  128.5 4.1 %collective-permute-start.10 = (f32[2,4096]{1,0:T(2,128)S(1)}, f32[2,4096]{1,0:T(2,128)S(1)}, u32[]{:S(2)}, u32[]{:S(2)}) collective-permute-start(f32[2,4096]{1,0:T(2,128)S(1)} %pad_maximum_fusion.12), channel_id=1, source_target_pairs={{0,12},{1,13},{2,14},{3,15},{4,8},{5,9},{6,10},{7,11},{8,4},{9,5},... | collective-permute-start | bytes 98312 | tf_op jit(solution)/shard_map/ppermute | solution.py:33
  130.5 4.1 %collective-permute-start.4 = (f32[2,4096]{1,0:T(2,128)S(1)}, f32[2,4096]{1,0:T(2,128)S(1)}, u32[]{:S(2)}, u32[]{:S(2)}) collective-permute-start(f32[2,4096]{1,0:T(2,128)S(1)} %pad_maximum_fusion.6), channel_id=1, source_target_pairs={{0,12},{1,13},{2,14},{3,15},{4,8},{5,9},{6,10},{7,11},{8,4},{9,5},... | collective-permute-start | bytes 98312 | tf_op jit(solution)/shard_map/ppermute | solution.py:33
  132.7 2.8 %collective-permute-start.11 = (f32[2,4096]{1,0:T(2,128)S(1)}, f32[2,4096]{1,0:T(2,128)S(1)}, u32[]{:S(2)}, u32[]{:S(2)}) collective-permute-start(f32[2,4096]{1,0:T(2,128)S(1)} %pad_maximum_fusion.13), channel_id=1, source_target_pairs={{0,16},{1,17},{2,18},{3,19},{4,20},{5,21},{6,22},{7,23},{8,24},{9,... | collective-permute-start | bytes 98312 | tf_op jit(solution)/shard_map/ppermute | solution.py:33
  134.7 2.8 %collective-permute-start.5 = (f32[2,4096]{1,0:T(2,128)S(1)}, f32[2,4096]{1,0:T(2,128)S(1)}, u32[]{:S(2)}, u32[]{:S(2)}) collective-permute-start(f32[2,4096]{1,0:T(2,128)S(1)} %pad_maximum_fusion.7), channel_id=1, source_target_pairs={{0,16},{1,17},{2,18},{3,19},{4,20},{5,21},{6,22},{7,23},{8,24},{9,... | collective-permute-start | bytes 98312 | tf_op jit(solution)/shard_map/ppermute | solution.py:33
  135.7 4.2 %collective-permute-start.12 = (f32[2,4096]{1,0:T(2,128)S(1)}, f32[2,4096]{1,0:T(2,128)S(1)}, u32[]{:S(2)}, u32[]{:S(2)}) collective-permute-start(f32[2,4096]{1,0:T(2,128)S(1)} %pad_maximum_fusion.14), channel_id=1, source_target_pairs={{0,48},{1,49},{2,50},{3,51},{4,52},{5,53},{6,54},{7,55},{8,56},{9,... | collective-permute-start | bytes 98312 | tf_op jit(solution)/shard_map/ppermute | solution.py:33
  137.6 4.2 %collective-permute-start.6 = (f32[2,4096]{1,0:T(2,128)S(1)}, f32[2,4096]{1,0:T(2,128)S(1)}, u32[]{:S(2)}, u32[]{:S(2)}) collective-permute-start(f32[2,4096]{1,0:T(2,128)S(1)} %pad_maximum_fusion.8), channel_id=1, source_target_pairs={{0,48},{1,49},{2,50},{3,51},{4,52},{5,53},{6,54},{7,55},{8,56},{9,... | collective-permute-start | bytes 98312 | tf_op jit(solution)/shard_map/ppermute | solution.py:33
  154.5 10.1 %copy-start = (f32[256,768]{1,0:T(8,128)S(1)}, f32[256,768]{1,0:T(8,128)}, u32[]{:S(2)}) copy-start(f32[256,768]{1,0:T(8,128)} %param.3) | copy-start | bytes 2359300
  154.6 10.0 %collective-permute-start.13 = (f32[256,768]{1,0:T(8,128)S(1)}, f32[256,768]{1,0:T(8,128)S(1)}, u32[]{:S(2)}, u32[]{:S(2)}) collective-permute-start(f32[256,768]{1,0:T(8,128)S(1)} %slice.159), channel_id=1, source_target_pairs={{0,64},{64,0},{1,65},{65,1},{2,66},{66,2},{3,67},{67,3},{4,68},{68... | collective-permute-start | bytes 2359304 | tf_op jit(solution)/shard_map/ppermute | solution.py:67
  163.3 1.2 collective-permute-start.14
Sparse Core Ops, SparseCore 0:
  10.7 93.9 all-gather.1
